TPU v7x, 512 devices: a whole 4x8x8 slice. The times are simulated.
512 devices in a mesh: gx: 16 (over z, core), gy: 32 (over y, x).
Axes of the slice: x: 4, y: 8, z: 8, core: 2. Of those that a mesh axis runs over, the one named last changes fastest.
Arguments:
- stencil: float32 [32, 64, 2, 32, 864], P('gx', 'gy'), may hold values from -0.21875 to 0.21875
- pattern: int32 [32, 64, 2, 27], P('gx', 'gy'), may hold values 0 or 1
- tentative: float32 [32, 64, 2, 32, 32], P('gx', 'gy'), may hold values from -1 to 1
- diag_inverse: float32 [32, 64, 2, 32, 32], P('gx', 'gy'), may hold values from -1 to 1
- coarse_pattern: int32 [16, 32, 9], P('gx', 'gy'), may hold values 0 or 1
- slot: int32 [16, 32], P('gx', 'gy'), may hold values from 0 to 3, as said below
Outputs:
- coarse_rows: float32 [16, 32, 32, 288], P('gx', 'gy')
- grouped: float32 [16, 32, 4, 32, 288], P('gx', 'gy')
Inputs may be any that keep to these rules, and one draw needn't show every extreme that they name: For each y, the four entries slot[4 g .. 4 g + 3, y] are 0, 1, 2, 3 in some order.
All inputs are finite; a program needn't handle non-finite values. No bound on the sum of `pattern` or of `coarse_pattern` on one device may be relied on, other than what follows from the above.
Results may differ from a plain program's by a relative error of at most 0.0003.
Values sent between devices are 32-bit elements; how exact they have to be, the bound alone decides.
No kernel may reach another device: no remote copies, remote signals or barrier semaphores. Data moves between devices by JAX's collectives and lax.ppermute only.
A program may use at most 64 MiB of HBM per device.

v0:
```python
import jax
import jax.numpy as jnp
import numpy as np
from jax import lax
from jax.sharding import PartitionSpec as P

OMEGA = 0.6
HI = lax.Precision.HIGHEST


def shift(block, axis, forward):
    count = lax.axis_size(axis)
    if forward:
        pairs = [(i, i + 1) for i in range(count - 1)]
    else:
        pairs = [(i + 1, i) for i in range(count - 1)]
    return lax.ppermute(block, axis, pairs)


def to_positions(rows):
    width = rows.shape[3]
    grid = rows.reshape(2, 2, 2, width, 3, 3, 3, -1)
    cells = []
    for cell_x in range(2):
        for cell_y in range(2):
            for cell_z in range(2):
                block = grid[cell_x, cell_y, cell_z]
                block = block[:, :, :, 1:3] if cell_z == 0 else block[:, :, :, 0:2]
                zeros_x = jnp.zeros_like(block[:, :1])
                block = jnp.concatenate([block, zeros_x] if cell_x == 0 else [zeros_x, block], axis=1)
                zeros_y = jnp.zeros_like(block[:, :, :1])
                block = jnp.concatenate([block, zeros_y] if cell_y == 0 else [zeros_y, block], axis=2)
                cells.append(block)
    return jnp.stack(cells).reshape(2, 2, 2, width, 4, 4, 2, -1)


def reach_mask():
    reach = [0, 1, 1, 2]
    table = np.zeros((4, 4, 3, 3), np.float32)
    for pos_x in range(4):
        for pos_y in range(4):
            table[pos_x, pos_y, reach[pos_x], reach[pos_y]] = 1.0
    return table


def local(stencil, pattern, tentative, diag_inverse, coarse_pattern, slot):
    width = tentative.shape[-1]
    keep_mask = jnp.repeat(pattern.astype(jnp.float32), width, axis=-1)[:, :, :, None, :]
    stencil_rows = stencil * keep_mask
    scaled_rows = jnp.einsum("xyzrs,xyzsk->xyzrk", diag_inverse, stencil_rows, precision=HI)
    both = to_positions(jnp.concatenate([stencil_rows, scaled_rows], axis=3))
    stencil_pos = both[:, :, :, :width].reshape(8 * width, 32 * width)
    scaled_pos = both[:, :, :, width:].reshape(8 * width, 32 * width)

    left = shift(tentative[1], "gx", True)
    right = shift(tentative[0], "gx", False)
    tent_x = jnp.concatenate([left[None], tentative, right[None]], axis=0)
    low = shift(tent_x[:, 1], "gy", True)
    high = shift(tent_x[:, 0], "gy", False)
    tent_frame = jnp.concatenate([low[:, None], tent_x, high[:, None]], axis=1)

    mask = jnp.asarray(reach_mask())
    tent_agg = tent_frame[:, :, :, :, None, None, :] * mask[:, :, None, None, :, :, None]
    smoothed = jnp.dot(scaled_pos, tent_agg.reshape(32 * width, 9 * width), precision=HI)
    centre = jnp.asarray(np.eye(9, dtype=np.float32)[4])
    own_tent = tentative.reshape(8 * width, 1, width) * centre[None, :, None]
    prolong_own = own_tent.reshape(8 * width, 9 * width) - OMEGA * smoothed

    grid = prolong_own.reshape(2, 2, 2, width, 3, 3, width)
    from_right = shift(grid[0, :, :, :, 0:2], "gx", False)
    from_left = shift(grid[1, :, :, :, 1:3], "gx", True)
    pad_x_low = ((0, 0), (0, 0), (0, 0), (0, 1), (0, 0), (0, 0))
    pad_x_high = ((0, 0), (0, 0), (0, 0), (1, 0), (0, 0), (0, 0))
    prolong_x = jnp.concatenate(
        [jnp.pad(from_left, pad_x_low)[None], grid, jnp.pad(from_right, pad_x_high)[None]], axis=0
    )
    from_high = shift(prolong_x[:, 0, :, :, :, 0:2], "gy", False)
    from_low = shift(prolong_x[:, 1, :, :, :, 1:3], "gy", True)
    pad_y_low = ((0, 0), (0, 0), (0, 0), (0, 0), (0, 1), (0, 0))
    pad_y_high = ((0, 0), (0, 0), (0, 0), (0, 0), (1, 0), (0, 0))
    prolong_frame = jnp.concatenate(
        [
            jnp.pad(from_low, pad_y_low)[:, None],
            prolong_x,
            jnp.pad(from_high, pad_y_high)[:, None],
        ],
        axis=1,
    )

    applied = jnp.dot(stencil_pos, prolong_frame.reshape(32 * width, 9 * width), precision=HI)
    product = lax.dot_general(prolong_own, applied, (((0,), (0,)), ((), ())), precision=HI)
    product = product.reshape(3, 3, width, 3, 3, width)
    product = jnp.pad(product, ((0, 0), (0, 0), (0, 0), (1, 1), (1, 1), (0, 0)))
    lines = []
    for row_x in range(3):
        column = []
        for row_y in range(3):
            piece = product[row_x, row_y, :, row_x : row_x + 3, row_y : row_y + 3, :]
            column.append(piece.reshape(width, 9 * width))
        lines.append(jnp.stack(column))
    partial_rows = jnp.stack(lines)

    acc = partial_rows[1] + shift(partial_rows[2], "gx", True) + shift(partial_rows[0], "gx", False)
    total = acc[1] + shift(acc[2], "gy", True) + shift(acc[0], "gy", False)
    column_mask = jnp.repeat(coarse_pattern[0, 0].astype(jnp.float32), width)[None, :]
    coarse_block = total * column_mask

    slot_row = jnp.broadcast_to(slot.astype(jnp.float32).reshape(1, 1), (1, 9 * width))
    payload = jnp.concatenate([coarse_block, slot_row], axis=0)
    count = lax.axis_size("gx")
    members = [payload]
    for step in (1, 2, 3):
        pairs = [(i, 4 * (i // 4) + (i % 4 + step) % 4) for i in range(count)]
        members.append(lax.ppermute(payload, "gx", pairs))
    grouped = []
    for target in range(4):
        chosen = jnp.zeros_like(coarse_block)
        for member in members:
            chosen = jnp.where(member[width:, :1] == float(target), member[:width], chosen)
        grouped.append(chosen)
    grouped = jnp.stack(grouped)
    return (coarse_block[None, None], grouped[None, None])


def solution(mesh):
    placed = (
        P("gx", "gy", None, None, None),
        P("gx", "gy", None, None),
        P("gx", "gy", None, None, None),
        P("gx", "gy", None, None, None),
        P("gx", "gy", None),
        P("gx", "gy"),
    )
    return jax.shard_map(
        local,
        mesh=mesh,
        in_specs=placed,
        out_specs=(P("gx", "gy", None, None), P("gx", "gy", None, None, None)),
        check_vma=False,
    )
```

profile of v0, /device:TPU:288, one launch (start us, length us, event | category | flops | bytes accessed | tf_op | source)
XLA Modules:
  0.0 159.3 jit_solution(7548942841601029017)
XLA Ops:
  0.6 0.9 slice_bitcast_fusion.13
  1.6 1.9 %collective-permute-start.1 = (f32[2,2,32,32]{3,2,1,0:T(8,128)S(1)}, f32[2,2,32,32]{3,2,1,0:T(8,128)S(1)}, u32[]{:S(2)}, u32[]{:S(2)}) collective-permute-start(f32[2,2,32,32]{3,2,1,0:T(8,128)S(1)} %get-tuple-element.34), channel_id=1, source_target_pairs={{32,0},{64,32},{96,64},{128,96},{160,128},{192,160},{224,192},{256... | collective-permute-start | bytes 49160 | tf_op jit(solution)/shard_map/ppermute | solution.py:17
  3.5 2.4 %collective-permute-start = (f32[2,2,32,32]{3,2,1,0:T(8,128)S(1)}, f32[2,2,32,32]{3,2,1,0:T(8,128)S(1)}, u32[]{:S(2)}, u32[]{:S(2)}) collective-permute-start(f32[2,2,32,32]{3,2,1,0:T(8,128)S(1)} %get-tuple-element.33), channel_id=1, source_target_pairs={{0,32},{32,64},{64,96},{96,128},{128,160},{160,192},{192,224},{224... | collective-permute-start | bytes 49160 | tf_op jit(solution)/shard_map/ppermute | solution.py:17
  5.9 0.7 convert_element_type.22
  6.7 0.1 mul.78
  6.8 1.3 broadcast_multiply_fusion.1
  8.1 0.9 convolution_bitcast_fusion
  9.0 0.1 pad_maximum_fusion.1
  9.1 2.4 %copy.27 = f32[2,2,2,64,864]{3,4,2,1,0:T(8,128)} copy(f32[2,2,2,64,864]{4,3,2,1,0:T(8,128)S(1)} %pad_maximum_fusion.1) | data formatting | bytes 3538944 | tf_op jit(solution)/shard_map/concatenate | solution.py:51
  11.6 2.3 %slice_bitcast_fusion = (f32[64,3,3,3,32]{0,4,3,2,1:T(8,128)S(1)}, f32[64,3,3,3,32]{0,4,3,2,1:T(8,128)S(1)}, f32[64,3,3,3,32]{0,4,3,2,1:T(8,128)S(1)}, f32[64,3,...) fusion(f32[2,2,2,64,3,3,3,32]{3,7,6,5,4,2,1,0:T(8,128)} %bitcas, ...), kind=kLoop, calls=%fused_computation.40 | loop fusion | bytes 3538944 | tf_op jit(solution)/shard_map/squeeze | solution.py:27
  14.5 0.4 copy-done.4
  15.0 4.6 %collective-permute-start.3 = (f32[4,2,32,32]{3,2,1,0:T(8,128)S(1)}, f32[4,2,32,32]{3,2,1,0:T(8,128)S(1)}, u32[]{:S(2)}, u32[]{:S(2)}) collective-permute-start(f32[4,2,32,32]{3,2,1,0:T(8,128)S(1)} %get-tuple-element.26), channel_id=1, source_target_pairs={{1,0},{2,1},{3,2},{4,3},{5,4},{6,5},{7,6},{8,7},{9,8},{10,9},{11,1... | collective-permute-start | bytes 98312 | tf_op jit(solution)/shard_map/ppermute | solution.py:17
  19.6 1.9 %collective-permute-start.2 = (f32[4,2,32,32]{3,2,1,0:T(8,128)S(1)}, f32[4,2,32,32]{3,2,1,0:T(8,128)S(1)}, u32[]{:S(2)}, u32[]{:S(2)}) collective-permute-start(f32[4,2,32,32]{3,2,1,0:T(8,128)S(1)} %get-tuple-element.25), channel_id=1, source_target_pairs={{0,1},{1,2},{2,3},{3,4},{4,5},{5,6},{6,7},{7,8},{8,9},{9,10},{10,1... | collective-permute-start | bytes 98312 | tf_op jit(solution)/shard_map/ppermute | solution.py:17
  21.5 4.9 %fusion.14 = (f32[2,2,2,32,4,4,2,32]{3,7,6,5,4,2,1,0:T(8,128)}, f32[2,2,2,32,4,4,2,32]{3,7,6,5,4,2,1,0:T(8,128)}) fusion(f32[2,2,2,64,4,4,2,32]{3,7,6,5,4,2,1,0:T(8,128)S(1)} %bitcast.151), kind=kLoop, calls=%fused_computation.72 | loop fusion | bytes 4194304 | tf_op jit(solution)/shard_map/slice | solution.py:52
  26.6 8.1 %copy.37 = f32[2,2,2,32,4,4,2,32]{7,6,5,4,3,2,1,0:T(2,128)} copy(f32[2,2,2,32,4,4,2,32]{3,7,6,5,4,2,1,0:T(8,128)} %get-tuple-element.3) | data formatting | bytes 2097152
  34.7 6.3 %reshape.55 = f32[256,1024]{1,0:T(8,128)S(1)} reshape(f32[2,2,2,32,4,4,2,32]{7,6,5,4,3,2,1,0:T(2,128)} %copy.37) | data formatting | bytes 2097152 | tf_op jit(solution)/shard_map/reshape | solution.py:53
  41.2 0.7 copy.31
  41.9 4.8 %broadcast_multiply_fusion = f32[4,4,2,32,3,3,32]{3,2,1,0,6,5,4:T(2,128)} fusion(f32[4,4,3,3]{1,0,3,2:T(4,128)S(1)} %copy-done.6, f32[4,4,2,32,32]{3,2,1,0,4:T(2,128)S(1)} %copy.31), kind=kLoop, calls=%fused_computation.9 | loop fusion | flops 294912 | bytes 1311296 | tf_op jit(solution)/shard_map/mul | solution.py:63
  46.7 6.9 %mul.84 = f32[1024,288]{0,1:T(8,128)S(1)} reshape(f32[4,4,2,32,3,3,32]{3,2,1,0,6,5,4:T(2,128)} %broadcast_multiply_fusion) | data formatting | bytes 2359296 | tf_op jit(solution)/shard_map/mul | solution.py:63
  53.6 1.1 fusion
  54.7 1.0 reshape.57
  55.7 0.4 slice_bitcast_fusion.9
  56.1 4.1 %collective-permute-start.5 = (f32[2,2,32,2,3,32]{2,1,0,5,4,3:T(2,128)S(1)}, f32[2,2,32,2,3,32]{2,1,0,5,4,3:T(2,128)S(1)}, u32[]{:S(2)}, u32[]{:S(2)}) collective-permute-start(f32[2,2,32,2,3,32]{2,1,0,5,4,3:T(2,128)S(1)} %get-tuple-element.24), channel_id=1, source_target_pairs={{32,0},{64,32},{96,64},{128,96},{160,128},{192,160},{224,192},{256... | collective-permute-start | bytes 294920 | tf_op jit(solution)/shard_map/ppermute | solution.py:17
  60.2 1.9 %collective-permute-start.4 = (f32[2,2,32,2,3,32]{2,1,0,5,4,3:T(2,128)S(1)}, f32[2,2,32,2,3,32]{2,1,0,5,4,3:T(2,128)S(1)}, u32[]{:S(2)}, u32[]{:S(2)}) collective-permute-start(f32[2,2,32,2,3,32]{2,1,0,5,4,3:T(2,128)S(1)} %get-tuple-element.23), channel_id=1, source_target_pairs={{0,32},{32,64},{64,96},{96,128},{128,160},{160,192},{192,224},{224... | collective-permute-start | bytes 294920 | tf_op jit(solution)/shard_map/ppermute | solution.py:17
  62.1 3.3 %collective-permute-done.5 = f32[2,2,32,2,3,32]{2,1,0,5,4,3:T(2,128)S(1)} collective-permute-done((f32[2,2,32,2,3,32]{2,1,0,5,4,3:T(2,128)S(1)}, f32[2,2,32,2,3,32]{2,1,0,5,4,3:T(2,128)S(1)}, u32[]{:S(2)}, u32[]{:S(2)}) %collective-permute-start.5) | collective-permute-done | bytes 98336 | tf_op jit(solution)/shard_map/ppermute | solution.py:17
  65.5 0.2 pad_bitcast_fusion.2
  65.7 4.8 %collective-permute-done.4 = f32[2,2,32,2,3,32]{2,1,0,5,4,3:T(2,128)S(1)} collective-permute-done((f32[2,2,32,2,3,32]{2,1,0,5,4,3:T(2,128)S(1)}, f32[2,2,32,2,3,32]{2,1,0,5,4,3:T(2,128)S(1)}, u32[]{:S(2)}, u32[]{:S(2)}) %collective-permute-start.4) | collective-permute-done | bytes 98336 | tf_op jit(solution)/shard_map/ppermute | solution.py:17
  70.5 0.2 pad_bitcast_fusion.3
  70.7 2.0 %maximum_bitcast_fusion = (f32[4,2,32,3,2,32]{2,1,0,5,4,3:T(2,128)}, f32[4,2,32,3,2,32]{2,1,0,5,4,3:T(2,128)}) fusion(f32[1,2,2,32,3,3,32]{3,2,1,0,6,5,4:T(2,128)S(1)} %pad_bitcast_fusion.2, f32[2,2,2,32,3,3,32]{3,2,1,0,6,5,4:T(2,128)S(1)} %reshape.57, f32[1,2,2,32,3,3,32]{3,2,1,0,6,5,4:T(2,128)S(1)} %pad_bitcast_fusion.3), kind=kLoop, calls=%fused_computation.19 | loop fusion | flops 196608 | bytes 983040 | tf_op jit(solution)/shard_map/squeeze | solution.py:78
  72.8 7.0 %collective-permute-start.7 = (f32[4,2,32,3,2,32]{2,1,0,5,4,3:T(2,128)}, f32[4,2,32,3,2,32]{2,1,0,5,4,3:T(2,128)}, u32[]{:S(2)}, u32[]{:S(2)}) collective-permute-start(f32[4,2,32,3,2,32]{2,1,0,5,4,3:T(2,128)} %get-tuple-element.13), channel_id=1, source_target_pairs={{1,0},{2,1},{3,2},{4,3},{5,4},{6,5},{7,6},{8,7},{9,8},{10,9},{11,1... | collective-permute-start | bytes 589832 | tf_op jit(solution)/shard_map/ppermute | solution.py:17
  79.7 2.1 %collective-permute-start.6 = (f32[4,2,32,3,2,32]{2,1,0,5,4,3:T(2,128)}, f32[4,2,32,3,2,32]{2,1,0,5,4,3:T(2,128)}, u32[]{:S(2)}, u32[]{:S(2)}) collective-permute-start(f32[4,2,32,3,2,32]{2,1,0,5,4,3:T(2,128)} %get-tuple-element.12), channel_id=1, source_target_pairs={{0,1},{1,2},{2,3},{3,4},{4,5},{5,6},{6,7},{7,8},{8,9},{9,10},{10,1... | collective-permute-start | bytes 589832 | tf_op jit(solution)/shard_map/ppermute | solution.py:17
  81.9 7.9 %copy.40 = f32[2,2,2,32,4,4,2,32]{7,6,5,4,3,2,1,0:T(2,128)} copy(f32[2,2,2,32,4,4,2,32]{3,7,6,5,4,2,1,0:T(8,128)} %get-tuple-element.2) | data formatting | bytes 2097152
  89.8 6.3 %reshape.56 = f32[256,1024]{1,0:T(8,128)S(1)} reshape(f32[2,2,2,32,4,4,2,32]{7,6,5,4,3,2,1,0:T(2,128)} %copy.40) | data formatting | bytes 2097152 | tf_op jit(solution)/shard_map/reshape | solution.py:52
  96.1 1.6 pad_bitcast_fusion
  97.6 3.5 %collective-permute-done.6 = f32[4,2,32,3,2,32]{2,1,0,5,4,3:T(2,128)} collective-permute-done((f32[4,2,32,3,2,32]{2,1,0,5,4,3:T(2,128)}, f32[4,2,32,3,2,32]{2,1,0,5,4,3:T(2,128)}, u32[]{:S(2)}, u32[]{:S(2)}) %collective-permute-start.6) | collective-permute-done | bytes 196640 | tf_op jit(solution)/shard_map/ppermute | solution.py:17
  101.1 1.6 pad_bitcast_fusion.1
  102.7 4.1 %pad_maximum_fusion = f32[4,4,2,32,3,3,32]{3,2,1,0,6,5,4:T(2,128)} fusion(f32[4,1,2,32,3,3,32]{3,2,1,0,6,5,4:T(2,128)S(1)} %pad_bitcast_fusion, f32[1,2,2,32,3,3,32]{3,2,1,0,6,5,4:T(2,128)S(1)} %pad_bitcast_fusion.2, f32[2,2,2,32,3,3,32]{3,2,1,0,6,5,4:T(2,128)S(1)} %reshape.57, f32[1,2,2,32,3,3,32]{3,2,1,0,6,5,4:T(2,128)S(1)} %pad_bitcast_fusion.3, ...), kind=kLoop, calls=%fused_computation.8 | loop fusion | flops 1179648 | bytes 2359296 | tf_op jit(solution)/shard_map/concatenate | solution.py:81
  106.7 6.9 %reshape.58 = f32[1024,288]{0,1:T(8,128)S(1)} reshape(f32[4,4,2,32,3,3,32]{3,2,1,0,6,5,4:T(2,128)} %pad_maximum_fusion) | data formatting | bytes 2359296 | tf_op jit(solution)/shard_map/reshape | solution.py:90
  113.7 1.1 fusion.15
  114.8 0.6 fusion.16
  115.5 0.7 reshape.59
  116.2 1.1 pad_slice_fusion.7
  117.3 1.1 stack_reshape_squeeze.35
  118.4 0.1 stack_reshape_squeeze.34
  118.5 0.1 stack_reshape_squeeze.33
  118.7 3.1 %collective-permute-start.9 = (f32[3,32,288]{2,1,0:T(8,128)S(1)}, f32[3,32,288]{2,1,0:T(8,128)S(1)}, u32[]{:S(2)}, u32[]{:S(2)}) collective-permute-start(f32[3,32,288]{2,1,0:T(8,128)S(1)} %pad_maximum_fusion.7), channel_id=1, source_target_pairs={{32,0},{64,32},{96,64},{128,96},{160,128},{192,160},{224,192},{256... | collective-permute-start | bytes 331784 | tf_op jit(solution)/shard_map/ppermute | solution.py:17
  121.8 0.1 stack_reshape_squeeze.32
  122.0 0.1 stack_reshape_squeeze.31
  122.1 0.1 stack_reshape_squeeze.30
  122.3 1.9 %collective-permute-start.8 = (f32[3,32,288]{2,1,0:T(8,128)S(1)}, f32[3,32,288]{2,1,0:T(8,128)S(1)}, u32[]{:S(2)}, u32[]{:S(2)}) collective-permute-start(f32[3,32,288]{2,1,0:T(8,128)S(1)} %pad_maximum_fusion.6), channel_id=1, source_target_pairs={{0,32},{32,64},{64,96},{96,128},{128,160},{160,192},{192,224},{224... | collective-permute-start | bytes 331784 | tf_op jit(solution)/shard_map/ppermute | solution.py:17
  124.2 0.1 stack_reshape_squeeze.29
  124.4 0.1 stack_reshape_squeeze.28
  124.5 0.1 stack_reshape_squeeze.27
  124.7 5.3 %collective-permute-done.8 = f32[3,32,288]{2,1,0:T(8,128)S(1)} collective-permute-done((f32[3,32,288]{2,1,0:T(8,128)S(1)}, f32[3,32,288]{2,1,0:T(8,128)S(1)}, u32[]{:S(2)}, u32[]{:S(2)}) %collective-permute-start.8) | collective-permute-done | bytes 110624 | tf_op jit(solution)/shard_map/ppermute | solution.py:17
  130.0 2.6 %collective-permute-start.11 = (f32[32,288]{1,0:T(8,128)S(1)}, f32[32,288]{1,0:T(8,128)S(1)}, u32[]{:S(2)}, u32[]{:S(2)}) collective-permute-start(f32[32,288]{1,0:T(8,128)S(1)} %get-tuple-element.32), channel_id=1, source_target_pairs={{1,0},{2,1},{3,2},{4,3},{5,4},{6,5},{7,6},{8,7},{9,8},{10,9},{11,1... | collective-permute-start | bytes 110600 | tf_op jit(solution)/shard_map/ppermute | solution.py:17
  132.6 3.2 %collective-permute-start.10 = (f32[32,288]{1,0:T(8,128)S(1)}, f32[32,288]{1,0:T(8,128)S(1)}, u32[]{:S(2)}, u32[]{:S(2)}) collective-permute-start(f32[32,288]{1,0:T(8,128)S(1)} %get-tuple-element.31), channel_id=1, source_target_pairs={{0,1},{1,2},{2,3},{3,4},{4,5},{5,6},{6,7},{7,8},{8,9},{9,10},{10,1... | collective-permute-start | bytes 110600 | tf_op jit(solution)/shard_map/ppermute | solution.py:17
  136.7 5.2 %collective-permute-done.10 = f32[32,288]{1,0:T(8,128)S(1)} collective-permute-done((f32[32,288]{1,0:T(8,128)S(1)}, f32[32,288]{1,0:T(8,128)S(1)}, u32[]{:S(2)}, u32[]{:S(2)}) %collective-permute-start.10) | collective-permute-done | bytes 36896 | tf_op jit(solution)/shard_map/ppermute | solution.py:17
  142.0 1.9 %collective-permute-start.14 = (f32[33,288]{1,0:T(8,128)S(1)}, f32[33,288]{1,0:T(8,128)S(1)}, u32[]{:S(2)}, u32[]{:S(2)}) collective-permute-start(f32[33,288]{1,0:T(8,128)S(1)} %concatenate.87), channel_id=1, source_target_pairs={{0,32},{32,64},{64,96},{96,0},{128,160},{160,192},{192,224},{224,1... | collective-permute-start | bytes 114056 | tf_op jit(solution)/shard_map/ppermute | solution.py:114
  143.9 1.9 %collective-permute-start.13 = (f32[33,288]{1,0:T(8,128)S(1)}, f32[33,288]{1,0:T(8,128)S(1)}, u32[]{:S(2)}, u32[]{:S(2)}) collective-permute-start(f32[33,288]{1,0:T(8,128)S(1)} %concatenate.87), channel_id=1, source_target_pairs={{0,64},{32,96},{64,0},{96,32},{128,192},{160,224},{192,128},{224,1... | collective-permute-start | bytes 114056 | tf_op jit(solution)/shard_map/ppermute | solution.py:114
  145.8 3.6 %collective-permute-start.12 = (f32[33,288]{1,0:T(8,128)S(1)}, f32[33,288]{1,0:T(8,128)S(1)}, u32[]{:S(2)}, u32[]{:S(2)}) collective-permute-start(f32[33,288]{1,0:T(8,128)S(1)} %concatenate.87), channel_id=1, source_target_pairs={{0,96},{32,0},{64,32},{96,64},{128,224},{160,128},{192,160},{224,1... | collective-permute-start | bytes 114056 | tf_op jit(solution)/shard_map/ppermute | solution.py:114
  149.5 0.5 slice.229
  151.3 0.6 slice.227
  153.3 0.5 slice.225
  158.6 0.7 maximum_bitcast_fusion.1
  (62 shorter events, 1.3 us)
Async XLA Ops:
  0.6 7.5 %copy-start = (f32[2,2,2,32,32]{4,3,2,1,0:T(8,128)S(1)}, f32[2,2,2,32,32]{4,3,2,1,0:T(8,128)}, u32[]{:S(2)}) copy-start(f32[2,2,2,32,32]{4,3,2,1,0:T(8,128)} %param.11) | copy-start | bytes 98308
  1.6 12.9 %collective-permute-start.1 = (f32[2,2,32,32]{3,2,1,0:T(8,128)S(1)}, f32[2,2,32,32]{3,2,1,0:T(8,128)S(1)}, u32[]{:S(2)}, u32[]{:S(2)}) collective-permute-start(f32[2,2,32,32]{3,2,1,0:T(8,128)S(1)} %get-tuple-element.34), channel_id=1, source_target_pairs={{32,0},{64,32},{96,64},{128,96},{160,128},{192,160},{224,192},{256... | collective-permute-start | bytes 49160 | tf_op jit(solution)/shard_map/ppermute | solution.py:17
  3.5 11.0 %collective-permute-start = (f32[2,2,32,32]{3,2,1,0:T(8,128)S(1)}, f32[2,2,32,32]{3,2,1,0:T(8,128)S(1)}, u32[]{:S(2)}, u32[]{:S(2)}) collective-permute-start(f32[2,2,32,32]{3,2,1,0:T(8,128)S(1)} %get-tuple-element.33), channel_id=1, source_target_pairs={{0,32},{32,64},{64,96},{96,128},{128,160},{160,192},{192,224},{224... | collective-permute-start | bytes 49160 | tf_op jit(solution)/shard_map/ppermute | solution.py:17
  14.0 0.9 copy-start.4
  15.0 26.1 %collective-permute-start.3 = (f32[4,2,32,32]{3,2,1,0:T(8,128)S(1)}, f32[4,2,32,32]{3,2,1,0:T(8,128)S(1)}, u32[]{:S(2)}, u32[]{:S(2)}) collective-permute-start(f32[4,2,32,32]{3,2,1,0:T(8,128)S(1)} %get-tuple-element.26), channel_id=1, source_target_pairs={{1,0},{2,1},{3,2},{4,3},{5,4},{6,5},{7,6},{8,7},{9,8},{10,9},{11,1... | collective-permute-start | bytes 98312 | tf_op jit(solution)/shard_map/ppermute | solution.py:17
  19.6 21.6 %collective-permute-start.2 = (f32[4,2,32,32]{3,2,1,0:T(8,128)S(1)}, f32[4,2,32,32]{3,2,1,0:T(8,128)S(1)}, u32[]{:S(2)}, u32[]{:S(2)}) collective-permute-start(f32[4,2,32,32]{3,2,1,0:T(8,128)S(1)} %get-tuple-element.25), channel_id=1, source_target_pairs={{0,1},{1,2},{2,3},{3,4},{4,5},{5,6},{6,7},{7,8},{8,9},{9,10},{10,1... | collective-permute-start | bytes 98312 | tf_op jit(solution)/shard_map/ppermute | solution.py:17
  21.5 4.9 %copy-start.7 = (f32[9]{0:T(128)S(1)}, f32[9]{0:T(128)}, u32[]{:S(2)}) copy-start(f32[9]{0:T(128)} %constant.7.clone) | copy-start | bytes 112
  34.7 7.2 %copy-start.6 = (f32[4,4,3,3]{1,0,3,2:T(4,128)S(1)}, f32[4,4,3,3]{1,0,3,2:T(4,128)}, u32[]{:S(2)}) copy-start(f32[4,4,3,3]{1,0,3,2:T(4,128)} %constant.6.clone) | copy-start | bytes 1732
  54.7 11.0 %copy-start.2 = (f32[256,288]{0,1:T(8,128)}, f32[256,288]{0,1:T(8,128)S(1)}, u32[]{:S(2)}) copy-start(f32[256,288]{0,1:T(8,128)S(1)} %fusion) | copy-start | bytes 884740
  56.1 9.4 %collective-permute-start.5 = (f32[2,2,32,2,3,32]{2,1,0,5,4,3:T(2,128)S(1)}, f32[2,2,32,2,3,32]{2,1,0,5,4,3:T(2,128)S(1)}, u32[]{:S(2)}, u32[]{:S(2)}) collective-permute-start(f32[2,2,32,2,3,32]{2,1,0,5,4,3:T(2,128)S(1)} %get-tuple-element.24), channel_id=1, source_target_pairs={{32,0},{64,32},{96,64},{128,96},{160,128},{192,160},{224,192},{256... | collective-permute-start | bytes 294920 | tf_op jit(solution)/shard_map/ppermute | solution.py:17
  60.2 10.3 %collective-permute-start.4 = (f32[2,2,32,2,3,32]{2,1,0,5,4,3:T(2,128)S(1)}, f32[2,2,32,2,3,32]{2,1,0,5,4,3:T(2,128)S(1)}, u32[]{:S(2)}, u32[]{:S(2)}) collective-permute-start(f32[2,2,32,2,3,32]{2,1,0,5,4,3:T(2,128)S(1)} %get-tuple-element.23), channel_id=1, source_target_pairs={{0,32},{32,64},{64,96},{96,128},{128,160},{160,192},{192,224},{224... | collective-permute-start | bytes 294920 | tf_op jit(solution)/shard_map/ppermute | solution.py:17
  72.8 23.3 %collective-permute-start.7 = (f32[4,2,32,3,2,32]{2,1,0,5,4,3:T(2,128)}, f32[4,2,32,3,2,32]{2,1,0,5,4,3:T(2,128)}, u32[]{:S(2)}, u32[]{:S(2)}) collective-permute-start(f32[4,2,32,3,2,32]{2,1,0,5,4,3:T(2,128)} %get-tuple-element.13), channel_id=1, source_target_pairs={{1,0},{2,1},{3,2},{4,3},{5,4},{6,5},{7,6},{8,7},{9,8},{10,9},{11,1... | collective-permute-start | bytes 589832 | tf_op jit(solution)/shard_map/ppermute | solution.py:17
  79.7 21.4 %collective-permute-start.6 = (f32[4,2,32,3,2,32]{2,1,0,5,4,3:T(2,128)}, f32[4,2,32,3,2,32]{2,1,0,5,4,3:T(2,128)}, u32[]{:S(2)}, u32[]{:S(2)}) collective-permute-start(f32[4,2,32,3,2,32]{2,1,0,5,4,3:T(2,128)} %get-tuple-element.12), channel_id=1, source_target_pairs={{0,1},{1,2},{2,3},{3,4},{4,5},{5,6},{6,7},{7,8},{8,9},{9,10},{10,1... | collective-permute-start | bytes 589832 | tf_op jit(solution)/shard_map/ppermute | solution.py:17
  106.7 8.1 %copy-start.3 = (f32[256,288]{0,1:T(8,128)S(1)}, f32[256,288]{0,1:T(8,128)}, u32[]{:S(2)}) copy-start(f32[256,288]{0,1:T(8,128)} %copy-done.2) | copy-start | bytes 884740
  115.5 43.9 %copy-start.1 = (f32[2,2,2,32,32]{4,3,2,1,0:T(8,128)S(1)}, f32[2,2,2,32,32]{4,3,2,1,0:T(8,128)}, u32[]{:S(2)}) copy-start(f32[2,2,2,32,32]{4,3,2,1,0:T(8,128)} %param.11) | copy-start | bytes 98308
  116.2 19.7 %copy-start.8 = (s32[1,1,9]{2,1,0:T(1,128)S(1)}, s32[1,1,9]{2,1,0:T(1,128)}, u32[]{:S(2)}) copy-start(s32[1,1,9]{2,1,0:T(1,128)} %param.12) | copy-start | bytes 112
  118.7 6.0 %collective-permute-start.9 = (f32[3,32,288]{2,1,0:T(8,128)S(1)}, f32[3,32,288]{2,1,0:T(8,128)S(1)}, u32[]{:S(2)}, u32[]{:S(2)}) collective-permute-start(f32[3,32,288]{2,1,0:T(8,128)S(1)} %pad_maximum_fusion.7), channel_id=1, source_target_pairs={{32,0},{64,32},{96,64},{128,96},{160,128},{192,160},{224,192},{256... | collective-permute-start | bytes 331784 | tf_op jit(solution)/shard_map/ppermute | solution.py:17
  122.3 7.7 %collective-permute-start.8 = (f32[3,32,288]{2,1,0:T(8,128)S(1)}, f32[3,32,288]{2,1,0:T(8,128)S(1)}, u32[]{:S(2)}, u32[]{:S(2)}) collective-permute-start(f32[3,32,288]{2,1,0:T(8,128)S(1)} %pad_maximum_fusion.6), channel_id=1, source_target_pairs={{0,32},{32,64},{64,96},{96,128},{128,160},{160,192},{192,224},{224... | collective-permute-start | bytes 331784 | tf_op jit(solution)/shard_map/ppermute | solution.py:17
  130.0 6.7 %collective-permute-start.11 = (f32[32,288]{1,0:T(8,128)S(1)}, f32[32,288]{1,0:T(8,128)S(1)}, u32[]{:S(2)}, u32[]{:S(2)}) collective-permute-start(f32[32,288]{1,0:T(8,128)S(1)} %get-tuple-element.32), channel_id=1, source_target_pairs={{1,0},{2,1},{3,2},{4,3},{5,4},{6,5},{7,6},{8,7},{9,8},{10,9},{11,1... | collective-permute-start | bytes 110600 | tf_op jit(solution)/shard_map/ppermute | solution.py:17
  132.6 9.3 %collective-permute-start.10 = (f32[32,288]{1,0:T(8,128)S(1)}, f32[32,288]{1,0:T(8,128)S(1)}, u32[]{:S(2)}, u32[]{:S(2)}) collective-permute-start(f32[32,288]{1,0:T(8,128)S(1)} %get-tuple-element.31), channel_id=1, source_target_pairs={{0,1},{1,2},{2,3},{3,4},{4,5},{5,6},{6,7},{7,8},{8,9},{9,10},{10,1... | collective-permute-start | bytes 110600 | tf_op jit(solution)/shard_map/ppermute | solution.py:17
  141.9 17.4 %copy-start.5 = (f32[32,288]{1,0:T(8,128)}, f32[32,288]{1,0:T(8,128)S(1)}, u32[]{:S(2)}) copy-start(f32[32,288]{1,0:T(8,128)S(1)} %fusion.13) | copy-start | bytes 110596
  142.0 7.5 %collective-permute-start.14 = (f32[33,288]{1,0:T(8,128)S(1)}, f32[33,288]{1,0:T(8,128)S(1)}, u32[]{:S(2)}, u32[]{:S(2)}) collective-permute-start(f32[33,288]{1,0:T(8,128)S(1)} %concatenate.87), channel_id=1, source_target_pairs={{0,32},{32,64},{64,96},{96,0},{128,160},{160,192},{192,224},{224,1... | collective-permute-start | bytes 114056 | tf_op jit(solution)/shard_map/ppermute | solution.py:114
  143.9 7.4 %collective-permute-start.13 = (f32[33,288]{1,0:T(8,128)S(1)}, f32[33,288]{1,0:T(8,128)S(1)}, u32[]{:S(2)}, u32[]{:S(2)}) collective-permute-start(f32[33,288]{1,0:T(8,128)S(1)} %concatenate.87), channel_id=1, source_target_pairs={{0,64},{32,96},{64,0},{96,32},{128,192},{160,224},{192,128},{224,1... | collective-permute-start | bytes 114056 | tf_op jit(solution)/shard_map/ppermute | solution.py:114
  145.8 7.4 %collective-permute-start.12 = (f32[33,288]{1,0:T(8,128)S(1)}, f32[33,288]{1,0:T(8,128)S(1)}, u32[]{:S(2)}, u32[]{:S(2)}) collective-permute-start(f32[33,288]{1,0:T(8,128)S(1)} %concatenate.87), channel_id=1, source_target_pairs={{0,96},{32,0},{64,32},{96,64},{128,224},{160,128},{192,160},{224,1... | collective-permute-start | bytes 114056 | tf_op jit(solution)/shard_map/ppermute | solution.py:114
where the time goes:
time: 161 us; the launch traced here: 159 us
  local copies, waits for them, and re-layouts  65.8 us (41%)
  starting transfers between devices  44.3 us (28%)
  waiting for transfers between devices  22.1 us (14%)
  other arithmetic  13.9 us (9%)
  between operations  9.46 us (6%)
  matrix products  3.8 us (2%)
    ppermute x12, starting transfers between devices, shift(): return lax.ppermute(block, axis, pairs)  36.8 us
    ppermute x12, waiting for transfers between devices, shift(): return lax.ppermute(block, axis, pairs)  22.1 us
    unnamed x27, local copies, waits for them, and re-layouts  16.8 us
    ppermute x3, starting transfers between devices, local(): members.append(lax.ppermute(payload, 'gx', pairs))  7.48 us
    reshape x1, local copies, waits for them, and re-layouts, local(): prolong_frame.reshape(32 * width, 9 * width)  6.94 us
    mul x1, local copies, waits for them, and re-layouts, local(): tent_frame[:, :, :, :, None, None, :] * mask[:, :, None, None, :, :, None]  6.9 us
    reshape x1, local copies, waits for them, and re-layouts, local(): scaled_pos = both[:, :, :, width:].reshape(8 * width, 32 * width)  6.27 us
    reshape x1, local copies, waits for them, and re-layouts, local(): stencil_pos = both[:, :, :, :width].reshape(8 * width, 32 * width)  6.26 us
  transfers between devices with their start and end apart: 15, of which 5 were waited for; matrix products, arithmetic and copies ran while one was open for 29% of the time, Pallas kernels for 0%

commit v1 on v0

v1 whole, which is shorter than its diff:
```python
import jax
import jax.numpy as jnp
import numpy as np
from jax import lax
from jax.sharding import PartitionSpec as P

OMEGA = 0.6
HI = lax.Precision.HIGHEST


def shift(block, axis, forward):
    count = lax.axis_size(axis)
    if forward:
        pairs = [(i, i + 1) for i in range(count - 1)]
    else:
        pairs = [(i + 1, i) for i in range(count - 1)]
    return lax.ppermute(block, axis, pairs)


def offset_number(shift_x, shift_y, shift_z):
    return 9 * (shift_x + 1) + 3 * (shift_y + 1) + (shift_z + 1)


POSITIONS = [(pos_x, pos_y, pos_z) for pos_x in range(4) for pos_y in range(4) for pos_z in range(2)]
CELLS = [(cell_x, cell_y, cell_z) for cell_x in range(2) for cell_y in range(2) for cell_z in range(2)]
REACH = [0, 1, 1, 2]


def to_positions(rows):
    width = rows.shape[-1] // 27
    lines = []
    for cell in CELLS:
        block = rows[cell]
        pieces = []
        for pos_x, pos_y, pos_z in POSITIONS:
            shift_x, shift_y, shift_z = pos_x - 1 - cell[0], pos_y - 1 - cell[1], pos_z - cell[2]
            if max(abs(shift_x), abs(shift_y), abs(shift_z)) <= 1:
                number = offset_number(shift_x, shift_y, shift_z)
                pieces.append(block[:, number * width : (number + 1) * width])
            else:
                pieces.append(jnp.zeros((block.shape[0], width), block.dtype))
        lines.append(jnp.concatenate(pieces, axis=1))
    return jnp.concatenate(lines, axis=0)


def local(stencil, pattern, tentative, diag_inverse, coarse_pattern, slot):
    width = tentative.shape[-1]
    zeros = jnp.zeros((width, width), jnp.float32)
    keep_mask = jnp.repeat(pattern.astype(jnp.float32), width, axis=-1)[:, :, :, None, :]
    stencil_rows = stencil * keep_mask
    scaled_rows = jnp.einsum("xyzrs,xyzsk->xyzrk", diag_inverse, stencil_rows, precision=HI)
    stencil_pos = to_positions(stencil_rows)
    scaled_pos = to_positions(scaled_rows)

    tent = {}
    for cell in CELLS:
        tent[(cell[0] + 1, cell[1] + 1, cell[2])] = tentative[cell]
    left = shift(tentative[1], "gx", True)
    right = shift(tentative[0], "gx", False)
    for cell_y in range(2):
        for cell_z in range(2):
            tent[(0, cell_y + 1, cell_z)] = left[cell_y, cell_z]
            tent[(3, cell_y + 1, cell_z)] = right[cell_y, cell_z]
    send_high = jnp.stack([tent[(pos_x, 2, pos_z)] for pos_x in range(4) for pos_z in range(2)])
    send_low = jnp.stack([tent[(pos_x, 1, pos_z)] for pos_x in range(4) for pos_z in range(2)])
    low = shift(send_high, "gy", True)
    high = shift(send_low, "gy", False)
    for pos_x in range(4):
        for pos_z in range(2):
            tent[(pos_x, 0, pos_z)] = low[2 * pos_x + pos_z]
            tent[(pos_x, 3, pos_z)] = high[2 * pos_x + pos_z]

    tent_rows = []
    for pos in POSITIONS:
        target = 3 * REACH[pos[0]] + REACH[pos[1]]
        tent_rows.append(
            jnp.concatenate([tent[pos] if number == target else zeros for number in range(9)], axis=1)
        )
    tent_agg = jnp.concatenate(tent_rows, axis=0)
    smoothed = jnp.dot(scaled_pos, tent_agg, precision=HI)
    own_tent = jnp.concatenate(
        [
            jnp.concatenate([tentative[cell] if number == 4 else zeros for number in range(9)], axis=1)
            for cell in CELLS
        ],
        axis=0,
    )
    prolong_own = own_tent - OMEGA * smoothed

    prolong = {}
    for number, cell in enumerate(CELLS):
        prolong[(cell[0] + 1, cell[1] + 1, cell[2])] = prolong_own[number * width : (number + 1) * width]
    to_low = jnp.stack([prolong[(1, pos_y, pos_z)][:, : 6 * width] for pos_y in (1, 2) for pos_z in range(2)])
    to_high = jnp.stack([prolong[(2, pos_y, pos_z)][:, 3 * width :] for pos_y in (1, 2) for pos_z in range(2)])
    from_right = shift(to_low, "gx", False)
    from_left = shift(to_high, "gx", True)
    wide_zeros = jnp.zeros((width, 3 * width), jnp.float32)
    for index, (pos_y, pos_z) in enumerate((pos_y, pos_z) for pos_y in (1, 2) for pos_z in range(2)):
        prolong[(3, pos_y, pos_z)] = jnp.concatenate([wide_zeros, from_right[index]], axis=1)
        prolong[(0, pos_y, pos_z)] = jnp.concatenate([from_left[index], wide_zeros], axis=1)

    def keep_y(block, first):
        return jnp.concatenate(
            [block[:, (3 * row + first) * width : (3 * row + first + 2) * width] for row in range(3)], axis=1
        )

    def spread_y(block, first):
        pieces = []
        for row in range(3):
            part = block[:, 2 * row * width : (2 * row + 2) * width]
            pieces.extend([zeros, part] if first == 1 else [part, zeros])
        return jnp.concatenate(pieces, axis=1)

    to_low = jnp.stack([keep_y(prolong[(pos_x, 1, pos_z)], 0) for pos_x in range(4) for pos_z in range(2)])
    to_high = jnp.stack([keep_y(prolong[(pos_x, 2, pos_z)], 1) for pos_x in range(4) for pos_z in range(2)])
    from_high = shift(to_low, "gy", False)
    from_low = shift(to_high, "gy", True)
    for pos_x in range(4):
        for pos_z in range(2):
            prolong[(pos_x, 3, pos_z)] = spread_y(from_high[2 * pos_x + pos_z], 1)
            prolong[(pos_x, 0, pos_z)] = spread_y(from_low[2 * pos_x + pos_z], 0)
    prolong_frame = jnp.concatenate([prolong[pos] for pos in POSITIONS], axis=0)

    applied = jnp.dot(stencil_pos, prolong_frame, precision=HI)
    product = lax.dot_general(prolong_own, applied, (((0,), (0,)), ((), ())), precision=HI)
    partial_rows = []
    for row_x in range(3):
        line = []
        for row_y in range(3):
            rows = product[(3 * row_x + row_y) * width : (3 * row_x + row_y + 1) * width]
            pieces = []
            for shift_x in (-1, 0, 1):
                for shift_y in (-1, 0, 1):
                    col_x, col_y = row_x + shift_x, row_y + shift_y
                    if 0 <= col_x <= 2 and 0 <= col_y <= 2:
                        number = 3 * col_x + col_y
                        pieces.append(rows[:, number * width : (number + 1) * width])
                    else:
                        pieces.append(zeros)
            line.append(jnp.concatenate(pieces, axis=1))
        partial_rows.append(jnp.stack(line))

    acc = partial_rows[1] + shift(partial_rows[2], "gx", True) + shift(partial_rows[0], "gx", False)
    total = acc[1] + shift(acc[2], "gy", True) + shift(acc[0], "gy", False)
    column_mask = jnp.repeat(coarse_pattern[0, 0].astype(jnp.float32), width)[None, :]
    coarse_block = total * column_mask

    slot_row = jnp.broadcast_to(slot.astype(jnp.float32).reshape(1, 1), (1, 9 * width))
    payload = jnp.concatenate([coarse_block, slot_row], axis=0)
    count = lax.axis_size("gx")
    members = [payload]
    for step in (1, 2, 3):
        pairs = [(i, 4 * (i // 4) + (i % 4 + step) % 4) for i in range(count)]
        members.append(lax.ppermute(payload, "gx", pairs))
    grouped = []
    for target in range(4):
        chosen = jnp.zeros_like(coarse_block)
        for member in members:
            chosen = jnp.where(member[width:, :1] == float(target), member[:width], chosen)
        grouped.append(chosen)
    grouped = jnp.stack(grouped)
    return (coarse_block[None, None], grouped[None, None])


def solution(mesh):
    placed = (
        P("gx", "gy", None, None, None),
        P("gx", "gy", None, None),
        P("gx", "gy", None, None, None),
        P("gx", "gy", None, None, None),
        P("gx", "gy", None),
        P("gx", "gy"),
    )
    return jax.shard_map(
        local,
        mesh=mesh,
        in_specs=placed,
        out_specs=(P("gx", "gy", None, None), P("gx", "gy", None, None, None)),
        check_vma=False,
    )
```

time: 161 us -> 168 us (1.043)
  the two profiles are of different devices: /device:TPU:288 before, /device:TPU:159 now
where the time goes in v1:
time: 168 us; the launch traced here: 165 us
  local copies, waits for them, and re-layouts  62.1 us (37%)
  starting transfers between devices  57.4 us (34%)
  waiting for transfers between devices  20.1 us (12%)
  between operations  10.4 us (6%)
  other arithmetic  9.85 us (6%)
  matrix products  5.3 us (3%)
    ppermute x12, starting transfers between devices, shift(): return lax.ppermute(block, axis, pairs)  45.7 us
    ppermute x12, waiting for transfers between devices, shift(): return lax.ppermute(block, axis, pairs)  20 us
    concatenate x32, local copies, waits for them, and re-layouts, spread_y(): return jnp.concatenate(pieces, axis=1)  13.8 us
    ppermute x3, starting transfers between devices, local(): members.append(lax.ppermute(payload, 'gx', pairs))  11.7 us
    concatenate x16, local copies, waits for them, and re-layouts, to_positions(): lines.append(jnp.concatenate(pieces, axis=1))  9.28 us
    unnamed x40, other arithmetic  6.83 us
    unnamed x81, local copies, waits for them, and re-layouts  6.25 us
    slice x8, local copies, waits for them, and re-layouts, to_positions(): pieces.append(block[:, number * width:(number + 1) * width])  4.98 us
  transfers between devices with their start and end apart: 15, of which 7 were waited for; matrix products, arithmetic and copies ran while one was open for 22% of the time, Pallas kernels for 0%

profile of v1, /device:TPU:159, one launch (start us, length us, event | category | flops | bytes accessed | tf_op | source)
XLA Modules:
  0.0 165.1 jit_solution(1085934366636351755)
XLA Ops:
  0.6 1.6 slice_bitcast_fusion.32
  2.2 4.5 %collective-permute-start = (f32[2,2,32,32]{3,2,1,0:T(8,128)}, f32[2,2,32,32]{3,2,1,0:T(8,128)}, u32[]{:S(2)}, u32[]{:S(2)}) collective-permute-start(f32[2,2,32,32]{3,2,1,0:T(8,128)} %get-tuple-element.121), channel_id=1, source_target_pairs={{0,32},{32,64},{64,96},{96,128},{128,160},{160,192},{192,224},{224... | collective-permute-start | bytes 49160 | tf_op jit(solution)/shard_map/ppermute | solution.py:17
  6.8 1.9 %collective-permute-start.1 = (f32[2,2,32,32]{3,2,1,0:T(8,128)}, f32[2,2,32,32]{3,2,1,0:T(8,128)}, u32[]{:S(2)}, u32[]{:S(2)}) collective-permute-start(f32[2,2,32,32]{3,2,1,0:T(8,128)} %get-tuple-element.120), channel_id=1, source_target_pairs={{32,0},{64,32},{96,64},{128,96},{160,128},{192,160},{224,192},{256... | collective-permute-start | bytes 49160 | tf_op jit(solution)/shard_map/ppermute | solution.py:17
  8.7 1.5 slice_bitcast_fusion.78
  11.1 1.3 broadcast_multiply_fusion
  12.5 0.9 convolution_bitcast_fusion
  16.4 0.9 constant_dynamic-update-slice_fusion.63
  17.4 1.6 concatenate.351
  19.0 0.9 constant_dynamic-update-slice_fusion.6
  19.9 1.7 %fusion.38 = (f32[32,64]{1,0:T(8,128)}, f32[32,64]{1,0:T(8,128)}, f32[32,64]{1,0:T(8,128)}, f32[32,64]{1,0:T(8,128)}, f32[32,64]{1,0:T(8,128)}, /*index=5*/f32[3...) fusion(f32[32,864]{1,0:T(8,128)S(1)} %get-tuple-element.18, ...), kind=kLoop, calls=%fused_computation.294 | loop fusion | bytes 294912 | tf_op jit(solution)/shard_map/slice | solution.py:39
  21.6 1.6 concatenate.352
  23.2 0.9 constant_dynamic-update-slice_fusion.5
  24.1 1.6 concatenate.353
  25.7 0.9 constant_dynamic-update-slice_fusion.4
  27.4 1.0 concatenate.354
  28.4 0.9 concatenate.355
  30.1 0.9 concatenate.356
  32.6 0.8 constant_dynamic-update-slice_fusion.23
  35.7 4.3 %collective-permute-start.2 = (f32[8,32,32]{2,1,0:T(8,128)S(1)}, f32[8,32,32]{2,1,0:T(8,128)S(1)}, u32[]{:S(2)}, u32[]{:S(2)}) collective-permute-start(f32[8,32,32]{2,1,0:T(8,128)S(1)} %get-tuple-element.295), channel_id=1, source_target_pairs={{0,1},{1,2},{2,3},{3,4},{4,5},{5,6},{6,7},{7,8},{8,9},{9,10},{10,1... | collective-permute-start | bytes 98312 | tf_op jit(solution)/shard_map/ppermute | solution.py:17
  40.1 1.9 %collective-permute-start.3 = (f32[8,32,32]{2,1,0:T(8,128)S(1)}, f32[8,32,32]{2,1,0:T(8,128)S(1)}, u32[]{:S(2)}, u32[]{:S(2)}) collective-permute-start(f32[8,32,32]{2,1,0:T(8,128)S(1)} %get-tuple-element.294), channel_id=1, source_target_pairs={{1,0},{2,1},{3,2},{4,3},{5,4},{6,5},{7,6},{8,7},{9,8},{10,9},{11,1... | collective-permute-start | bytes 98312 | tf_op jit(solution)/shard_map/ppermute | solution.py:17
  42.0 0.8 slice_bitcast_fusion.76
  42.8 1.4 slice_bitcast_fusion.74
  45.2 5.1 %collective-permute-done.3 = f32[8,32,32]{2,1,0:T(8,128)S(1)} collective-permute-done((f32[8,32,32]{2,1,0:T(8,128)S(1)}, f32[8,32,32]{2,1,0:T(8,128)S(1)}, u32[]{:S(2)}, u32[]{:S(2)}) %collective-permute-start.3) | collective-permute-done | bytes 32800 | tf_op jit(solution)/shard_map/ppermute | solution.py:17
  53.3 0.8 copy.242
  54.8 0.8 copy.240
  55.6 0.8 copy.239
  56.4 0.8 copy.238
  57.1 0.8 constant_dynamic-update-slice_fusion.33
  57.9 0.8 constant_dynamic-update-slice_fusion.32
  58.8 0.8 constant_dynamic-update-slice_fusion.31
  59.6 0.8 constant_dynamic-update-slice_fusion.30
  60.4 0.8 constant_dynamic-update-slice_fusion.29
  61.5 1.6 concatenate.349
  63.0 2.6 %fusion = f32[256,288]{0,1:T(8,128)S(1)} fusion(f32[256,288]{0,1:T(8,128)S(1)} %concatenate.349, f32[256,1024]{1,0:T(8,128)S(1)} %constant_dynamic-update-slice_fusion, f32[1024,288]{1,0:T(8,128)S(1)} %constant_dynamic-update-slice_fusion.24), kind=kOutput, calls=%fused_computation.2 | convolution fusion | flops 906117120 | bytes 2818048 | tf_op jit(solution)/shard_map/dot_general | solution.py:80
  66.2 2.8 %collective-permute-start.5 = (f32[4,32,192]{1,2,0:T(8,128)S(1)}, f32[4,32,192]{1,2,0:T(8,128)S(1)}, u32[]{:S(2)}, u32[]{:S(2)}) collective-permute-start(f32[4,32,192]{1,2,0:T(8,128)S(1)} %pad_maximum_fusion.1), channel_id=1, source_target_pairs={{32,0},{64,32},{96,64},{128,96},{160,128},{192,160},{224,192},{256... | collective-permute-start | bytes 294920 | tf_op jit(solution)/shard_map/ppermute | solution.py:17
  69.1 3.7 %collective-permute-start.4 = (f32[4,32,192]{1,2,0:T(8,128)S(1)}, f32[4,32,192]{1,2,0:T(8,128)S(1)}, u32[]{:S(2)}, u32[]{:S(2)}) collective-permute-start(f32[4,32,192]{1,2,0:T(8,128)S(1)} %pad_maximum_fusion), channel_id=1, source_target_pairs={{0,32},{32,64},{64,96},{96,128},{128,160},{160,192},{192,224},{224... | collective-permute-start | bytes 294920 | tf_op jit(solution)/shard_map/ppermute | solution.py:17
  74.6 2.0 %collective-permute-done.5 = f32[4,32,192]{1,2,0:T(8,128)S(1)} collective-permute-done((f32[4,32,192]{1,2,0:T(8,128)S(1)}, f32[4,32,192]{1,2,0:T(8,128)S(1)}, u32[]{:S(2)}, u32[]{:S(2)}) %collective-permute-start.5) | collective-permute-done | bytes 98336 | tf_op jit(solution)/shard_map/ppermute | solution.py:17
  79.7 1.9 %collective-permute-start.7 = (f32[8,32,192]{2,1,0:T(8,128)S(1)}, f32[8,32,192]{2,1,0:T(8,128)S(1)}, u32[]{:S(2)}, u32[]{:S(2)}) collective-permute-start(f32[8,32,192]{2,1,0:T(8,128)S(1)} %get-tuple-element.372), channel_id=1, source_target_pairs={{1,0},{2,1},{3,2},{4,3},{5,4},{6,5},{7,6},{8,7},{9,8},{10,9},{11,1... | collective-permute-start | bytes 589832 | tf_op jit(solution)/shard_map/ppermute | solution.py:17
  84.4 6.9 %collective-permute-start.6 = (f32[8,32,192]{2,1,0:T(8,128)S(1)}, f32[8,32,192]{2,1,0:T(8,128)S(1)}, u32[]{:S(2)}, u32[]{:S(2)}) collective-permute-start(f32[8,32,192]{2,1,0:T(8,128)S(1)} %get-tuple-element.373), channel_id=1, source_target_pairs={{0,1},{1,2},{2,3},{3,4},{4,5},{5,6},{6,7},{7,8},{8,9},{9,10},{10,1... | collective-permute-start | bytes 589832 | tf_op jit(solution)/shard_map/ppermute | solution.py:17
  92.2 0.8 copy.301
  93.2 0.8 copy.300
  94.0 1.8 %collective-permute-done.6 = f32[8,32,192]{2,1,0:T(8,128)S(1)} collective-permute-done((f32[8,32,192]{2,1,0:T(8,128)S(1)}, f32[8,32,192]{2,1,0:T(8,128)S(1)}, u32[]{:S(2)}, u32[]{:S(2)}) %collective-permute-start.6) | collective-permute-done | bytes 196640 | tf_op jit(solution)/shard_map/ppermute | solution.py:17
  96.0 0.8 copy.299
  97.8 0.8 copy.297
  98.8 0.8 copy.296
  100.7 0.8 copy.294
  101.6 0.8 copy.293
  102.5 0.8 copy.292
  103.5 0.8 copy.291
  105.4 0.8 copy.289
  106.3 0.8 copy.288
  107.2 0.8 copy.287
  108.2 0.8 copy.286
  108.9 3.3 %concatenate.433 = f32[1024,288]{0,1:T(8,128)S(1)} concatenate(f32[32,288]{0,1:T(8,128)} %copy.286, f32[32,288]{0,1:T(8,128)} %copy.287, f32[32,288]{0,1:T(8,128)S(1)} %concatenate.403, f32[32,288]{0,1:T(8,128)} %concatenate.404, f32[32,288]{0,1:T(8,128)} %concatenate.405, f32[32,288]{0,1:T(8,128)} %concatenate.406, f32[32,288]{0,1:T(8,128)} %copy.288, f32[32,288]{0,1:T(8,128)} %copy.289, ...), dimensions={0} | concatenate | bytes 2359296 | tf_op jit(solution)/shard_map/concatenate | solution.py:122
  112.2 1.1 fusion.66
  114.4 6.5 %collective-permute-start.8 = (f32[3,32,288]{2,1,0:T(8,128)S(1)}, f32[3,32,288]{2,1,0:T(8,128)S(1)}, u32[]{:S(2)}, u32[]{:S(2)}) collective-permute-start(f32[3,32,288]{2,1,0:T(8,128)S(1)} %pad_maximum_fusion.20), channel_id=1, source_target_pairs={{0,32},{32,64},{64,96},{96,128},{128,160},{160,192},{192,224},{224... | collective-permute-start | bytes 331784 | tf_op jit(solution)/shard_map/ppermute | solution.py:17
  121.1 1.9 %collective-permute-start.9 = (f32[3,32,288]{2,1,0:T(8,128)S(1)}, f32[3,32,288]{2,1,0:T(8,128)S(1)}, u32[]{:S(2)}, u32[]{:S(2)}) collective-permute-start(f32[3,32,288]{2,1,0:T(8,128)S(1)} %pad_maximum_fusion.21), channel_id=1, source_target_pairs={{32,0},{64,32},{96,64},{128,96},{160,128},{192,160},{224,192},{256... | collective-permute-start | bytes 331784 | tf_op jit(solution)/shard_map/ppermute | solution.py:17
  123.3 4.3 %collective-permute-done.9 = f32[3,32,288]{2,1,0:T(8,128)S(1)} collective-permute-done((f32[3,32,288]{2,1,0:T(8,128)S(1)}, f32[3,32,288]{2,1,0:T(8,128)S(1)}, u32[]{:S(2)}, u32[]{:S(2)}) %collective-permute-start.9) | collective-permute-done | bytes 110624 | tf_op jit(solution)/shard_map/ppermute | solution.py:17
  127.7 7.4 %collective-permute-start.10 = (f32[32,288]{1,0:T(8,128)S(1)}, f32[32,288]{1,0:T(8,128)S(1)}, u32[]{:S(2)}, u32[]{:S(2)}) collective-permute-start(f32[32,288]{1,0:T(8,128)S(1)} %get-tuple-element.100), channel_id=1, source_target_pairs={{0,1},{1,2},{2,3},{3,4},{4,5},{5,6},{6,7},{7,8},{8,9},{9,10},{10,1... | collective-permute-start | bytes 110600 | tf_op jit(solution)/shard_map/ppermute | solution.py:17
  135.1 1.9 %collective-permute-start.11 = (f32[32,288]{1,0:T(8,128)S(1)}, f32[32,288]{1,0:T(8,128)S(1)}, u32[]{:S(2)}, u32[]{:S(2)}) collective-permute-start(f32[32,288]{1,0:T(8,128)S(1)} %get-tuple-element.101), channel_id=1, source_target_pairs={{1,0},{2,1},{3,2},{4,3},{5,4},{6,5},{7,6},{8,7},{9,8},{10,9},{11,1... | collective-permute-start | bytes 110600 | tf_op jit(solution)/shard_map/ppermute | solution.py:17
  137.9 5.4 %collective-permute-done.11 = f32[32,288]{1,0:T(8,128)S(1)} collective-permute-done((f32[32,288]{1,0:T(8,128)S(1)}, f32[32,288]{1,0:T(8,128)S(1)}, u32[]{:S(2)}, u32[]{:S(2)}) %collective-permute-start.11) | collective-permute-done | bytes 36896 | tf_op jit(solution)/shard_map/ppermute | solution.py:17
  143.3 1.9 %collective-permute-start.12 = (f32[33,288]{1,0:T(8,128)S(1)}, f32[33,288]{1,0:T(8,128)S(1)}, u32[]{:S(2)}, u32[]{:S(2)}) collective-permute-start(f32[33,288]{1,0:T(8,128)S(1)} %concatenate.442), channel_id=1, source_target_pairs={{0,96},{32,0},{64,32},{96,64},{128,224},{160,128},{192,160},{224,1... | collective-permute-start | bytes 114056 | tf_op jit(solution)/shard_map/ppermute | solution.py:154
  145.2 5.8 %collective-permute-start.13 = (f32[33,288]{1,0:T(8,128)S(1)}, f32[33,288]{1,0:T(8,128)S(1)}, u32[]{:S(2)}, u32[]{:S(2)}) collective-permute-start(f32[33,288]{1,0:T(8,128)S(1)} %concatenate.442), channel_id=1, source_target_pairs={{0,64},{32,96},{64,0},{96,32},{128,192},{160,224},{192,128},{224,1... | collective-permute-start | bytes 114056 | tf_op jit(solution)/shard_map/ppermute | solution.py:154
  151.1 3.9 %collective-permute-start.14 = (f32[33,288]{1,0:T(8,128)S(1)}, f32[33,288]{1,0:T(8,128)S(1)}, u32[]{:S(2)}, u32[]{:S(2)}) collective-permute-start(f32[33,288]{1,0:T(8,128)S(1)} %concatenate.442), channel_id=1, source_target_pairs={{0,32},{32,64},{64,96},{96,0},{128,160},{160,192},{192,224},{224,1... | collective-permute-start | bytes 114056 | tf_op jit(solution)/shard_map/ppermute | solution.py:154
  (289 shorter events, 31.9 us)
Async XLA Ops:
  0.6 11.8 %copy-start = (f32[2,2,2,32,32]{4,3,2,1,0:T(8,128)S(1)}, f32[2,2,2,32,32]{4,3,2,1,0:T(8,128)}, u32[]{:S(2)}) copy-start(f32[2,2,2,32,32]{4,3,2,1,0:T(8,128)} %param.9) | copy-start | bytes 98308
  2.2 30.3 %collective-permute-start = (f32[2,2,32,32]{3,2,1,0:T(8,128)}, f32[2,2,32,32]{3,2,1,0:T(8,128)}, u32[]{:S(2)}, u32[]{:S(2)}) collective-permute-start(f32[2,2,32,32]{3,2,1,0:T(8,128)} %get-tuple-element.121), channel_id=1, source_target_pairs={{0,32},{32,64},{64,96},{96,128},{128,160},{160,192},{192,224},{224... | collective-permute-start | bytes 49160 | tf_op jit(solution)/shard_map/ppermute | solution.py:17
  6.8 27.5 %collective-permute-start.1 = (f32[2,2,32,32]{3,2,1,0:T(8,128)}, f32[2,2,32,32]{3,2,1,0:T(8,128)}, u32[]{:S(2)}, u32[]{:S(2)}) collective-permute-start(f32[2,2,32,32]{3,2,1,0:T(8,128)} %get-tuple-element.120), channel_id=1, source_target_pairs={{32,0},{64,32},{96,64},{128,96},{160,128},{192,160},{224,192},{256... | collective-permute-start | bytes 49160 | tf_op jit(solution)/shard_map/ppermute | solution.py:17
  27.4 3.7 %copy-start.5 = (f32[32,64]{1,0:T(8,128)S(1)}, f32[32,64]{1,0:T(8,128)}, u32[]{:S(2)}) copy-start(f32[32,64]{1,0:T(8,128)} %get-tuple-element.185) | copy-start | bytes 24580
  27.4 3.7 %copy-start.6 = (f32[32,64]{1,0:T(8,128)S(1)}, f32[32,64]{1,0:T(8,128)}, u32[]{:S(2)}) copy-start(f32[32,64]{1,0:T(8,128)} %get-tuple-element.186) | copy-start | bytes 24580
  27.4 3.8 %copy-start.7 = (f32[32,64]{1,0:T(8,128)S(1)}, f32[32,64]{1,0:T(8,128)}, u32[]{:S(2)}) copy-start(f32[32,64]{1,0:T(8,128)} %get-tuple-element.187) | copy-start | bytes 24580
  27.4 3.8 %copy-start.8 = (f32[32,64]{1,0:T(8,128)S(1)}, f32[32,64]{1,0:T(8,128)}, u32[]{:S(2)}) copy-start(f32[32,64]{1,0:T(8,128)} %get-tuple-element.188) | copy-start | bytes 24580
  27.4 3.8 %copy-start.9 = (f32[32,64]{1,0:T(8,128)S(1)}, f32[32,64]{1,0:T(8,128)}, u32[]{:S(2)}) copy-start(f32[32,64]{1,0:T(8,128)} %get-tuple-element.189) | copy-start | bytes 24580
  27.4 3.8 %copy-start.10 = (f32[32,64]{1,0:T(8,128)S(1)}, f32[32,64]{1,0:T(8,128)}, u32[]{:S(2)}) copy-start(f32[32,64]{1,0:T(8,128)} %get-tuple-element.190) | copy-start | bytes 24580
  27.4 3.8 %copy-start.11 = (f32[32,64]{1,0:T(8,128)S(1)}, f32[32,64]{1,0:T(8,128)}, u32[]{:S(2)}) copy-start(f32[32,64]{1,0:T(8,128)} %get-tuple-element.191) | copy-start | bytes 24580
  27.4 3.8 %copy-start.12 = (f32[32,64]{1,0:T(8,128)S(1)}, f32[32,64]{1,0:T(8,128)}, u32[]{:S(2)}) copy-start(f32[32,64]{1,0:T(8,128)} %get-tuple-element.192) | copy-start | bytes 24580
  31.8 2.3 %copy-start.3 = (f32[2,2,2,32,32]{4,3,2,1,0:T(8,128)S(1)}, f32[2,2,2,32,32]{4,3,2,1,0:T(8,128)}, u32[]{:S(2)}) copy-start(f32[2,2,2,32,32]{4,3,2,1,0:T(8,128)} %param.8) | copy-start | bytes 98308
  32.4 18.9 %copy-start.22 = (f32[32,32]{1,0:T(8,128)S(1)}, f32[32,32]{1,0:T(8,128)}, u32[]{:S(2)}) copy-start(f32[32,32]{1,0:T(8,128)} %get-tuple-element.129) | copy-start | bytes 12292
  32.4 19.0 %copy-start.21 = (f32[32,32]{1,0:T(8,128)S(1)}, f32[32,32]{1,0:T(8,128)}, u32[]{:S(2)}) copy-start(f32[32,32]{1,0:T(8,128)} %get-tuple-element.128) | copy-start | bytes 12292
  32.5 18.9 %copy-start.20 = (f32[32,32]{1,0:T(8,128)S(1)}, f32[32,32]{1,0:T(8,128)}, u32[]{:S(2)}) copy-start(f32[32,32]{1,0:T(8,128)} %get-tuple-element.127) | copy-start | bytes 12292
  32.5 19.0 %copy-start.19 = (f32[32,32]{1,0:T(8,128)S(1)}, f32[32,32]{1,0:T(8,128)}, u32[]{:S(2)}) copy-start(f32[32,32]{1,0:T(8,128)} %get-tuple-element.126) | copy-start | bytes 12292
  32.5 12.2 %copy-start.1 = (f32[256,1024]{1,0:T(8,128)}, f32[256,1024]{1,0:T(8,128)S(1)}, u32[]{:S(2)}) copy-start(f32[256,1024]{1,0:T(8,128)S(1)} %constant_dynamic-update-slice_fusion.56) | copy-start | bytes 3145732
  34.2 17.7 %copy-start.18 = (f32[32,32]{1,0:T(8,128)S(1)}, f32[32,32]{1,0:T(8,128)}, u32[]{:S(2)}) copy-start(f32[32,32]{1,0:T(8,128)} %get-tuple-element.125) | copy-start | bytes 12292
  35.7 8.5 %collective-permute-start.2 = (f32[8,32,32]{2,1,0:T(8,128)S(1)}, f32[8,32,32]{2,1,0:T(8,128)S(1)}, u32[]{:S(2)}, u32[]{:S(2)}) collective-permute-start(f32[8,32,32]{2,1,0:T(8,128)S(1)} %get-tuple-element.295), channel_id=1, source_target_pairs={{0,1},{1,2},{2,3},{3,4},{4,5},{5,6},{6,7},{7,8},{8,9},{9,10},{10,1... | collective-permute-start | bytes 98312 | tf_op jit(solution)/shard_map/ppermute | solution.py:17
  40.0 12.0 %copy-start.17 = (f32[32,32]{1,0:T(8,128)S(1)}, f32[32,32]{1,0:T(8,128)}, u32[]{:S(2)}) copy-start(f32[32,32]{1,0:T(8,128)} %get-tuple-element.124) | copy-start | bytes 12292
  40.1 10.2 %collective-permute-start.3 = (f32[8,32,32]{2,1,0:T(8,128)S(1)}, f32[8,32,32]{2,1,0:T(8,128)S(1)}, u32[]{:S(2)}, u32[]{:S(2)}) collective-permute-start(f32[8,32,32]{2,1,0:T(8,128)S(1)} %get-tuple-element.294), channel_id=1, source_target_pairs={{1,0},{2,1},{3,2},{4,3},{5,4},{6,5},{7,6},{8,7},{9,8},{10,9},{11,1... | collective-permute-start | bytes 98312 | tf_op jit(solution)/shard_map/ppermute | solution.py:17
  42.8 9.4 %copy-start.16 = (f32[32,32]{1,0:T(8,128)S(1)}, f32[32,32]{1,0:T(8,128)}, u32[]{:S(2)}) copy-start(f32[32,32]{1,0:T(8,128)} %get-tuple-element.123) | copy-start | bytes 12292
  44.2 8.0 %copy-start.15 = (f32[32,32]{1,0:T(8,128)S(1)}, f32[32,32]{1,0:T(8,128)}, u32[]{:S(2)}) copy-start(f32[32,32]{1,0:T(8,128)} %get-tuple-element.122) | copy-start | bytes 12292
  52.5 8.8 %copy-start.23 = (f32[32,32]{1,0:T(8,128)S(1)}, f32[32,32]{1,0:T(8,128)}, u32[]{:S(2)}) copy-start(f32[32,32]{1,0:T(8,128)} %get-tuple-element.290) | copy-start | bytes 12292
  52.5 8.9 %copy-start.14 = (f32[32,32]{1,0:T(8,128)S(1)}, f32[32,32]{1,0:T(8,128)}, u32[]{:S(2)}) copy-start(f32[32,32]{1,0:T(8,128)} %get-tuple-element.103) | copy-start | bytes 12292
  52.5 8.9 %copy-start.13 = (f32[32,32]{1,0:T(8,128)S(1)}, f32[32,32]{1,0:T(8,128)}, u32[]{:S(2)}) copy-start(f32[32,32]{1,0:T(8,128)} %get-tuple-element.102) | copy-start | bytes 12292
  53.3 7.9 %copy-start.25 = (f32[32,32]{1,0:T(8,128)S(1)}, f32[32,32]{1,0:T(8,128)}, u32[]{:S(2)}) copy-start(f32[32,32]{1,0:T(8,128)} %get-tuple-element.293) | copy-start | bytes 12292
  53.3 7.9 %copy-start.24 = (f32[32,32]{1,0:T(8,128)S(1)}, f32[32,32]{1,0:T(8,128)}, u32[]{:S(2)}) copy-start(f32[32,32]{1,0:T(8,128)} %get-tuple-element.291) | copy-start | bytes 12292
  66.2 10.3 %collective-permute-start.5 = (f32[4,32,192]{1,2,0:T(8,128)S(1)}, f32[4,32,192]{1,2,0:T(8,128)S(1)}, u32[]{:S(2)}, u32[]{:S(2)}) collective-permute-start(f32[4,32,192]{1,2,0:T(8,128)S(1)} %pad_maximum_fusion.1), channel_id=1, source_target_pairs={{32,0},{64,32},{96,64},{128,96},{160,128},{192,160},{224,192},{256... | collective-permute-start | bytes 294920 | tf_op jit(solution)/shard_map/ppermute | solution.py:17
  69.1 8.4 %collective-permute-start.4 = (f32[4,32,192]{1,2,0:T(8,128)S(1)}, f32[4,32,192]{1,2,0:T(8,128)S(1)}, u32[]{:S(2)}, u32[]{:S(2)}) collective-permute-start(f32[4,32,192]{1,2,0:T(8,128)S(1)} %pad_maximum_fusion), channel_id=1, source_target_pairs={{0,32},{32,64},{64,96},{96,128},{128,160},{160,192},{192,224},{224... | collective-permute-start | bytes 294920 | tf_op jit(solution)/shard_map/ppermute | solution.py:17
  79.7 12.3 %collective-permute-start.7 = (f32[8,32,192]{2,1,0:T(8,128)S(1)}, f32[8,32,192]{2,1,0:T(8,128)S(1)}, u32[]{:S(2)}, u32[]{:S(2)}) collective-permute-start(f32[8,32,192]{2,1,0:T(8,128)S(1)} %get-tuple-element.372), channel_id=1, source_target_pairs={{1,0},{2,1},{3,2},{4,3},{5,4},{6,5},{7,6},{8,7},{9,8},{10,9},{11,1... | collective-permute-start | bytes 589832 | tf_op jit(solution)/shard_map/ppermute | solution.py:17
  84.4 11.3 %collective-permute-start.6 = (f32[8,32,192]{2,1,0:T(8,128)S(1)}, f32[8,32,192]{2,1,0:T(8,128)S(1)}, u32[]{:S(2)}, u32[]{:S(2)}) collective-permute-start(f32[8,32,192]{2,1,0:T(8,128)S(1)} %get-tuple-element.373), channel_id=1, source_target_pairs={{0,1},{1,2},{2,3},{3,4},{4,5},{5,6},{6,7},{7,8},{8,9},{9,10},{10,1... | collective-permute-start | bytes 589832 | tf_op jit(solution)/shard_map/ppermute | solution.py:17
  108.9 3.3 %copy-start.2 = (f32[256,1024]{1,0:T(8,128)S(1)}, f32[256,1024]{1,0:T(8,128)}, u32[]{:S(2)}) copy-start(f32[256,1024]{1,0:T(8,128)} %copy-done.1) | copy-start | bytes 3145732
  114.0 23.0 %copy-start.26 = (s32[1,1,9]{2,1,0:T(1,128)S(1)}, s32[1,1,9]{2,1,0:T(1,128)}, u32[]{:S(2)}) copy-start(s32[1,1,9]{2,1,0:T(1,128)} %param.10) | copy-start | bytes 112
  114.4 8.8 %collective-permute-start.8 = (f32[3,32,288]{2,1,0:T(8,128)S(1)}, f32[3,32,288]{2,1,0:T(8,128)S(1)}, u32[]{:S(2)}, u32[]{:S(2)}) collective-permute-start(f32[3,32,288]{2,1,0:T(8,128)S(1)} %pad_maximum_fusion.20), channel_id=1, source_target_pairs={{0,32},{32,64},{64,96},{96,128},{128,160},{160,192},{192,224},{224... | collective-permute-start | bytes 331784 | tf_op jit(solution)/shard_map/ppermute | solution.py:17
  121.1 6.5 %collective-permute-start.9 = (f32[3,32,288]{2,1,0:T(8,128)S(1)}, f32[3,32,288]{2,1,0:T(8,128)S(1)}, u32[]{:S(2)}, u32[]{:S(2)}) collective-permute-start(f32[3,32,288]{2,1,0:T(8,128)S(1)} %pad_maximum_fusion.21), channel_id=1, source_target_pairs={{32,0},{64,32},{96,64},{128,96},{160,128},{192,160},{224,192},{256... | collective-permute-start | bytes 331784 | tf_op jit(solution)/shard_map/ppermute | solution.py:17
  127.7 10.2 %collective-permute-start.10 = (f32[32,288]{1,0:T(8,128)S(1)}, f32[32,288]{1,0:T(8,128)S(1)}, u32[]{:S(2)}, u32[]{:S(2)}) collective-permute-start(f32[32,288]{1,0:T(8,128)S(1)} %get-tuple-element.100), channel_id=1, source_target_pairs={{0,1},{1,2},{2,3},{3,4},{4,5},{5,6},{6,7},{7,8},{8,9},{9,10},{10,1... | collective-permute-start | bytes 110600 | tf_op jit(solution)/shard_map/ppermute | solution.py:17
  135.1 8.2 %collective-permute-start.11 = (f32[32,288]{1,0:T(8,128)S(1)}, f32[32,288]{1,0:T(8,128)S(1)}, u32[]{:S(2)}, u32[]{:S(2)}) collective-permute-start(f32[32,288]{1,0:T(8,128)S(1)} %get-tuple-element.101), channel_id=1, source_target_pairs={{1,0},{2,1},{3,2},{4,3},{5,4},{6,5},{7,6},{8,7},{9,8},{10,9},{11,1... | collective-permute-start | bytes 110600 | tf_op jit(solution)/shard_map/ppermute | solution.py:17
  143.3 21.9 %copy-start.4 = (f32[32,288]{1,0:T(8,128)}, f32[32,288]{1,0:T(8,128)S(1)}, u32[]{:S(2)}) copy-start(f32[32,288]{1,0:T(8,128)S(1)} %fusion.8) | copy-start | bytes 110596
  143.3 11.7 %collective-permute-start.12 = (f32[33,288]{1,0:T(8,128)S(1)}, f32[33,288]{1,0:T(8,128)S(1)}, u32[]{:S(2)}, u32[]{:S(2)}) collective-permute-start(f32[33,288]{1,0:T(8,128)S(1)} %concatenate.442), channel_id=1, source_target_pairs={{0,96},{32,0},{64,32},{96,64},{128,224},{160,128},{192,160},{224,1... | collective-permute-start | bytes 114056 | tf_op jit(solution)/shard_map/ppermute | solution.py:154
  145.2 11.6 %collective-permute-start.13 = (f32[33,288]{1,0:T(8,128)S(1)}, f32[33,288]{1,0:T(8,128)S(1)}, u32[]{:S(2)}, u32[]{:S(2)}) collective-permute-start(f32[33,288]{1,0:T(8,128)S(1)} %concatenate.442), channel_id=1, source_target_pairs={{0,64},{32,96},{64,0},{96,32},{128,192},{160,224},{192,128},{224,1... | collective-permute-start | bytes 114056 | tf_op jit(solution)/shard_map/ppermute | solution.py:154
  151.1 7.6 %collective-permute-start.14 = (f32[33,288]{1,0:T(8,128)S(1)}, f32[33,288]{1,0:T(8,128)S(1)}, u32[]{:S(2)}, u32[]{:S(2)}) collective-permute-start(f32[33,288]{1,0:T(8,128)S(1)} %concatenate.442), channel_id=1, source_target_pairs={{0,32},{32,64},{64,96},{96,0},{128,160},{160,192},{192,224},{224,1... | collective-permute-start | bytes 114056 | tf_op jit(solution)/shard_map/ppermute | solution.py:154

commit v2 on v1

--- a/solution.py
+++ b/solution.py
@@ -48,9 +48,15 @@
     zeros = jnp.zeros((width, width), jnp.float32)
     keep_mask = jnp.repeat(pattern.astype(jnp.float32), width, axis=-1)[:, :, :, None, :]
     stencil_rows = stencil * keep_mask
-    scaled_rows = jnp.einsum("xyzrs,xyzsk->xyzrk", diag_inverse, stencil_rows, precision=HI)
     stencil_pos = to_positions(stencil_rows)
-    scaled_pos = to_positions(scaled_rows)
+
+    here_x = lax.axis_index("gx")
+    here_y = lax.axis_index("gy")
+    block_of = np.arange(9 * width) // width
+    repeat = jnp.asarray(np.tile(np.eye(width, dtype=np.float32), (1, 9)))
+
+    def column_block(shift_x, shift_y):
+        return 3 * ((here_x + shift_x + 3) % 3) + (here_y + shift_y + 3) % 3
 
     tent = {}
     for cell in CELLS:
@@ -70,59 +76,43 @@
             tent[(pos_x, 0, pos_z)] = low[2 * pos_x + pos_z]
             tent[(pos_x, 3, pos_z)] = high[2 * pos_x + pos_z]
 
-    tent_rows = []
-    for pos in POSITIONS:
-        target = 3 * REACH[pos[0]] + REACH[pos[1]]
-        tent_rows.append(
-            jnp.concatenate([tent[pos] if number == target else zeros for number in range(9)], axis=1)
-        )
-    tent_agg = jnp.concatenate(tent_rows, axis=0)
-    smoothed = jnp.dot(scaled_pos, tent_agg, precision=HI)
-    own_tent = jnp.concatenate(
-        [
-            jnp.concatenate([tentative[cell] if number == 4 else zeros for number in range(9)], axis=1)
-            for cell in CELLS
-        ],
-        axis=0,
-    )
-    prolong_own = own_tent - OMEGA * smoothed
+    tent_frame = jnp.concatenate([tent[pos] for pos in POSITIONS], axis=0)
+    reach_x = np.array([REACH[pos[0]] - 1 for pos in POSITIONS])
+    reach_y = np.array([REACH[pos[1]] - 1 for pos in POSITIONS])
+    target = column_block(reach_x, reach_y)
+    agg_mask = (block_of[None, :] == target[:, None]).astype(jnp.float32)
+    agg_mask = jnp.broadcast_to(agg_mask[:, None, :], (32, width, 9 * width)).reshape(32 * width, 9 * width)
+    tent_agg = jnp.dot(tent_frame, repeat, precision=HI) * agg_mask
+    coupled = jnp.dot(stencil_pos, tent_agg, precision=HI).reshape(8, width, 9 * width)
+    smoothed = jnp.einsum("crs,csn->crn", diag_inverse.reshape(8, width, width), coupled, precision=HI)
+    own_mask = (block_of == column_block(0, 0)).astype(jnp.float32)[None, :]
+    own_tent = jnp.dot(tentative.reshape(8 * width, width), repeat, precision=HI) * own_mask
+    prolong_own = own_tent - OMEGA * smoothed.reshape(8 * width, 9 * width)
 
     prolong = {}
     for number, cell in enumerate(CELLS):
         prolong[(cell[0] + 1, cell[1] + 1, cell[2])] = prolong_own[number * width : (number + 1) * width]
-    to_low = jnp.stack([prolong[(1, pos_y, pos_z)][:, : 6 * width] for pos_y in (1, 2) for pos_z in range(2)])
-    to_high = jnp.stack([prolong[(2, pos_y, pos_z)][:, 3 * width :] for pos_y in (1, 2) for pos_z in range(2)])
-    from_right = shift(to_low, "gx", False)
-    from_left = shift(to_high, "gx", True)
-    wide_zeros = jnp.zeros((width, 3 * width), jnp.float32)
-    for index, (pos_y, pos_z) in enumerate((pos_y, pos_z) for pos_y in (1, 2) for pos_z in range(2)):
-        prolong[(3, pos_y, pos_z)] = jnp.concatenate([wide_zeros, from_right[index]], axis=1)
-        prolong[(0, pos_y, pos_z)] = jnp.concatenate([from_left[index], wide_zeros], axis=1)
-
-    def keep_y(block, first):
-        return jnp.concatenate(
-            [block[:, (3 * row + first) * width : (3 * row + first + 2) * width] for row in range(3)], axis=1
-        )
-
-    def spread_y(block, first):
-        pieces = []
-        for row in range(3):
-            part = block[:, 2 * row * width : (2 * row + 2) * width]
-            pieces.extend([zeros, part] if first == 1 else [part, zeros])
-        return jnp.concatenate(pieces, axis=1)
-
-    to_low = jnp.stack([keep_y(prolong[(pos_x, 1, pos_z)], 0) for pos_x in range(4) for pos_z in range(2)])
-    to_high = jnp.stack([keep_y(prolong[(pos_x, 2, pos_z)], 1) for pos_x in range(4) for pos_z in range(2)])
-    from_high = shift(to_low, "gy", False)
-    from_low = shift(to_high, "gy", True)
-    for pos_x in range(4):
-        for pos_z in range(2):
-            prolong[(pos_x, 3, pos_z)] = spread_y(from_high[2 * pos_x + pos_z], 1)
-            prolong[(pos_x, 0, pos_z)] = spread_y(from_low[2 * pos_x + pos_z], 0)
+    edge = [(pos_y, pos_z) for pos_y in (1, 2) for pos_z in range(2)]
+    from_right = shift(jnp.stack([prolong[(1,) + spot] for spot in edge]), "gx", False)
+    from_left = shift(jnp.stack([prolong[(2,) + spot] for spot in edge]), "gx", True)
+    for index, spot in enumerate(edge):
+        prolong[(3,) + spot] = from_right[index]
+        prolong[(0,) + spot] = from_left[index]
+    row = [(pos_x, pos_z) for pos_x in range(4) for pos_z in range(2)]
+    from_high = shift(jnp.stack([prolong[(spot[0], 1, spot[1])] for spot in row]), "gy", False)
+    from_low = shift(jnp.stack([prolong[(spot[0], 2, spot[1])] for spot in row]), "gy", True)
+    for index, spot in enumerate(row):
+        prolong[(spot[0], 3, spot[1])] = from_high[index]
+        prolong[(spot[0], 0, spot[1])] = from_low[index]
     prolong_frame = jnp.concatenate([prolong[pos] for pos in POSITIONS], axis=0)
 
-    applied = jnp.dot(stencil_pos, prolong_frame, precision=HI)
-    product = lax.dot_general(prolong_own, applied, (((0,), (0,)), ((), ())), precision=HI)
+    relative = np.arange(9 * width) // width
+    moved = column_block(relative // 3 - 1, relative % 3 - 1)
+    lane = np.arange(9 * width) % width
+    reorder = ((block_of[:, None] == moved[None, :]) & (lane[:, None] == lane[None, :])).astype(jnp.float32)
+    applied = jnp.dot(jnp.dot(stencil_pos, prolong_frame, precision=HI), reorder, precision=HI)
+    prolong_rel = jnp.dot(prolong_own, reorder, precision=HI)
+    product = lax.dot_general(prolong_rel, applied, (((0,), (0,)), ((), ())), precision=HI)
     partial_rows = []
     for row_x in range(3):
         line = []

time: 168 us -> 130 us (0.77); the launches traced: 165 us -> 129 us
  local copies, waits for them, and re-layouts: 62.1 us -> 35.4 us
  other arithmetic: 9.85 us -> 1.84 us
  starting transfers between devices: 57.4 us -> 54 us
  matrix products: 5.3 us -> 7.08 us
    concatenate x50 -> x1, local copies, waits for them, and re-layouts: 22.2 us -> 0.18 us  [local(): tent_frame = jnp.concatenate([tent[pos] for pos in POSITIONS], axis=0)]
    unnamed x81 -> x88, local copies, waits for them, and re-layouts: 6.25 us -> 21.7 us
    concatenate x16 -> x8, local copies, waits for them, and re-layouts: 9.28 us -> 0.85 us  [to_positions(): lines.append(jnp.concatenate(pieces, axis=1))]
    unnamed x40 -> x0, other arithmetic: 6.83 us -> none
    slice x8 -> x4, local copies, waits for them, and re-layouts: 4.98 us -> 0.46 us  [to_positions(): pieces.append(block[:, number * width:(number + 1) * width])]
    ppermute x12, starting transfers between devices: 45.7 us -> 42.5 us  [shift(): return lax.ppermute(block, axis, pairs)]
    squeeze x6 -> x0, local copies, waits for them, and re-layouts: 3.16 us -> none  [the longest x1 1.57 us: local(): right = shift(tentative[0], 'gx', False)]
    slice x66 -> x6, local copies, waits for them, and re-layouts: 4.41 us -> 1.91 us  [the longest x1 0.97 us: local(): right = shift(tentative[0], 'gx', False)]
  transfers between devices with their start and end apart: 15 -> 15, of which waited for: 7 -> 6; matrix products, arithmetic and copies ran while one was open for 22% -> 14% of each run, Pallas kernels for 0% -> 0%
where the time goes in v2:
time: 130 us; the launch traced here: 129 us
  starting transfers between devices  54 us (42%)
  local copies, waits for them, and re-layouts  35.4 us (27%)
  waiting for transfers between devices  21.1 us (16%)
  between operations  9.93 us (8%)
  matrix products  7.08 us (5%)
  other arithmetic  1.84 us (1%)
    ppermute x12, starting transfers between devices, shift(): return lax.ppermute(block, axis, pairs)  42.5 us
    unnamed x88, local copies, waits for them, and re-layouts  21.7 us
    ppermute x12, waiting for transfers between devices, shift(): return lax.ppermute(block, axis, pairs)  21.1 us
    ppermute x3, starting transfers between devices, local(): members.append(lax.ppermute(payload, 'gx', pairs))  11.6 us
    concatenate x1, local copies, waits for them, and re-layouts, local(): prolong_frame = jnp.concatenate([prolong[pos] for pos in POSITIONS], axis=0)  3.18 us
  transfers between devices with their start and end apart: 15, of which 6 were waited for; matrix products, arithmetic and copies ran while one was open for 14% of the time, Pallas kernels for 0%

profile of v2, /device:TPU:159, one launch (start us, length us, event | category | flops | bytes accessed | tf_op | source)
XLA Modules:
  0.0 129.4 jit_solution(17772726347281405633)
XLA Ops:
  0.7 1.0 fusion.30
  1.7 4.6 %collective-permute-start = (f32[2,2,32,32]{2,3,1,0:T(8,128)S(1)}, f32[2,2,32,32]{2,3,1,0:T(8,128)S(1)}, u32[]{:S(2)}, u32[]{:S(2)}) collective-permute-start(f32[2,2,32,32]{2,3,1,0:T(8,128)S(1)} %bitcast.270), channel_id=1, source_target_pairs={{0,32},{32,64},{64,96},{96,128},{128,160},{160,192},{192,224},{224... | collective-permute-start | bytes 49160 | tf_op jit(solution)/shard_map/ppermute | solution.py:17
  6.4 1.9 %collective-permute-start.1 = (f32[2,2,32,32]{2,3,1,0:T(8,128)S(1)}, f32[2,2,32,32]{2,3,1,0:T(8,128)S(1)}, u32[]{:S(2)}, u32[]{:S(2)}) collective-permute-start(f32[2,2,32,32]{2,3,1,0:T(8,128)S(1)} %bitcast.269), channel_id=1, source_target_pairs={{32,0},{64,32},{96,64},{128,96},{160,128},{192,160},{224,192},{256... | collective-permute-start | bytes 49160 | tf_op jit(solution)/shard_map/ppermute | solution.py:17
  8.3 0.9 fusion.29
  9.2 0.7 convert_element_type.24
  13.2 1.5 %copy.83 = f32[1024,288]{0,1:T(8,128)} copy(f32[1024,288]{1,0:T(8,128)S(1)} %bitcast.228) | data formatting | bytes 2359296 | tf_op jit(solution)/shard_map/reshape | solution.py:84
  14.8 2.6 %collective-permute-start.3 = (f32[8,32,32]{1,2,0:T(8,128)S(1)}, f32[8,32,32]{1,2,0:T(8,128)S(1)}, u32[]{:S(2)}, u32[]{:S(2)}) collective-permute-start(f32[8,32,32]{1,2,0:T(8,128)S(1)} %get-tuple-element.172), channel_id=1, source_target_pairs={{1,0},{2,1},{3,2},{4,3},{5,4},{6,5},{7,6},{8,7},{9,8},{10,9},{11,1... | collective-permute-start | bytes 98312 | tf_op jit(solution)/shard_map/ppermute | solution.py:17
  17.4 6.1 %collective-permute-start.2 = (f32[8,32,32]{1,2,0:T(8,128)S(1)}, f32[8,32,32]{1,2,0:T(8,128)S(1)}, u32[]{:S(2)}, u32[]{:S(2)}) collective-permute-start(f32[8,32,32]{1,2,0:T(8,128)S(1)} %get-tuple-element.173), channel_id=1, source_target_pairs={{0,1},{1,2},{2,3},{3,4},{4,5},{5,6},{6,7},{7,8},{8,9},{9,10},{10,1... | collective-permute-start | bytes 98312 | tf_op jit(solution)/shard_map/ppermute | solution.py:17
  23.6 1.9 %collective-permute-done.3 = f32[8,32,32]{1,2,0:T(8,128)S(1)} collective-permute-done((f32[8,32,32]{1,2,0:T(8,128)S(1)}, f32[8,32,32]{1,2,0:T(8,128)S(1)}, u32[]{:S(2)}, u32[]{:S(2)}) %collective-permute-start.3) | collective-permute-done | bytes 32800 | tf_op jit(solution)/shard_map/ppermute | solution.py:17
  25.5 0.9 collective-permute-done.2
  26.6 1.1 convolution_multiply_fusion
  27.7 1.8 %fusion.39 = f32[256,288]{1,0:T(8,128)S(1)} fusion(f32[256,1024]{1,0:T(8,128)S(1)} %constant_dynamic-update-slice_fusion, f32[1024,288]{0,1:T(8,128)S(1)} %convolution_multiply_fusion), kind=kOutput, calls=%fused_computation.147 | convolution fusion | flops 905969664 | bytes 2523136 | tf_op jit(solution)/shard_map/dot_general | solution.py:86
  31.7 4.6 %collective-permute-start.4 = (f32[4,32,288]{2,1,0:T(8,128)S(1)}, f32[4,32,288]{2,1,0:T(8,128)S(1)}, u32[]{:S(2)}, u32[]{:S(2)}) collective-permute-start(f32[4,32,288]{2,1,0:T(8,128)S(1)} %pad_maximum_fusion), channel_id=1, source_target_pairs={{0,32},{32,64},{64,96},{96,128},{128,160},{160,192},{192,224},{224... | collective-permute-start | bytes 442376 | tf_op jit(solution)/shard_map/ppermute | solution.py:17
  36.7 1.9 %collective-permute-start.5 = (f32[4,32,288]{2,1,0:T(8,128)S(1)}, f32[4,32,288]{2,1,0:T(8,128)S(1)}, u32[]{:S(2)}, u32[]{:S(2)}) collective-permute-start(f32[4,32,288]{2,1,0:T(8,128)S(1)} %pad_maximum_fusion.1), channel_id=1, source_target_pairs={{32,0},{64,32},{96,64},{128,96},{160,128},{192,160},{224,192},{256... | collective-permute-start | bytes 442376 | tf_op jit(solution)/shard_map/ppermute | solution.py:17
  38.7 0.7 fusion.3
  39.4 0.7 fusion.26
  40.1 0.7 slice_dynamic-update-slice_fusion.1
  40.9 0.6 constant_dynamic-update-slice_fusion.27
  41.5 0.6 constant_dynamic-update-slice_fusion.26
  42.1 0.6 constant_dynamic-update-slice_fusion.25
  42.7 0.6 constant_dynamic-update-slice_fusion.24
  43.3 0.6 constant_dynamic-update-slice_fusion.31
  43.9 0.6 constant_dynamic-update-slice_fusion.30
  44.6 0.6 constant_dynamic-update-slice_fusion.29
  45.2 0.6 constant_dynamic-update-slice_fusion.28
  45.8 0.7 slice_dynamic-update-slice_fusion
  46.5 7.4 %collective-permute-start.6 = (f32[8,32,288]{2,1,0:T(8,128)}, f32[8,32,288]{2,1,0:T(8,128)S(1)}, u32[]{:S(2)}, u32[]{:S(2)}) collective-permute-start(f32[8,32,288]{2,1,0:T(8,128)} %get-tuple-element.61), channel_id=1, source_target_pairs={{0,1},{1,2},{2,3},{3,4},{4,5},{5,6},{6,7},{7,8},{8,9},{9,10},{10,1... | collective-permute-start | bytes 884744 | tf_op jit(solution)/shard_map/ppermute | solution.py:17
  53.9 1.9 %collective-permute-start.7 = (f32[8,32,288]{2,1,0:T(8,128)}, f32[8,32,288]{2,1,0:T(8,128)S(1)}, u32[]{:S(2)}, u32[]{:S(2)}) collective-permute-start(f32[8,32,288]{2,1,0:T(8,128)} %get-tuple-element.60), channel_id=1, source_target_pairs={{1,0},{2,1},{3,2},{4,3},{5,4},{6,5},{7,6},{8,7},{9,8},{10,9},{11,1... | collective-permute-start | bytes 884744 | tf_op jit(solution)/shard_map/ppermute | solution.py:17
  56.6 0.8 copy.141
  57.3 0.8 copy.142
  58.1 4.6 %collective-permute-done.6 = f32[8,32,288]{2,1,0:T(8,128)S(1)} collective-permute-done((f32[8,32,288]{2,1,0:T(8,128)}, f32[8,32,288]{2,1,0:T(8,128)S(1)}, u32[]{:S(2)}, u32[]{:S(2)}) %collective-permute-start.6) | collective-permute-done | bytes 294944 | tf_op jit(solution)/shard_map/ppermute | solution.py:17
  62.7 0.8 copy.137
  63.5 0.8 copy.138
  64.3 5.5 %collective-permute-done.7 = f32[8,32,288]{2,1,0:T(8,128)S(1)} collective-permute-done((f32[8,32,288]{2,1,0:T(8,128)}, f32[8,32,288]{2,1,0:T(8,128)S(1)}, u32[]{:S(2)}, u32[]{:S(2)}) %collective-permute-start.7) | collective-permute-done | bytes 294944 | tf_op jit(solution)/shard_map/ppermute | solution.py:17
  69.8 0.8 copy.143
  70.6 0.8 copy.144
  71.3 0.8 copy.145
  72.1 0.8 copy.146
  72.9 0.8 copy.147
  73.6 0.8 copy.148
  74.4 0.8 copy.149
  75.2 0.8 copy.150
  75.9 0.8 copy.151
  76.7 0.8 copy.152
  77.5 0.8 copy.153
  78.2 0.8 copy.154
  79.0 0.8 copy.159
  79.8 0.8 copy.160
  80.5 3.2 %concatenate.89 = f32[1024,288]{0,1:T(8,128)S(1)} concatenate(f32[32,288]{0,1:T(8,128)} %bitcast.241, f32[32,288]{0,1:T(8,128)} %bitcast.242, f32[32,288]{0,1:T(8,128)S(1)} %bitcast.237, f32[32,288]{0,1:T(8,128)S(1)} %bitcast.238, f32[32,288]{0,1:T(8,128)} %bitcast.239, f32[32,288]{0,1:T(8,128)} %bitcast.240, f32[32,288]{0,1:T(8,128)} %bitcast.243, f32[32,288]{0,1:T(8,128)} %bitcast.244, ...), dimensions={0} | concatenate | bytes 2359296 | tf_op jit(solution)/shard_map/concatenate | solution.py:107
  83.7 1.1 fusion.40
  84.9 0.7 fusion.2
  85.6 0.6 fusion.41
  86.7 4.3 %collective-permute-start.8 = (f32[3,32,288]{2,1,0:T(8,128)S(1)}, f32[3,32,288]{2,1,0:T(8,128)S(1)}, u32[]{:S(2)}, u32[]{:S(2)}) collective-permute-start(f32[3,32,288]{2,1,0:T(8,128)S(1)} %pad_maximum_fusion.2), channel_id=1, source_target_pairs={{0,32},{32,64},{64,96},{96,128},{128,160},{160,192},{192,224},{224... | collective-permute-start | bytes 331784 | tf_op jit(solution)/shard_map/ppermute | solution.py:17
  91.2 1.9 %collective-permute-start.9 = (f32[3,32,288]{2,1,0:T(8,128)S(1)}, f32[3,32,288]{2,1,0:T(8,128)S(1)}, u32[]{:S(2)}, u32[]{:S(2)}) collective-permute-start(f32[3,32,288]{2,1,0:T(8,128)S(1)} %pad_maximum_fusion.3), channel_id=1, source_target_pairs={{32,0},{64,32},{96,64},{128,96},{160,128},{192,160},{224,192},{256... | collective-permute-start | bytes 331784 | tf_op jit(solution)/shard_map/ppermute | solution.py:17
  93.3 4.3 %collective-permute-done.9 = f32[3,32,288]{2,1,0:T(8,128)S(1)} collective-permute-done((f32[3,32,288]{2,1,0:T(8,128)S(1)}, f32[3,32,288]{2,1,0:T(8,128)S(1)}, u32[]{:S(2)}, u32[]{:S(2)}) %collective-permute-start.9) | collective-permute-done | bytes 110624 | tf_op jit(solution)/shard_map/ppermute | solution.py:17
  97.7 1.9 %collective-permute-start.10 = (f32[32,288]{1,0:T(8,128)S(1)}, f32[32,288]{1,0:T(8,128)S(1)}, u32[]{:S(2)}, u32[]{:S(2)}) collective-permute-start(f32[32,288]{1,0:T(8,128)S(1)} %get-tuple-element.68), channel_id=1, source_target_pairs={{0,1},{1,2},{2,3},{3,4},{4,5},{5,6},{6,7},{7,8},{8,9},{9,10},{10,1... | collective-permute-start | bytes 110600 | tf_op jit(solution)/shard_map/ppermute | solution.py:17
  99.6 3.4 %collective-permute-start.11 = (f32[32,288]{1,0:T(8,128)S(1)}, f32[32,288]{1,0:T(8,128)S(1)}, u32[]{:S(2)}, u32[]{:S(2)}) collective-permute-start(f32[32,288]{1,0:T(8,128)S(1)} %get-tuple-element.69), channel_id=1, source_target_pairs={{1,0},{2,1},{3,2},{4,3},{5,4},{6,5},{7,6},{8,7},{9,8},{10,9},{11,1... | collective-permute-start | bytes 110600 | tf_op jit(solution)/shard_map/ppermute | solution.py:17
  103.8 3.9 %collective-permute-done.11 = f32[32,288]{1,0:T(8,128)S(1)} collective-permute-done((f32[32,288]{1,0:T(8,128)S(1)}, f32[32,288]{1,0:T(8,128)S(1)}, u32[]{:S(2)}, u32[]{:S(2)}) %collective-permute-start.11) | collective-permute-done | bytes 36896 | tf_op jit(solution)/shard_map/ppermute | solution.py:17
  107.8 1.9 %collective-permute-start.12 = (f32[33,288]{1,0:T(8,128)S(1)}, f32[33,288]{1,0:T(8,128)S(1)}, u32[]{:S(2)}, u32[]{:S(2)}) collective-permute-start(f32[33,288]{1,0:T(8,128)S(1)} %concatenate.98), channel_id=1, source_target_pairs={{0,96},{32,0},{64,32},{96,64},{128,224},{160,128},{192,160},{224,1... | collective-permute-start | bytes 114056 | tf_op jit(solution)/shard_map/ppermute | solution.py:144
  109.7 5.7 %collective-permute-start.13 = (f32[33,288]{1,0:T(8,128)S(1)}, f32[33,288]{1,0:T(8,128)S(1)}, u32[]{:S(2)}, u32[]{:S(2)}) collective-permute-start(f32[33,288]{1,0:T(8,128)S(1)} %concatenate.98), channel_id=1, source_target_pairs={{0,64},{32,96},{64,0},{96,32},{128,192},{160,224},{192,128},{224,1... | collective-permute-start | bytes 114056 | tf_op jit(solution)/shard_map/ppermute | solution.py:144
  115.4 3.9 %collective-permute-start.14 = (f32[33,288]{1,0:T(8,128)S(1)}, f32[33,288]{1,0:T(8,128)S(1)}, u32[]{:S(2)}, u32[]{:S(2)}) collective-permute-start(f32[33,288]{1,0:T(8,128)S(1)} %concatenate.98), channel_id=1, source_target_pairs={{0,32},{32,64},{64,96},{96,0},{128,160},{160,192},{192,224},{224,1... | collective-permute-start | bytes 114056 | tf_op jit(solution)/shard_map/ppermute | solution.py:144
  119.4 0.6 slice.1147
  121.2 0.6 slice.1149
  128.7 0.7 maximum_bitcast_fusion
  (143 shorter events, 8.3 us)
Async XLA Ops:
  0.6 29.0 %copy-start = (f32[2,2,2,32,32]{4,3,2,1,0:T(8,128)S(1)}, f32[2,2,2,32,32]{4,3,2,1,0:T(8,128)}, u32[]{:S(2)}) copy-start(f32[2,2,2,32,32]{4,3,2,1,0:T(8,128)} %param.18) | copy-start | bytes 98308
  0.6 9.4 %copy-start.3 = (f32[2,2,2,32,864]{4,3,2,1,0:T(8,128)S(1)}, f32[2,2,2,32,864]{4,3,2,1,0:T(8,128)}, u32[]{:S(2)}) copy-start(f32[2,2,2,32,864]{4,3,2,1,0:T(8,128)} %param.15) | copy-start | bytes 2654212
  1.7 13.0 %collective-permute-start = (f32[2,2,32,32]{2,3,1,0:T(8,128)S(1)}, f32[2,2,32,32]{2,3,1,0:T(8,128)S(1)}, u32[]{:S(2)}, u32[]{:S(2)}) collective-permute-start(f32[2,2,32,32]{2,3,1,0:T(8,128)S(1)} %bitcast.270), channel_id=1, source_target_pairs={{0,32},{32,64},{64,96},{96,128},{128,160},{160,192},{192,224},{224... | collective-permute-start | bytes 49160 | tf_op jit(solution)/shard_map/ppermute | solution.py:17
  6.4 8.4 %collective-permute-start.1 = (f32[2,2,32,32]{2,3,1,0:T(8,128)S(1)}, f32[2,2,32,32]{2,3,1,0:T(8,128)S(1)}, u32[]{:S(2)}, u32[]{:S(2)}) collective-permute-start(f32[2,2,32,32]{2,3,1,0:T(8,128)S(1)} %bitcast.269), channel_id=1, source_target_pairs={{32,0},{64,32},{96,64},{128,96},{160,128},{192,160},{224,192},{256... | collective-permute-start | bytes 49160 | tf_op jit(solution)/shard_map/ppermute | solution.py:17
  10.2 0.7 copy-start.11
  10.2 0.7 copy-start.12
  10.2 0.7 copy-start.8
  11.6 0.7 copy-start.9
  11.6 0.7 copy-start.10
  14.7 11.9 %copy-start.1 = (f32[1024,288]{0,1:T(8,128)S(1)}, f32[1024,288]{0,1:T(8,128)}, u32[]{:S(2)}) copy-start(f32[1024,288]{0,1:T(8,128)} %copy.83) | copy-start | bytes 3538948
  14.7 11.9 %copy-start.7 = (f32[32,288]{1,0:T(8,128)S(1)}, f32[32,288]{1,0:T(8,128)}, u32[]{:S(2)}) copy-start(f32[32,288]{1,0:T(8,128)} %constant.76.clone) | copy-start | bytes 110596
  14.8 10.6 %collective-permute-start.3 = (f32[8,32,32]{1,2,0:T(8,128)S(1)}, f32[8,32,32]{1,2,0:T(8,128)S(1)}, u32[]{:S(2)}, u32[]{:S(2)}) collective-permute-start(f32[8,32,32]{1,2,0:T(8,128)S(1)} %get-tuple-element.172), channel_id=1, source_target_pairs={{1,0},{2,1},{3,2},{4,3},{5,4},{6,5},{7,6},{8,7},{9,8},{10,9},{11,1... | collective-permute-start | bytes 98312 | tf_op jit(solution)/shard_map/ppermute | solution.py:17
  17.4 8.9 %collective-permute-start.2 = (f32[8,32,32]{1,2,0:T(8,128)S(1)}, f32[8,32,32]{1,2,0:T(8,128)S(1)}, u32[]{:S(2)}, u32[]{:S(2)}) collective-permute-start(f32[8,32,32]{1,2,0:T(8,128)S(1)} %get-tuple-element.173), channel_id=1, source_target_pairs={{0,1},{1,2},{2,3},{3,4},{4,5},{5,6},{6,7},{7,8},{8,9},{9,10},{10,1... | collective-permute-start | bytes 98312 | tf_op jit(solution)/shard_map/ppermute | solution.py:17
  29.6 0.9 copy-start.2
  31.2 7.4 %copy-start.5 = (pred[288,288]{1,0:T(32,128)(4,1)S(1)}, pred[288,288]{1,0:T(32,128)(4,1)}, u32[]{:S(2)}) copy-start(pred[288,288]{1,0:T(32,128)(4,1)} %constant.84.clone) | copy-start | bytes 248836
  31.7 8.4 %collective-permute-start.4 = (f32[4,32,288]{2,1,0:T(8,128)S(1)}, f32[4,32,288]{2,1,0:T(8,128)S(1)}, u32[]{:S(2)}, u32[]{:S(2)}) collective-permute-start(f32[4,32,288]{2,1,0:T(8,128)S(1)} %pad_maximum_fusion), channel_id=1, source_target_pairs={{0,32},{32,64},{64,96},{96,128},{128,160},{160,192},{192,224},{224... | collective-permute-start | bytes 442376 | tf_op jit(solution)/shard_map/ppermute | solution.py:17
  36.7 9.1 %collective-permute-start.5 = (f32[4,32,288]{2,1,0:T(8,128)S(1)}, f32[4,32,288]{2,1,0:T(8,128)S(1)}, u32[]{:S(2)}, u32[]{:S(2)}) collective-permute-start(f32[4,32,288]{2,1,0:T(8,128)S(1)} %pad_maximum_fusion.1), channel_id=1, source_target_pairs={{32,0},{64,32},{96,64},{128,96},{160,128},{192,160},{224,192},{256... | collective-permute-start | bytes 442376 | tf_op jit(solution)/shard_map/ppermute | solution.py:17
  46.5 16.2 %collective-permute-start.6 = (f32[8,32,288]{2,1,0:T(8,128)}, f32[8,32,288]{2,1,0:T(8,128)S(1)}, u32[]{:S(2)}, u32[]{:S(2)}) collective-permute-start(f32[8,32,288]{2,1,0:T(8,128)} %get-tuple-element.61), channel_id=1, source_target_pairs={{0,1},{1,2},{2,3},{3,4},{4,5},{5,6},{6,7},{7,8},{8,9},{9,10},{10,1... | collective-permute-start | bytes 884744 | tf_op jit(solution)/shard_map/ppermute | solution.py:17
  53.9 15.8 %collective-permute-start.7 = (f32[8,32,288]{2,1,0:T(8,128)}, f32[8,32,288]{2,1,0:T(8,128)S(1)}, u32[]{:S(2)}, u32[]{:S(2)}) collective-permute-start(f32[8,32,288]{2,1,0:T(8,128)} %get-tuple-element.60), channel_id=1, source_target_pairs={{1,0},{2,1},{3,2},{4,3},{5,4},{6,5},{7,6},{8,7},{9,8},{10,9},{11,1... | collective-permute-start | bytes 884744 | tf_op jit(solution)/shard_map/ppermute | solution.py:17
  83.7 1.1 copy-start.6
  86.4 16.5 %copy-start.13 = (s32[1,1,9]{2,1,0:T(1,128)S(1)}, s32[1,1,9]{2,1,0:T(1,128)}, u32[]{:S(2)}) copy-start(s32[1,1,9]{2,1,0:T(1,128)} %param.19) | copy-start | bytes 112
  86.7 6.6 %collective-permute-start.8 = (f32[3,32,288]{2,1,0:T(8,128)S(1)}, f32[3,32,288]{2,1,0:T(8,128)S(1)}, u32[]{:S(2)}, u32[]{:S(2)}) collective-permute-start(f32[3,32,288]{2,1,0:T(8,128)S(1)} %pad_maximum_fusion.2), channel_id=1, source_target_pairs={{0,32},{32,64},{64,96},{96,128},{128,160},{160,192},{192,224},{224... | collective-permute-start | bytes 331784 | tf_op jit(solution)/shard_map/ppermute | solution.py:17
  91.2 6.5 %collective-permute-start.9 = (f32[3,32,288]{2,1,0:T(8,128)S(1)}, f32[3,32,288]{2,1,0:T(8,128)S(1)}, u32[]{:S(2)}, u32[]{:S(2)}) collective-permute-start(f32[3,32,288]{2,1,0:T(8,128)S(1)} %pad_maximum_fusion.3), channel_id=1, source_target_pairs={{32,0},{64,32},{96,64},{128,96},{160,128},{192,160},{224,192},{256... | collective-permute-start | bytes 331784 | tf_op jit(solution)/shard_map/ppermute | solution.py:17
  97.7 6.1 %collective-permute-start.10 = (f32[32,288]{1,0:T(8,128)S(1)}, f32[32,288]{1,0:T(8,128)S(1)}, u32[]{:S(2)}, u32[]{:S(2)}) collective-permute-start(f32[32,288]{1,0:T(8,128)S(1)} %get-tuple-element.68), channel_id=1, source_target_pairs={{0,1},{1,2},{2,3},{3,4},{4,5},{5,6},{6,7},{7,8},{8,9},{9,10},{10,1... | collective-permute-start | bytes 110600 | tf_op jit(solution)/shard_map/ppermute | solution.py:17
  99.6 8.2 %collective-permute-start.11 = (f32[32,288]{1,0:T(8,128)S(1)}, f32[32,288]{1,0:T(8,128)S(1)}, u32[]{:S(2)}, u32[]{:S(2)}) collective-permute-start(f32[32,288]{1,0:T(8,128)S(1)} %get-tuple-element.69), channel_id=1, source_target_pairs={{1,0},{2,1},{3,2},{4,3},{5,4},{6,5},{7,6},{8,7},{9,8},{10,9},{11,1... | collective-permute-start | bytes 110600 | tf_op jit(solution)/shard_map/ppermute | solution.py:17
  107.8 21.7 %copy-start.4 = (f32[32,288]{1,0:T(8,128)}, f32[32,288]{1,0:T(8,128)S(1)}, u32[]{:S(2)}) copy-start(f32[32,288]{1,0:T(8,128)S(1)} %fusion.11) | copy-start | bytes 110596
  107.8 11.6 %collective-permute-start.12 = (f32[33,288]{1,0:T(8,128)S(1)}, f32[33,288]{1,0:T(8,128)S(1)}, u32[]{:S(2)}, u32[]{:S(2)}) collective-permute-start(f32[33,288]{1,0:T(8,128)S(1)} %concatenate.98), channel_id=1, source_target_pairs={{0,96},{32,0},{64,32},{96,64},{128,224},{160,128},{192,160},{224,1... | collective-permute-start | bytes 114056 | tf_op jit(solution)/shard_map/ppermute | solution.py:144
  109.7 11.5 %collective-permute-start.13 = (f32[33,288]{1,0:T(8,128)S(1)}, f32[33,288]{1,0:T(8,128)S(1)}, u32[]{:S(2)}, u32[]{:S(2)}) collective-permute-start(f32[33,288]{1,0:T(8,128)S(1)} %concatenate.98), channel_id=1, source_target_pairs={{0,64},{32,96},{64,0},{96,32},{128,192},{160,224},{192,128},{224,1... | collective-permute-start | bytes 114056 | tf_op jit(solution)/shard_map/ppermute | solution.py:144
  115.4 7.6 %collective-permute-start.14 = (f32[33,288]{1,0:T(8,128)S(1)}, f32[33,288]{1,0:T(8,128)S(1)}, u32[]{:S(2)}, u32[]{:S(2)}) collective-permute-start(f32[33,288]{1,0:T(8,128)S(1)} %concatenate.98), channel_id=1, source_target_pairs={{0,32},{32,64},{64,96},{96,0},{128,160},{160,192},{192,224},{224,1... | collective-permute-start | bytes 114056 | tf_op jit(solution)/shard_map/ppermute | solution.py:144

commit v3 on v2

--- a/solution.py
+++ b/solution.py
@@ -21,7 +21,16 @@
     return 9 * (shift_x + 1) + 3 * (shift_y + 1) + (shift_z + 1)
 
 
-POSITIONS = [(pos_x, pos_y, pos_z) for pos_x in range(4) for pos_y in range(4) for pos_z in range(2)]
+EDGE = [(pos_y, pos_z) for pos_y in (1, 2) for pos_z in range(2)]
+ROW = [(pos_x, pos_z) for pos_x in range(4) for pos_z in range(2)]
+GROUPS = [
+    [(cell_x + 1, cell_y + 1, cell_z) for cell_x in range(2) for cell_y in range(2) for cell_z in range(2)],
+    [(0,) + spot for spot in EDGE],
+    [(3,) + spot for spot in EDGE],
+    [(spot[0], 0, spot[1]) for spot in ROW],
+    [(spot[0], 3, spot[1]) for spot in ROW],
+]
+POSITIONS = [pos for group in GROUPS for pos in group]
 CELLS = [(cell_x, cell_y, cell_z) for cell_x in range(2) for cell_y in range(2) for cell_z in range(2)]
 REACH = [0, 1, 1, 2]
 
@@ -92,25 +101,27 @@
     prolong = {}
     for number, cell in enumerate(CELLS):
         prolong[(cell[0] + 1, cell[1] + 1, cell[2])] = prolong_own[number * width : (number + 1) * width]
-    edge = [(pos_y, pos_z) for pos_y in (1, 2) for pos_z in range(2)]
-    from_right = shift(jnp.stack([prolong[(1,) + spot] for spot in edge]), "gx", False)
-    from_left = shift(jnp.stack([prolong[(2,) + spot] for spot in edge]), "gx", True)
-    for index, spot in enumerate(edge):
+    from_right = shift(jnp.stack([prolong[(1,) + spot] for spot in EDGE]), "gx", False)
+    from_left = shift(jnp.stack([prolong[(2,) + spot] for spot in EDGE]), "gx", True)
+    for index, spot in enumerate(EDGE):
         prolong[(3,) + spot] = from_right[index]
         prolong[(0,) + spot] = from_left[index]
-    row = [(pos_x, pos_z) for pos_x in range(4) for pos_z in range(2)]
-    from_high = shift(jnp.stack([prolong[(spot[0], 1, spot[1])] for spot in row]), "gy", False)
-    from_low = shift(jnp.stack([prolong[(spot[0], 2, spot[1])] for spot in row]), "gy", True)
-    for index, spot in enumerate(row):
-        prolong[(spot[0], 3, spot[1])] = from_high[index]
-        prolong[(spot[0], 0, spot[1])] = from_low[index]
-    prolong_frame = jnp.concatenate([prolong[pos] for pos in POSITIONS], axis=0)
+    from_high = shift(jnp.stack([prolong[(spot[0], 1, spot[1])] for spot in ROW]), "gy", False)
+    from_low = shift(jnp.stack([prolong[(spot[0], 2, spot[1])] for spot in ROW]), "gy", True)
+    parts = [prolong_own, from_left, from_right, from_low, from_high]
+    applied = None
+    first = 0
+    for group, part in zip(GROUPS, parts):
+        last = first + len(group) * width
+        term = jnp.dot(stencil_pos[:, first:last], part.reshape(len(group) * width, -1), precision=HI)
+        applied = term if applied is None else applied + term
+        first = last
 
     relative = np.arange(9 * width) // width
     moved = column_block(relative // 3 - 1, relative % 3 - 1)
     lane = np.arange(9 * width) % width
     reorder = ((block_of[:, None] == moved[None, :]) & (lane[:, None] == lane[None, :])).astype(jnp.float32)
-    applied = jnp.dot(jnp.dot(stencil_pos, prolong_frame, precision=HI), reorder, precision=HI)
+    applied = jnp.dot(applied, reorder, precision=HI)
     prolong_rel = jnp.dot(prolong_own, reorder, precision=HI)
     product = lax.dot_general(prolong_rel, applied, (((0,), (0,)), ((), ())), precision=HI)
     partial_rows = []

time: 130 us -> 110 us (0.85)
  the two profiles are of different devices: /device:TPU:159 before, /device:TPU:160 now
where the time goes in v3:
time: 110 us; the launch traced here: 109 us
  starting transfers between devices  50.5 us (46%)
  waiting for transfers between devices  26.6 us (24%)
  local copies, waits for them, and re-layouts  10.7 us (10%)
  between operations  10.2 us (9%)
  matrix products  9.05 us (8%)
  other arithmetic  1.84 us (2%)
    ppermute x12, starting transfers between devices, shift(): return lax.ppermute(block, axis, pairs)  40.9 us
    ppermute x12, waiting for transfers between devices, shift(): return lax.ppermute(block, axis, pairs)  26.6 us
    ppermute x3, starting transfers between devices, local(): members.append(lax.ppermute(payload, 'gx', pairs))  9.56 us
    dot_general x5, matrix products, local(): jnp.dot(stencil_pos[:, first:last], part.reshape(len(group) * width, -1),...  3.1 us
  transfers between devices with their start and end apart: 15, of which 8 were waited for; matrix products, arithmetic and copies ran while one was open for 9% of the time, Pallas kernels for 0%

profile of v3, /device:TPU:160, one launch (start us, length us, event | category | flops | bytes accessed | tf_op | source)
XLA Modules:
  0.0 108.9 jit_solution(5569008819246665696)
XLA Ops:
  0.7 1.0 fusion.34
  1.7 1.9 %collective-permute-start = (f32[2,2,32,32]{2,3,1,0:T(8,128)S(1)}, f32[2,2,32,32]{2,3,1,0:T(8,128)S(1)}, u32[]{:S(2)}, u32[]{:S(2)}) collective-permute-start(f32[2,2,32,32]{2,3,1,0:T(8,128)S(1)} %bitcast.233), channel_id=1, source_target_pairs={{0,32},{32,64},{64,96},{96,128},{128,160},{160,192},{192,224},{224... | collective-permute-start | bytes 49160 | tf_op jit(solution)/shard_map/ppermute | solution.py:17
  3.7 3.6 %collective-permute-start.1 = (f32[2,2,32,32]{2,3,1,0:T(8,128)S(1)}, f32[2,2,32,32]{2,3,1,0:T(8,128)S(1)}, u32[]{:S(2)}, u32[]{:S(2)}) collective-permute-start(f32[2,2,32,32]{2,3,1,0:T(8,128)S(1)} %bitcast.232), channel_id=1, source_target_pairs={{32,0},{64,32},{96,64},{128,96},{160,128},{192,160},{224,192},{256... | collective-permute-start | bytes 49160 | tf_op jit(solution)/shard_map/ppermute | solution.py:17
  7.4 0.9 fusion.35
  8.3 0.7 convert_element_type.24
  9.1 0.1 mul.55
  9.4 0.1 fusion.42
  9.7 0.3 copy-done.10
  10.2 0.1 fusion.40
  10.5 0.1 fusion.38
  10.9 0.1 fusion.36
  11.1 0.1 concatenate.81
  11.2 0.2 copy-done.8
  11.4 0.1 concatenate.82
  11.5 0.1 broadcast_in_dim.146
  11.6 1.5 %copy.63 = f32[1024,288]{0,1:T(8,128)} copy(f32[1024,288]{1,0:T(8,128)S(1)} %bitcast.211) | data formatting | bytes 2359296 | tf_op jit(solution)/shard_map/reshape | solution.py:93
  13.9 3.4 %collective-permute-start.2 = (f32[8,32,32]{1,2,0:T(8,128)S(1)}, f32[8,32,32]{1,2,0:T(8,128)S(1)}, u32[]{:S(2)}, u32[]{:S(2)}) collective-permute-start(f32[8,32,32]{1,2,0:T(8,128)S(1)} %constant_dynamic-update-slice_fusion.8), channel_id=1, source_target_pairs={{0,1},{1,2},{2,3},{3,4},{4,5},{5,6},{6,7},{7,8},{8,9},{9,10},{10,1... | collective-permute-start | bytes 98312 | tf_op jit(solution)/shard_map/ppermute | solution.py:17
  17.3 5.8 %collective-permute-start.3 = (f32[8,32,32]{1,2,0:T(8,128)S(1)}, f32[8,32,32]{1,2,0:T(8,128)S(1)}, u32[]{:S(2)}, u32[]{:S(2)}) collective-permute-start(f32[8,32,32]{1,2,0:T(8,128)S(1)} %get-tuple-element.142), channel_id=1, source_target_pairs={{1,0},{2,1},{3,2},{4,3},{5,4},{6,5},{7,6},{8,7},{9,8},{10,9},{11,1... | collective-permute-start | bytes 98312 | tf_op jit(solution)/shard_map/ppermute | solution.py:17
  23.1 2.2 %collective-permute-done.2 = f32[8,32,32]{1,2,0:T(8,128)S(1)} collective-permute-done((f32[8,32,32]{1,2,0:T(8,128)S(1)}, f32[8,32,32]{1,2,0:T(8,128)S(1)}, u32[]{:S(2)}, u32[]{:S(2)}) %collective-permute-start.2) | collective-permute-done | bytes 32800 | tf_op jit(solution)/shard_map/ppermute | solution.py:17
  25.3 1.2 %collective-permute-done.3 = f32[8,32,32]{1,2,0:T(8,128)S(1)} collective-permute-done((f32[8,32,32]{1,2,0:T(8,128)S(1)}, f32[8,32,32]{1,2,0:T(8,128)S(1)}, u32[]{:S(2)}, u32[]{:S(2)}) %collective-permute-start.3) | collective-permute-done | bytes 32800 | tf_op jit(solution)/shard_map/ppermute | solution.py:17
  26.5 0.2 concatenate.84
  26.7 1.1 %convolution_multiply_fusion = f32[1024,288]{0,1:T(8,128)S(1)} fusion(f32[1024,288]{0,1:T(8,128)S(1)} %copy-done.1, f32[1024,32]{0,1:T(8,128)S(1)} %concatenate.84, f32[32,288]{1,0:T(8,128)S(1)} %copy-done.6), kind=kOutput, calls=%fused_computation | convolution fusion | flops 113541120 | bytes 2527232 | tf_op jit(solution)/shard_map/dot_general | solution.py:94
  27.8 1.8 %fusion.44 = f32[256,288]{1,0:T(8,128)S(1)} fusion(f32[256,1024]{1,0:T(8,128)S(1)} %constant_dynamic-update-slice_fusion, f32[1024,288]{0,1:T(8,128)S(1)} %convolution_multiply_fusion), kind=kOutput, calls=%fused_computation.154 | convolution fusion | flops 905969664 | bytes 2523136 | tf_op jit(solution)/shard_map/dot_general | solution.py:95
  29.7 0.5 convolution_multiply_fusion.1
  30.2 0.1 copy.65
  30.3 0.3 copy-done.2
  30.6 0.4 fusion.2
  31.0 0.3 slice_bitcast_fusion.1
  31.4 0.1 copy.68
  31.5 0.1 copy.67
  31.6 0.1 copy.66
  31.8 1.9 %collective-permute-start.4 = (f32[4,32,288]{2,1,0:T(8,128)S(1)}, f32[4,32,288]{2,1,0:T(8,128)S(1)}, u32[]{:S(2)}, u32[]{:S(2)}) collective-permute-start(f32[4,32,288]{2,1,0:T(8,128)S(1)} %pad_maximum_fusion), channel_id=1, source_target_pairs={{0,32},{32,64},{64,96},{96,128},{128,160},{160,192},{192,224},{224... | collective-permute-start | bytes 442376 | tf_op jit(solution)/shard_map/ppermute | solution.py:17
  33.8 0.1 copy.73
  33.9 0.1 copy.71
  34.0 0.1 copy.70
  34.2 3.8 %collective-permute-start.5 = (f32[4,32,288]{2,1,0:T(8,128)S(1)}, f32[4,32,288]{2,1,0:T(8,128)S(1)}, u32[]{:S(2)}, u32[]{:S(2)}) collective-permute-start(f32[4,32,288]{2,1,0:T(8,128)S(1)} %pad_maximum_fusion.1), channel_id=1, source_target_pairs={{32,0},{64,32},{96,64},{128,96},{160,128},{192,160},{224,192},{256... | collective-permute-start | bytes 442376 | tf_op jit(solution)/shard_map/ppermute | solution.py:17
  38.0 0.4 fusion.10
  38.4 0.4 collective-permute-done.4
  38.9 2.2 %collective-permute-done.5 = f32[4,32,288]{2,1,0:T(8,128)S(1)} collective-permute-done((f32[4,32,288]{2,1,0:T(8,128)S(1)}, f32[4,32,288]{2,1,0:T(8,128)S(1)}, u32[]{:S(2)}, u32[]{:S(2)}) %collective-permute-start.5) | collective-permute-done | bytes 147488 | tf_op jit(solution)/shard_map/ppermute | solution.py:17
  41.2 7.7 %collective-permute-start.7 = (f32[8,32,288]{2,1,0:T(8,128)S(1)}, f32[8,32,288]{2,1,0:T(8,128)S(1)}, u32[]{:S(2)}, u32[]{:S(2)}) collective-permute-start(f32[8,32,288]{2,1,0:T(8,128)S(1)} %get-tuple-element.39), channel_id=1, source_target_pairs={{1,0},{2,1},{3,2},{4,3},{5,4},{6,5},{7,6},{8,7},{9,8},{10,9},{11,1... | collective-permute-start | bytes 884744 | tf_op jit(solution)/shard_map/ppermute | solution.py:17
  48.9 0.7 fusion.5
  49.6 2.1 %collective-permute-start.6 = (f32[8,32,288]{2,1,0:T(8,128)S(1)}, f32[8,32,288]{2,1,0:T(8,128)S(1)}, u32[]{:S(2)}, u32[]{:S(2)}) collective-permute-start(f32[8,32,288]{2,1,0:T(8,128)S(1)} %get-tuple-element.38), channel_id=1, source_target_pairs={{0,1},{1,2},{2,3},{3,4},{4,5},{5,6},{6,7},{7,8},{8,9},{9,10},{10,1... | collective-permute-start | bytes 884744 | tf_op jit(solution)/shard_map/ppermute | solution.py:17
  51.7 0.5 convolution_add_fusion.1
  52.3 4.6 %collective-permute-done.7 = f32[8,32,288]{2,1,0:T(8,128)S(1)} collective-permute-done((f32[8,32,288]{2,1,0:T(8,128)S(1)}, f32[8,32,288]{2,1,0:T(8,128)S(1)}, u32[]{:S(2)}, u32[]{:S(2)}) %collective-permute-start.7) | collective-permute-done | bytes 294944 | tf_op jit(solution)/shard_map/ppermute | solution.py:17
  56.9 0.8 fusion.6
  57.7 8.0 %collective-permute-done.6 = f32[8,32,288]{2,1,0:T(8,128)S(1)} collective-permute-done((f32[8,32,288]{2,1,0:T(8,128)S(1)}, f32[8,32,288]{2,1,0:T(8,128)S(1)}, u32[]{:S(2)}, u32[]{:S(2)}) %collective-permute-start.6) | collective-permute-done | bytes 294944 | tf_op jit(solution)/shard_map/ppermute | solution.py:17
  65.6 0.8 fusion.8
  66.4 0.6 fusion.3
  67.0 0.7 fusion.4
  67.7 0.6 fusion.45
  68.7 0.1 maximum_bitcast_fusion.1
  68.9 2.2 %collective-permute-start.9 = (f32[3,32,288]{2,1,0:T(8,128)S(1)}, f32[3,32,288]{2,1,0:T(8,128)S(1)}, u32[]{:S(2)}, u32[]{:S(2)}) collective-permute-start(f32[3,32,288]{2,1,0:T(8,128)S(1)} %pad_maximum_fusion.3), channel_id=1, source_target_pairs={{32,0},{64,32},{96,64},{128,96},{160,128},{192,160},{224,192},{256... | collective-permute-start | bytes 331784 | tf_op jit(solution)/shard_map/ppermute | solution.py:17
  71.2 2.7 %collective-permute-start.8 = (f32[3,32,288]{2,1,0:T(8,128)S(1)}, f32[3,32,288]{2,1,0:T(8,128)S(1)}, u32[]{:S(2)}, u32[]{:S(2)}) collective-permute-start(f32[3,32,288]{2,1,0:T(8,128)S(1)} %pad_maximum_fusion.2), channel_id=1, source_target_pairs={{0,32},{32,64},{64,96},{96,128},{128,160},{160,192},{192,224},{224... | collective-permute-start | bytes 331784 | tf_op jit(solution)/shard_map/ppermute | solution.py:17
  74.0 3.6 %collective-permute-done.8 = f32[3,32,288]{2,1,0:T(8,128)S(1)} collective-permute-done((f32[3,32,288]{2,1,0:T(8,128)S(1)}, f32[3,32,288]{2,1,0:T(8,128)S(1)}, u32[]{:S(2)}, u32[]{:S(2)}) %collective-permute-start.8) | collective-permute-done | bytes 110624 | tf_op jit(solution)/shard_map/ppermute | solution.py:17
  77.7 1.9 %collective-permute-start.11 = (f32[32,288]{1,0:T(8,128)S(1)}, f32[32,288]{1,0:T(8,128)S(1)}, u32[]{:S(2)}, u32[]{:S(2)}) collective-permute-start(f32[32,288]{1,0:T(8,128)S(1)} %get-tuple-element.43), channel_id=1, source_target_pairs={{1,0},{2,1},{3,2},{4,3},{5,4},{6,5},{7,6},{8,7},{9,8},{10,9},{11,1... | collective-permute-start | bytes 110600 | tf_op jit(solution)/shard_map/ppermute | solution.py:17
  79.6 3.9 %collective-permute-start.10 = (f32[32,288]{1,0:T(8,128)S(1)}, f32[32,288]{1,0:T(8,128)S(1)}, u32[]{:S(2)}, u32[]{:S(2)}) collective-permute-start(f32[32,288]{1,0:T(8,128)S(1)} %get-tuple-element.42), channel_id=1, source_target_pairs={{0,1},{1,2},{2,3},{3,4},{4,5},{5,6},{6,7},{7,8},{8,9},{9,10},{10,1... | collective-permute-start | bytes 110600 | tf_op jit(solution)/shard_map/ppermute | solution.py:17
  84.4 4.5 %collective-permute-done.10 = f32[32,288]{1,0:T(8,128)S(1)} collective-permute-done((f32[32,288]{1,0:T(8,128)S(1)}, f32[32,288]{1,0:T(8,128)S(1)}, u32[]{:S(2)}, u32[]{:S(2)}) %collective-permute-start.10) | collective-permute-done | bytes 36896 | tf_op jit(solution)/shard_map/ppermute | solution.py:17
  88.9 1.9 %collective-permute-start.14 = (f32[33,288]{1,0:T(8,128)S(1)}, f32[33,288]{1,0:T(8,128)S(1)}, u32[]{:S(2)}, u32[]{:S(2)}) collective-permute-start(f32[33,288]{1,0:T(8,128)S(1)} %concatenate.93), channel_id=1, source_target_pairs={{0,32},{32,64},{64,96},{96,0},{128,160},{160,192},{192,224},{224,1... | collective-permute-start | bytes 114056 | tf_op jit(solution)/shard_map/ppermute | solution.py:155
  90.9 4.9 %collective-permute-start.13 = (f32[33,288]{1,0:T(8,128)S(1)}, f32[33,288]{1,0:T(8,128)S(1)}, u32[]{:S(2)}, u32[]{:S(2)}) collective-permute-start(f32[33,288]{1,0:T(8,128)S(1)} %concatenate.93), channel_id=1, source_target_pairs={{0,64},{32,96},{64,0},{96,32},{128,192},{160,224},{192,128},{224,1... | collective-permute-start | bytes 114056 | tf_op jit(solution)/shard_map/ppermute | solution.py:155
  95.8 2.8 %collective-permute-start.12 = (f32[33,288]{1,0:T(8,128)S(1)}, f32[33,288]{1,0:T(8,128)S(1)}, u32[]{:S(2)}, u32[]{:S(2)}) collective-permute-start(f32[33,288]{1,0:T(8,128)S(1)} %concatenate.93), channel_id=1, source_target_pairs={{0,96},{32,0},{64,32},{96,64},{128,224},{160,128},{192,160},{224,1... | collective-permute-start | bytes 114056 | tf_op jit(solution)/shard_map/ppermute | solution.py:155
  98.5 0.5 slice.1054
  100.4 0.6 slice.1052
  102.4 0.5 slice.1050
  108.2 0.7 maximum_bitcast_fusion
  (117 shorter events, 3.2 us)
Async XLA Ops:
  0.6 29.1 %copy-start = (f32[2,2,2,32,32]{4,3,2,1,0:T(8,128)S(1)}, f32[2,2,2,32,32]{4,3,2,1,0:T(8,128)}, u32[]{:S(2)}) copy-start(f32[2,2,2,32,32]{4,3,2,1,0:T(8,128)} %param.18) | copy-start | bytes 98308
  0.6 8.5 %copy-start.3 = (f32[2,2,2,32,864]{4,3,2,1,0:T(8,128)S(1)}, f32[2,2,2,32,864]{4,3,2,1,0:T(8,128)}, u32[]{:S(2)}) copy-start(f32[2,2,2,32,864]{4,3,2,1,0:T(8,128)} %param.15) | copy-start | bytes 2654212
  1.7 12.0 %collective-permute-start = (f32[2,2,32,32]{2,3,1,0:T(8,128)S(1)}, f32[2,2,32,32]{2,3,1,0:T(8,128)S(1)}, u32[]{:S(2)}, u32[]{:S(2)}) collective-permute-start(f32[2,2,32,32]{2,3,1,0:T(8,128)S(1)} %bitcast.233), channel_id=1, source_target_pairs={{0,32},{32,64},{64,96},{96,128},{128,160},{160,192},{192,224},{224... | collective-permute-start | bytes 49160 | tf_op jit(solution)/shard_map/ppermute | solution.py:17
  3.7 10.2 %collective-permute-start.1 = (f32[2,2,32,32]{2,3,1,0:T(8,128)S(1)}, f32[2,2,32,32]{2,3,1,0:T(8,128)S(1)}, u32[]{:S(2)}, u32[]{:S(2)}) collective-permute-start(f32[2,2,32,32]{2,3,1,0:T(8,128)S(1)} %bitcast.232), channel_id=1, source_target_pairs={{32,0},{64,32},{96,64},{128,96},{160,128},{192,160},{224,192},{256... | collective-permute-start | bytes 49160 | tf_op jit(solution)/shard_map/ppermute | solution.py:17
  9.3 0.7 copy-start.10
  9.3 0.7 copy-start.11
  9.3 0.7 copy-start.7
  10.7 0.7 copy-start.8
  10.7 0.7 copy-start.9
  13.2 13.5 %copy-start.1 = (f32[1024,288]{0,1:T(8,128)S(1)}, f32[1024,288]{0,1:T(8,128)}, u32[]{:S(2)}) copy-start(f32[1024,288]{0,1:T(8,128)} %copy.63) | copy-start | bytes 3538948
  13.2 13.5 %copy-start.6 = (f32[32,288]{1,0:T(8,128)S(1)}, f32[32,288]{1,0:T(8,128)}, u32[]{:S(2)}) copy-start(f32[32,288]{1,0:T(8,128)} %constant.76.clone) | copy-start | bytes 110596
  13.9 11.4 %collective-permute-start.2 = (f32[8,32,32]{1,2,0:T(8,128)S(1)}, f32[8,32,32]{1,2,0:T(8,128)S(1)}, u32[]{:S(2)}, u32[]{:S(2)}) collective-permute-start(f32[8,32,32]{1,2,0:T(8,128)S(1)} %constant_dynamic-update-slice_fusion.8), channel_id=1, source_target_pairs={{0,1},{1,2},{2,3},{3,4},{4,5},{5,6},{6,7},{7,8},{8,9},{9,10},{10,1... | collective-permute-start | bytes 98312 | tf_op jit(solution)/shard_map/ppermute | solution.py:17
  17.3 9.1 %collective-permute-start.3 = (f32[8,32,32]{1,2,0:T(8,128)S(1)}, f32[8,32,32]{1,2,0:T(8,128)S(1)}, u32[]{:S(2)}, u32[]{:S(2)}) collective-permute-start(f32[8,32,32]{1,2,0:T(8,128)S(1)} %get-tuple-element.142), channel_id=1, source_target_pairs={{1,0},{2,1},{3,2},{4,3},{5,4},{6,5},{7,6},{8,7},{9,8},{10,9},{11,1... | collective-permute-start | bytes 98312 | tf_op jit(solution)/shard_map/ppermute | solution.py:17
  29.7 0.9 copy-start.2
  31.8 7.0 %collective-permute-start.4 = (f32[4,32,288]{2,1,0:T(8,128)S(1)}, f32[4,32,288]{2,1,0:T(8,128)S(1)}, u32[]{:S(2)}, u32[]{:S(2)}) collective-permute-start(f32[4,32,288]{2,1,0:T(8,128)S(1)} %pad_maximum_fusion), channel_id=1, source_target_pairs={{0,32},{32,64},{64,96},{96,128},{128,160},{160,192},{192,224},{224... | collective-permute-start | bytes 442376 | tf_op jit(solution)/shard_map/ppermute | solution.py:17
  34.2 14.7 %copy-start.5 = (pred[288,288]{1,0:T(32,128)(4,1)S(1)}, pred[288,288]{1,0:T(32,128)(4,1)}, u32[]{:S(2)}) copy-start(pred[288,288]{1,0:T(32,128)(4,1)} %constant.84.clone) | copy-start | bytes 248836
  34.2 6.9 %collective-permute-start.5 = (f32[4,32,288]{2,1,0:T(8,128)S(1)}, f32[4,32,288]{2,1,0:T(8,128)S(1)}, u32[]{:S(2)}, u32[]{:S(2)}) collective-permute-start(f32[4,32,288]{2,1,0:T(8,128)S(1)} %pad_maximum_fusion.1), channel_id=1, source_target_pairs={{32,0},{64,32},{96,64},{128,96},{160,128},{192,160},{224,192},{256... | collective-permute-start | bytes 442376 | tf_op jit(solution)/shard_map/ppermute | solution.py:17
  41.2 15.7 %collective-permute-start.7 = (f32[8,32,288]{2,1,0:T(8,128)S(1)}, f32[8,32,288]{2,1,0:T(8,128)S(1)}, u32[]{:S(2)}, u32[]{:S(2)}) collective-permute-start(f32[8,32,288]{2,1,0:T(8,128)S(1)} %get-tuple-element.39), channel_id=1, source_target_pairs={{1,0},{2,1},{3,2},{4,3},{5,4},{6,5},{7,6},{8,7},{9,8},{10,9},{11,1... | collective-permute-start | bytes 884744 | tf_op jit(solution)/shard_map/ppermute | solution.py:17
  49.6 16.0 %collective-permute-start.6 = (f32[8,32,288]{2,1,0:T(8,128)S(1)}, f32[8,32,288]{2,1,0:T(8,128)S(1)}, u32[]{:S(2)}, u32[]{:S(2)}) collective-permute-start(f32[8,32,288]{2,1,0:T(8,128)S(1)} %get-tuple-element.38), channel_id=1, source_target_pairs={{0,1},{1,2},{2,3},{3,4},{4,5},{5,6},{6,7},{7,8},{8,9},{9,10},{10,1... | collective-permute-start | bytes 884744 | tf_op jit(solution)/shard_map/ppermute | solution.py:17
  68.6 14.9 %copy-start.12 = (s32[1,1,9]{2,1,0:T(1,128)S(1)}, s32[1,1,9]{2,1,0:T(1,128)}, u32[]{:S(2)}) copy-start(s32[1,1,9]{2,1,0:T(1,128)} %param.19) | copy-start | bytes 112
  68.9 5.2 %collective-permute-start.9 = (f32[3,32,288]{2,1,0:T(8,128)S(1)}, f32[3,32,288]{2,1,0:T(8,128)S(1)}, u32[]{:S(2)}, u32[]{:S(2)}) collective-permute-start(f32[3,32,288]{2,1,0:T(8,128)S(1)} %pad_maximum_fusion.3), channel_id=1, source_target_pairs={{32,0},{64,32},{96,64},{128,96},{160,128},{192,160},{224,192},{256... | collective-permute-start | bytes 331784 | tf_op jit(solution)/shard_map/ppermute | solution.py:17
  71.2 6.5 %collective-permute-start.8 = (f32[3,32,288]{2,1,0:T(8,128)S(1)}, f32[3,32,288]{2,1,0:T(8,128)S(1)}, u32[]{:S(2)}, u32[]{:S(2)}) collective-permute-start(f32[3,32,288]{2,1,0:T(8,128)S(1)} %pad_maximum_fusion.2), channel_id=1, source_target_pairs={{0,32},{32,64},{64,96},{96,128},{128,160},{160,192},{192,224},{224... | collective-permute-start | bytes 331784 | tf_op jit(solution)/shard_map/ppermute | solution.py:17
  77.7 6.7 %collective-permute-start.11 = (f32[32,288]{1,0:T(8,128)S(1)}, f32[32,288]{1,0:T(8,128)S(1)}, u32[]{:S(2)}, u32[]{:S(2)}) collective-permute-start(f32[32,288]{1,0:T(8,128)S(1)} %get-tuple-element.43), channel_id=1, source_target_pairs={{1,0},{2,1},{3,2},{4,3},{5,4},{6,5},{7,6},{8,7},{9,8},{10,9},{11,1... | collective-permute-start | bytes 110600 | tf_op jit(solution)/shard_map/ppermute | solution.py:17
  79.6 9.3 %collective-permute-start.10 = (f32[32,288]{1,0:T(8,128)S(1)}, f32[32,288]{1,0:T(8,128)S(1)}, u32[]{:S(2)}, u32[]{:S(2)}) collective-permute-start(f32[32,288]{1,0:T(8,128)S(1)} %get-tuple-element.42), channel_id=1, source_target_pairs={{0,1},{1,2},{2,3},{3,4},{4,5},{5,6},{6,7},{7,8},{8,9},{9,10},{10,1... | collective-permute-start | bytes 110600 | tf_op jit(solution)/shard_map/ppermute | solution.py:17
  88.9 20.0 %copy-start.4 = (f32[32,288]{1,0:T(8,128)}, f32[32,288]{1,0:T(8,128)S(1)}, u32[]{:S(2)}) copy-start(f32[32,288]{1,0:T(8,128)S(1)} %fusion.21) | copy-start | bytes 110596
  88.9 9.6 %collective-permute-start.14 = (f32[33,288]{1,0:T(8,128)S(1)}, f32[33,288]{1,0:T(8,128)S(1)}, u32[]{:S(2)}, u32[]{:S(2)}) collective-permute-start(f32[33,288]{1,0:T(8,128)S(1)} %concatenate.93), channel_id=1, source_target_pairs={{0,32},{32,64},{64,96},{96,0},{128,160},{160,192},{192,224},{224,1... | collective-permute-start | bytes 114056 | tf_op jit(solution)/shard_map/ppermute | solution.py:155
  90.9 9.5 %collective-permute-start.13 = (f32[33,288]{1,0:T(8,128)S(1)}, f32[33,288]{1,0:T(8,128)S(1)}, u32[]{:S(2)}, u32[]{:S(2)}) collective-permute-start(f32[33,288]{1,0:T(8,128)S(1)} %concatenate.93), channel_id=1, source_target_pairs={{0,64},{32,96},{64,0},{96,32},{128,192},{160,224},{192,128},{224,1... | collective-permute-start | bytes 114056 | tf_op jit(solution)/shard_map/ppermute | solution.py:155
  95.8 6.6 %collective-permute-start.12 = (f32[33,288]{1,0:T(8,128)S(1)}, f32[33,288]{1,0:T(8,128)S(1)}, u32[]{:S(2)}, u32[]{:S(2)}) collective-permute-start(f32[33,288]{1,0:T(8,128)S(1)} %concatenate.93), channel_id=1, source_target_pairs={{0,96},{32,0},{64,32},{96,64},{128,224},{160,128},{192,160},{224,1... | collective-permute-start | bytes 114056 | tf_op jit(solution)/shard_map/ppermute | solution.py:155

commit v4 on v3

--- a/solution.py
+++ b/solution.py
@@ -149,10 +149,11 @@
     slot_row = jnp.broadcast_to(slot.astype(jnp.float32).reshape(1, 1), (1, 9 * width))
     payload = jnp.concatenate([coarse_block, slot_row], axis=0)
     count = lax.axis_size("gx")
-    members = [payload]
-    for step in (1, 2, 3):
-        pairs = [(i, 4 * (i // 4) + (i % 4 + step) % 4) for i in range(count)]
-        members.append(lax.ppermute(payload, "gx", pairs))
+    held = payload[None]
+    for level in (0, 1):
+        partner = lax.ppermute(held, "gx", [(i, i ^ (1 << level)) for i in range(count)])
+        held = jnp.concatenate([held, partner], axis=0)
+    members = [held[index] for index in range(4)]
     grouped = []
     for target in range(4):
         chosen = jnp.zeros_like(coarse_block)

time: 110 us -> 109 us (level)
  the two profiles are of different devices: /device:TPU:160 before, /device:TPU:288 now
where the time goes in v4:
time: 109 us; the launch traced here: 108 us
  starting transfers between devices  46.6 us (43%)
  waiting for transfers between devices  29.9 us (27%)
  local copies, waits for them, and re-layouts  10.6 us (10%)
  between operations  9.99 us (9%)
  matrix products  9.05 us (8%)
  other arithmetic  1.86 us (2%)
    ppermute x12, starting transfers between devices, shift(): return lax.ppermute(block, axis, pairs)  42.8 us
    ppermute x12, waiting for transfers between devices, shift(): return lax.ppermute(block, axis, pairs)  26.5 us
    ppermute x2, starting transfers between devices, local(): lax.ppermute(held, 'gx', [(i, i ^ 1 << level) for i in range(count)])  3.84 us
    ppermute x2, waiting for transfers between devices, local(): lax.ppermute(held, 'gx', [(i, i ^ 1 << level) for i in range(count)])  3.45 us
    dot_general x5, matrix products, local(): jnp.dot(stencil_pos[:, first:last], part.reshape(len(group) * width, -1),...  3.1 us
  transfers between devices with their start and end apart: 14, of which 10 were waited for; matrix products, arithmetic and copies ran while one was open for 9% of the time, Pallas kernels for 0%

profile of v4, /device:TPU:288, one launch (start us, length us, event | category | flops | bytes accessed | tf_op | source)
XLA Modules:
  0.0 108.1 jit_solution(7431517410810089457)
XLA Ops:
  0.7 1.0 fusion.34
  1.7 1.9 %collective-permute-start = (f32[2,2,32,32]{2,3,1,0:T(8,128)S(1)}, f32[2,2,32,32]{2,3,1,0:T(8,128)S(1)}, u32[]{:S(2)}, u32[]{:S(2)}) collective-permute-start(f32[2,2,32,32]{2,3,1,0:T(8,128)S(1)} %bitcast.271), channel_id=1, source_target_pairs={{0,32},{32,64},{64,96},{96,128},{128,160},{160,192},{192,224},{224... | collective-permute-start | bytes 49160 | tf_op jit(solution)/shard_map/ppermute | solution.py:17
  3.7 4.9 %collective-permute-start.1 = (f32[2,2,32,32]{2,3,1,0:T(8,128)S(1)}, f32[2,2,32,32]{2,3,1,0:T(8,128)S(1)}, u32[]{:S(2)}, u32[]{:S(2)}) collective-permute-start(f32[2,2,32,32]{2,3,1,0:T(8,128)S(1)} %bitcast.270), channel_id=1, source_target_pairs={{32,0},{64,32},{96,64},{128,96},{160,128},{192,160},{224,192},{256... | collective-permute-start | bytes 49160 | tf_op jit(solution)/shard_map/ppermute | solution.py:17
  8.6 0.9 fusion.35
  9.5 0.7 convert_element_type.24
  10.3 0.1 mul.55
  10.6 0.1 fusion.42
  10.9 0.3 copy-done.10
  11.4 0.1 fusion.40
  11.8 0.1 fusion.38
  12.2 0.1 fusion.36
  12.3 0.1 concatenate.84
  12.4 0.2 copy-done.8
  12.6 0.1 concatenate.85
  12.8 1.5 %copy.63 = f32[1024,288]{0,1:T(8,128)} copy(f32[1024,288]{1,0:T(8,128)S(1)} %bitcast.248) | data formatting | bytes 2359296 | tf_op jit(solution)/shard_map/reshape | solution.py:93
  15.1 3.4 %collective-permute-start.2 = (f32[8,32,32]{1,2,0:T(8,128)S(1)}, f32[8,32,32]{1,2,0:T(8,128)S(1)}, u32[]{:S(2)}, u32[]{:S(2)}) collective-permute-start(f32[8,32,32]{1,2,0:T(8,128)S(1)} %constant_dynamic-update-slice_fusion.8), channel_id=1, source_target_pairs={{0,1},{1,2},{2,3},{3,4},{4,5},{5,6},{6,7},{7,8},{8,9},{9,10},{10,1... | collective-permute-start | bytes 98312 | tf_op jit(solution)/shard_map/ppermute | solution.py:17
  18.5 5.8 %collective-permute-start.3 = (f32[8,32,32]{1,2,0:T(8,128)S(1)}, f32[8,32,32]{1,2,0:T(8,128)S(1)}, u32[]{:S(2)}, u32[]{:S(2)}) collective-permute-start(f32[8,32,32]{1,2,0:T(8,128)S(1)} %get-tuple-element.144), channel_id=1, source_target_pairs={{1,0},{2,1},{3,2},{4,3},{5,4},{6,5},{7,6},{8,7},{9,8},{10,9},{11,1... | collective-permute-start | bytes 98312 | tf_op jit(solution)/shard_map/ppermute | solution.py:17
  24.3 1.0 collective-permute-done.2
  25.3 1.5 %collective-permute-done.3 = f32[8,32,32]{1,2,0:T(8,128)S(1)} collective-permute-done((f32[8,32,32]{1,2,0:T(8,128)S(1)}, f32[8,32,32]{1,2,0:T(8,128)S(1)}, u32[]{:S(2)}, u32[]{:S(2)}) %collective-permute-start.3) | collective-permute-done | bytes 32800 | tf_op jit(solution)/shard_map/ppermute | solution.py:17
  26.8 0.2 concatenate.87
  27.0 1.1 %convolution_multiply_fusion = f32[1024,288]{0,1:T(8,128)S(1)} fusion(f32[1024,288]{0,1:T(8,128)S(1)} %copy-done.1, f32[1024,32]{0,1:T(8,128)S(1)} %concatenate.87, f32[32,288]{1,0:T(8,128)S(1)} %copy-done.6), kind=kOutput, calls=%fused_computation | convolution fusion | flops 113541120 | bytes 2527232 | tf_op jit(solution)/shard_map/dot_general | solution.py:94
  28.2 1.8 %fusion.44 = f32[256,288]{1,0:T(8,128)S(1)} fusion(f32[256,1024]{1,0:T(8,128)S(1)} %constant_dynamic-update-slice_fusion, f32[1024,288]{0,1:T(8,128)S(1)} %convolution_multiply_fusion), kind=kOutput, calls=%fused_computation.161 | convolution fusion | flops 905969664 | bytes 2523136 | tf_op jit(solution)/shard_map/dot_general | solution.py:95
  30.0 0.5 convolution_multiply_fusion.1
  30.5 0.1 copy.65
  30.7 0.3 copy-done.2
  30.9 0.4 fusion.2
  31.4 0.3 slice_bitcast_fusion.1
  31.8 0.1 copy.68
  31.9 0.1 copy.67
  32.0 0.1 copy.66
  32.1 1.9 %collective-permute-start.4 = (f32[4,32,288]{2,1,0:T(8,128)S(1)}, f32[4,32,288]{2,1,0:T(8,128)S(1)}, u32[]{:S(2)}, u32[]{:S(2)}) collective-permute-start(f32[4,32,288]{2,1,0:T(8,128)S(1)} %pad_maximum_fusion), channel_id=1, source_target_pairs={{0,32},{32,64},{64,96},{96,128},{128,160},{160,192},{192,224},{224... | collective-permute-start | bytes 442376 | tf_op jit(solution)/shard_map/ppermute | solution.py:17
  34.1 0.1 copy.73
  34.3 0.1 copy.71
  34.4 0.1 copy.70
  34.5 5.0 %collective-permute-start.5 = (f32[4,32,288]{2,1,0:T(8,128)S(1)}, f32[4,32,288]{2,1,0:T(8,128)S(1)}, u32[]{:S(2)}, u32[]{:S(2)}) collective-permute-start(f32[4,32,288]{2,1,0:T(8,128)S(1)} %pad_maximum_fusion.1), channel_id=1, source_target_pairs={{32,0},{64,32},{96,64},{128,96},{160,128},{192,160},{224,192},{256... | collective-permute-start | bytes 442376 | tf_op jit(solution)/shard_map/ppermute | solution.py:17
  39.5 0.4 fusion.10
  40.0 0.4 collective-permute-done.4
  40.5 2.2 %collective-permute-done.5 = f32[4,32,288]{2,1,0:T(8,128)S(1)} collective-permute-done((f32[4,32,288]{2,1,0:T(8,128)S(1)}, f32[4,32,288]{2,1,0:T(8,128)S(1)}, u32[]{:S(2)}, u32[]{:S(2)}) %collective-permute-start.5) | collective-permute-done | bytes 147488 | tf_op jit(solution)/shard_map/ppermute | solution.py:17
  42.7 7.7 %collective-permute-start.7 = (f32[8,32,288]{2,1,0:T(8,128)S(1)}, f32[8,32,288]{2,1,0:T(8,128)S(1)}, u32[]{:S(2)}, u32[]{:S(2)}) collective-permute-start(f32[8,32,288]{2,1,0:T(8,128)S(1)} %get-tuple-element.39), channel_id=1, source_target_pairs={{1,0},{2,1},{3,2},{4,3},{5,4},{6,5},{7,6},{8,7},{9,8},{10,9},{11,1... | collective-permute-start | bytes 884744 | tf_op jit(solution)/shard_map/ppermute | solution.py:17
  50.4 0.7 fusion.5
  51.1 2.1 %collective-permute-start.6 = (f32[8,32,288]{2,1,0:T(8,128)S(1)}, f32[8,32,288]{2,1,0:T(8,128)S(1)}, u32[]{:S(2)}, u32[]{:S(2)}) collective-permute-start(f32[8,32,288]{2,1,0:T(8,128)S(1)} %get-tuple-element.38), channel_id=1, source_target_pairs={{0,1},{1,2},{2,3},{3,4},{4,5},{5,6},{6,7},{7,8},{8,9},{9,10},{10,1... | collective-permute-start | bytes 884744 | tf_op jit(solution)/shard_map/ppermute | solution.py:17
  53.2 0.5 convolution_add_fusion.1
  53.8 4.5 %collective-permute-done.7 = f32[8,32,288]{2,1,0:T(8,128)S(1)} collective-permute-done((f32[8,32,288]{2,1,0:T(8,128)S(1)}, f32[8,32,288]{2,1,0:T(8,128)S(1)}, u32[]{:S(2)}, u32[]{:S(2)}) %collective-permute-start.7) | collective-permute-done | bytes 294944 | tf_op jit(solution)/shard_map/ppermute | solution.py:17
  58.2 0.8 fusion.6
  59.0 7.4 %collective-permute-done.6 = f32[8,32,288]{2,1,0:T(8,128)S(1)} collective-permute-done((f32[8,32,288]{2,1,0:T(8,128)S(1)}, f32[8,32,288]{2,1,0:T(8,128)S(1)}, u32[]{:S(2)}, u32[]{:S(2)}) %collective-permute-start.6) | collective-permute-done | bytes 294944 | tf_op jit(solution)/shard_map/ppermute | solution.py:17
  66.4 0.8 fusion.8
  67.2 0.6 fusion.3
  67.8 0.7 fusion.4
  68.5 0.6 fusion.45
  69.5 0.1 maximum_bitcast_fusion.1
  69.6 1.9 %collective-permute-start.9 = (f32[3,32,288]{2,1,0:T(8,128)S(1)}, f32[3,32,288]{2,1,0:T(8,128)S(1)}, u32[]{:S(2)}, u32[]{:S(2)}) collective-permute-start(f32[3,32,288]{2,1,0:T(8,128)S(1)} %pad_maximum_fusion.3), channel_id=1, source_target_pairs={{32,0},{64,32},{96,64},{128,96},{160,128},{192,160},{224,192},{256... | collective-permute-start | bytes 331784 | tf_op jit(solution)/shard_map/ppermute | solution.py:17
  71.7 2.4 %collective-permute-start.8 = (f32[3,32,288]{2,1,0:T(8,128)S(1)}, f32[3,32,288]{2,1,0:T(8,128)S(1)}, u32[]{:S(2)}, u32[]{:S(2)}) collective-permute-start(f32[3,32,288]{2,1,0:T(8,128)S(1)} %pad_maximum_fusion.2), channel_id=1, source_target_pairs={{0,32},{32,64},{64,96},{96,128},{128,160},{160,192},{192,224},{224... | collective-permute-start | bytes 331784 | tf_op jit(solution)/shard_map/ppermute | solution.py:17
  74.3 5.0 %collective-permute-done.8 = f32[3,32,288]{2,1,0:T(8,128)S(1)} collective-permute-done((f32[3,32,288]{2,1,0:T(8,128)S(1)}, f32[3,32,288]{2,1,0:T(8,128)S(1)}, u32[]{:S(2)}, u32[]{:S(2)}) %collective-permute-start.8) | collective-permute-done | bytes 110624 | tf_op jit(solution)/shard_map/ppermute | solution.py:17
  79.4 1.9 %collective-permute-start.11 = (f32[32,288]{1,0:T(8,128)S(1)}, f32[32,288]{1,0:T(8,128)S(1)}, u32[]{:S(2)}, u32[]{:S(2)}) collective-permute-start(f32[32,288]{1,0:T(8,128)S(1)} %get-tuple-element.43), channel_id=1, source_target_pairs={{1,0},{2,1},{3,2},{4,3},{5,4},{6,5},{7,6},{8,7},{9,8},{10,9},{11,1... | collective-permute-start | bytes 110600 | tf_op jit(solution)/shard_map/ppermute | solution.py:17
  81.3 3.9 %collective-permute-start.10 = (f32[32,288]{1,0:T(8,128)S(1)}, f32[32,288]{1,0:T(8,128)S(1)}, u32[]{:S(2)}, u32[]{:S(2)}) collective-permute-start(f32[32,288]{1,0:T(8,128)S(1)} %get-tuple-element.42), channel_id=1, source_target_pairs={{0,1},{1,2},{2,3},{3,4},{4,5},{5,6},{6,7},{7,8},{8,9},{9,10},{10,1... | collective-permute-start | bytes 110600 | tf_op jit(solution)/shard_map/ppermute | solution.py:17
  86.1 4.5 %collective-permute-done.10 = f32[32,288]{1,0:T(8,128)S(1)} collective-permute-done((f32[32,288]{1,0:T(8,128)S(1)}, f32[32,288]{1,0:T(8,128)S(1)}, u32[]{:S(2)}, u32[]{:S(2)}) %collective-permute-start.10) | collective-permute-done | bytes 36896 | tf_op jit(solution)/shard_map/ppermute | solution.py:17
  90.7 1.9 %collective-permute-start.12 = (f32[1,33,288]{2,1,0:T(8,128)S(1)}, f32[1,33,288]{2,1,0:T(8,128)S(1)}, u32[]{:S(2)}, u32[]{:S(2)}) collective-permute-start(f32[1,33,288]{2,1,0:T(8,128)S(1)} %pad_bitcast_fusion), channel_id=1, source_target_pairs={{0,32},{32,0},{64,96},{96,64},{128,160},{160,128},{192,224},{224,1... | collective-permute-start | bytes 114056 | tf_op jit(solution)/shard_map/ppermute | solution.py:154
  92.6 1.2 %collective-permute-done.12 = f32[1,33,288]{2,1,0:T(8,128)S(1)} collective-permute-done((f32[1,33,288]{2,1,0:T(8,128)S(1)}, f32[1,33,288]{2,1,0:T(8,128)S(1)}, u32[]{:S(2)}, u32[]{:S(2)}) %collective-permute-start.12) | collective-permute-done | bytes 38048 | tf_op jit(solution)/shard_map/ppermute | solution.py:154
  93.8 1.9 %collective-permute-start.13 = (f32[2,33,288]{2,1,0:T(8,128)S(1)}, f32[2,33,288]{2,1,0:T(8,128)S(1)}, u32[]{:S(2)}, u32[]{:S(2)}) collective-permute-start(f32[2,33,288]{2,1,0:T(8,128)S(1)} %pad_maximum_fusion.4), channel_id=1, source_target_pairs={{0,64},{32,96},{64,0},{96,32},{128,192},{160,224},{192,128},{224,1... | collective-permute-start | bytes 228104 | tf_op jit(solution)/shard_map/ppermute | solution.py:154
  95.8 0.5 slice.1078
  98.9 2.2 %collective-permute-done.13 = f32[2,33,288]{2,1,0:T(8,128)S(1)} collective-permute-done((f32[2,33,288]{2,1,0:T(8,128)S(1)}, f32[2,33,288]{2,1,0:T(8,128)S(1)}, u32[]{:S(2)}, u32[]{:S(2)}) %collective-permute-start.13) | collective-permute-done | bytes 76064 | tf_op jit(solution)/shard_map/ppermute | solution.py:154
  101.1 0.5 slice.1076
  102.9 0.5 slice.1073
  107.4 0.7 maximum_bitcast_fusion
  (117 shorter events, 3.4 us)
Async XLA Ops:
  0.6 29.4 %copy-start = (f32[2,2,2,32,32]{4,3,2,1,0:T(8,128)S(1)}, f32[2,2,2,32,32]{4,3,2,1,0:T(8,128)}, u32[]{:S(2)}) copy-start(f32[2,2,2,32,32]{4,3,2,1,0:T(8,128)} %param.18) | copy-start | bytes 98308
  0.6 9.7 %copy-start.3 = (f32[2,2,2,32,864]{4,3,2,1,0:T(8,128)S(1)}, f32[2,2,2,32,864]{4,3,2,1,0:T(8,128)}, u32[]{:S(2)}) copy-start(f32[2,2,2,32,864]{4,3,2,1,0:T(8,128)} %param.15) | copy-start | bytes 2654212
  1.7 13.2 %collective-permute-start = (f32[2,2,32,32]{2,3,1,0:T(8,128)S(1)}, f32[2,2,32,32]{2,3,1,0:T(8,128)S(1)}, u32[]{:S(2)}, u32[]{:S(2)}) collective-permute-start(f32[2,2,32,32]{2,3,1,0:T(8,128)S(1)} %bitcast.271), channel_id=1, source_target_pairs={{0,32},{32,64},{64,96},{96,128},{128,160},{160,192},{192,224},{224... | collective-permute-start | bytes 49160 | tf_op jit(solution)/shard_map/ppermute | solution.py:17
  3.7 11.4 %collective-permute-start.1 = (f32[2,2,32,32]{2,3,1,0:T(8,128)S(1)}, f32[2,2,32,32]{2,3,1,0:T(8,128)S(1)}, u32[]{:S(2)}, u32[]{:S(2)}) collective-permute-start(f32[2,2,32,32]{2,3,1,0:T(8,128)S(1)} %bitcast.270), channel_id=1, source_target_pairs={{32,0},{64,32},{96,64},{128,96},{160,128},{192,160},{224,192},{256... | collective-permute-start | bytes 49160 | tf_op jit(solution)/shard_map/ppermute | solution.py:17
  10.5 0.7 copy-start.10
  10.5 0.7 copy-start.11
  10.5 0.7 copy-start.7
  11.9 0.7 copy-start.8
  11.9 0.7 copy-start.9
  14.4 12.6 %copy-start.1 = (f32[1024,288]{0,1:T(8,128)S(1)}, f32[1024,288]{0,1:T(8,128)}, u32[]{:S(2)}) copy-start(f32[1024,288]{0,1:T(8,128)} %copy.63) | copy-start | bytes 3538948
  14.4 12.7 %copy-start.6 = (f32[32,288]{1,0:T(8,128)S(1)}, f32[32,288]{1,0:T(8,128)}, u32[]{:S(2)}) copy-start(f32[32,288]{1,0:T(8,128)} %constant.76.clone) | copy-start | bytes 110596
  15.1 10.2 %collective-permute-start.2 = (f32[8,32,32]{1,2,0:T(8,128)S(1)}, f32[8,32,32]{1,2,0:T(8,128)S(1)}, u32[]{:S(2)}, u32[]{:S(2)}) collective-permute-start(f32[8,32,32]{1,2,0:T(8,128)S(1)} %constant_dynamic-update-slice_fusion.8), channel_id=1, source_target_pairs={{0,1},{1,2},{2,3},{3,4},{4,5},{5,6},{6,7},{7,8},{8,9},{9,10},{10,1... | collective-permute-start | bytes 98312 | tf_op jit(solution)/shard_map/ppermute | solution.py:17
  18.5 8.3 %collective-permute-start.3 = (f32[8,32,32]{1,2,0:T(8,128)S(1)}, f32[8,32,32]{1,2,0:T(8,128)S(1)}, u32[]{:S(2)}, u32[]{:S(2)}) collective-permute-start(f32[8,32,32]{1,2,0:T(8,128)S(1)} %get-tuple-element.144), channel_id=1, source_target_pairs={{1,0},{2,1},{3,2},{4,3},{5,4},{6,5},{7,6},{8,7},{9,8},{10,9},{11,1... | collective-permute-start | bytes 98312 | tf_op jit(solution)/shard_map/ppermute | solution.py:17
  30.0 0.9 copy-start.2
  32.1 8.2 %collective-permute-start.4 = (f32[4,32,288]{2,1,0:T(8,128)S(1)}, f32[4,32,288]{2,1,0:T(8,128)S(1)}, u32[]{:S(2)}, u32[]{:S(2)}) collective-permute-start(f32[4,32,288]{2,1,0:T(8,128)S(1)} %pad_maximum_fusion), channel_id=1, source_target_pairs={{0,32},{32,64},{64,96},{96,128},{128,160},{160,192},{192,224},{224... | collective-permute-start | bytes 442376 | tf_op jit(solution)/shard_map/ppermute | solution.py:17
  34.5 15.9 %copy-start.5 = (pred[288,288]{1,0:T(32,128)(4,1)S(1)}, pred[288,288]{1,0:T(32,128)(4,1)}, u32[]{:S(2)}) copy-start(pred[288,288]{1,0:T(32,128)(4,1)} %constant.84.clone) | copy-start | bytes 248836
  34.5 8.2 %collective-permute-start.5 = (f32[4,32,288]{2,1,0:T(8,128)S(1)}, f32[4,32,288]{2,1,0:T(8,128)S(1)}, u32[]{:S(2)}, u32[]{:S(2)}) collective-permute-start(f32[4,32,288]{2,1,0:T(8,128)S(1)} %pad_maximum_fusion.1), channel_id=1, source_target_pairs={{32,0},{64,32},{96,64},{128,96},{160,128},{192,160},{224,192},{256... | collective-permute-start | bytes 442376 | tf_op jit(solution)/shard_map/ppermute | solution.py:17
  42.7 15.5 %collective-permute-start.7 = (f32[8,32,288]{2,1,0:T(8,128)S(1)}, f32[8,32,288]{2,1,0:T(8,128)S(1)}, u32[]{:S(2)}, u32[]{:S(2)}) collective-permute-start(f32[8,32,288]{2,1,0:T(8,128)S(1)} %get-tuple-element.39), channel_id=1, source_target_pairs={{1,0},{2,1},{3,2},{4,3},{5,4},{6,5},{7,6},{8,7},{9,8},{10,9},{11,1... | collective-permute-start | bytes 884744 | tf_op jit(solution)/shard_map/ppermute | solution.py:17
  51.1 15.3 %collective-permute-start.6 = (f32[8,32,288]{2,1,0:T(8,128)S(1)}, f32[8,32,288]{2,1,0:T(8,128)S(1)}, u32[]{:S(2)}, u32[]{:S(2)}) collective-permute-start(f32[8,32,288]{2,1,0:T(8,128)S(1)} %get-tuple-element.38), channel_id=1, source_target_pairs={{0,1},{1,2},{2,3},{3,4},{4,5},{5,6},{6,7},{7,8},{8,9},{9,10},{10,1... | collective-permute-start | bytes 884744 | tf_op jit(solution)/shard_map/ppermute | solution.py:17
  69.4 15.9 %copy-start.12 = (s32[1,1,9]{2,1,0:T(1,128)S(1)}, s32[1,1,9]{2,1,0:T(1,128)}, u32[]{:S(2)}) copy-start(s32[1,1,9]{2,1,0:T(1,128)} %param.19) | copy-start | bytes 112
  69.6 4.7 %collective-permute-start.9 = (f32[3,32,288]{2,1,0:T(8,128)S(1)}, f32[3,32,288]{2,1,0:T(8,128)S(1)}, u32[]{:S(2)}, u32[]{:S(2)}) collective-permute-start(f32[3,32,288]{2,1,0:T(8,128)S(1)} %pad_maximum_fusion.3), channel_id=1, source_target_pairs={{32,0},{64,32},{96,64},{128,96},{160,128},{192,160},{224,192},{256... | collective-permute-start | bytes 331784 | tf_op jit(solution)/shard_map/ppermute | solution.py:17
  71.7 7.7 %collective-permute-start.8 = (f32[3,32,288]{2,1,0:T(8,128)S(1)}, f32[3,32,288]{2,1,0:T(8,128)S(1)}, u32[]{:S(2)}, u32[]{:S(2)}) collective-permute-start(f32[3,32,288]{2,1,0:T(8,128)S(1)} %pad_maximum_fusion.2), channel_id=1, source_target_pairs={{0,32},{32,64},{64,96},{96,128},{128,160},{160,192},{192,224},{224... | collective-permute-start | bytes 331784 | tf_op jit(solution)/shard_map/ppermute | solution.py:17
  79.4 6.7 %collective-permute-start.11 = (f32[32,288]{1,0:T(8,128)S(1)}, f32[32,288]{1,0:T(8,128)S(1)}, u32[]{:S(2)}, u32[]{:S(2)}) collective-permute-start(f32[32,288]{1,0:T(8,128)S(1)} %get-tuple-element.43), channel_id=1, source_target_pairs={{1,0},{2,1},{3,2},{4,3},{5,4},{6,5},{7,6},{8,7},{9,8},{10,9},{11,1... | collective-permute-start | bytes 110600 | tf_op jit(solution)/shard_map/ppermute | solution.py:17
  81.3 9.3 %collective-permute-start.10 = (f32[32,288]{1,0:T(8,128)S(1)}, f32[32,288]{1,0:T(8,128)S(1)}, u32[]{:S(2)}, u32[]{:S(2)}) collective-permute-start(f32[32,288]{1,0:T(8,128)S(1)} %get-tuple-element.42), channel_id=1, source_target_pairs={{0,1},{1,2},{2,3},{3,4},{4,5},{5,6},{6,7},{7,8},{8,9},{9,10},{10,1... | collective-permute-start | bytes 110600 | tf_op jit(solution)/shard_map/ppermute | solution.py:17
  90.7 17.4 %copy-start.4 = (f32[32,288]{1,0:T(8,128)}, f32[32,288]{1,0:T(8,128)S(1)}, u32[]{:S(2)}) copy-start(f32[32,288]{1,0:T(8,128)S(1)} %fusion.21) | copy-start | bytes 110596
  90.7 3.1 %collective-permute-start.12 = (f32[1,33,288]{2,1,0:T(8,128)S(1)}, f32[1,33,288]{2,1,0:T(8,128)S(1)}, u32[]{:S(2)}, u32[]{:S(2)}) collective-permute-start(f32[1,33,288]{2,1,0:T(8,128)S(1)} %pad_bitcast_fusion), channel_id=1, source_target_pairs={{0,32},{32,0},{64,96},{96,64},{128,160},{160,128},{192,224},{224,1... | collective-permute-start | bytes 114056 | tf_op jit(solution)/shard_map/ppermute | solution.py:154
  93.8 7.3 %collective-permute-start.13 = (f32[2,33,288]{2,1,0:T(8,128)S(1)}, f32[2,33,288]{2,1,0:T(8,128)S(1)}, u32[]{:S(2)}, u32[]{:S(2)}) collective-permute-start(f32[2,33,288]{2,1,0:T(8,128)S(1)} %pad_maximum_fusion.4), channel_id=1, source_target_pairs={{0,64},{32,96},{64,0},{96,32},{128,192},{160,224},{192,128},{224,1... | collective-permute-start | bytes 228104 | tf_op jit(solution)/shard_map/ppermute | solution.py:154

commit v5 on v4

--- a/solution.py
+++ b/solution.py
@@ -141,18 +141,39 @@
             line.append(jnp.concatenate(pieces, axis=1))
         partial_rows.append(jnp.stack(line))
 
-    acc = partial_rows[1] + shift(partial_rows[2], "gx", True) + shift(partial_rows[0], "gx", False)
-    total = acc[1] + shift(acc[2], "gy", True) + shift(acc[0], "gy", False)
+    partial_rows = jnp.stack(partial_rows)
+    acc = partial_rows[:, 1] + shift(partial_rows[:, 2], "gy", True) + shift(partial_rows[:, 0], "gy", False)
     column_mask = jnp.repeat(coarse_pattern[0, 0].astype(jnp.float32), width)[None, :]
-    coarse_block = total * column_mask
-
     slot_row = jnp.broadcast_to(slot.astype(jnp.float32).reshape(1, 1), (1, 9 * width))
-    payload = jnp.concatenate([coarse_block, slot_row], axis=0)
+    mine = jnp.concatenate([acc.reshape(3 * width, 9 * width), column_mask, slot_row], axis=0)
     count = lax.axis_size("gx")
-    held = payload[None]
-    for level in (0, 1):
-        partner = lax.ppermute(held, "gx", [(i, i ^ (1 << level)) for i in range(count)])
-        held = jnp.concatenate([held, partner], axis=0)
+    odd = here_x % 2 == 1
+    partner = lax.ppermute(mine, "gx", [(i, i ^ 1) for i in range(count)])
+    edge_piece = jnp.where(odd, acc[2], acc[0])
+    near_pairs = [(i, i + 1 if i % 2 else i - 1) for i in range(count)]
+    far_pairs = [(i, i + 2 if i % 2 else i - 2) for i in range(count)]
+    near = lax.ppermute(edge_piece, "gx", [pair for pair in near_pairs if 0 <= pair[1] < count])
+    far = lax.ppermute(edge_piece, "gx", [pair for pair in far_pairs if 0 <= pair[1] < count])
+    before = jnp.where(odd, far, near)
+    after = jnp.where(odd, near, far)
+    lower = jnp.where(odd, partner, mine)
+    upper = jnp.where(odd, mine, partner)
+
+    def rows_of(held, index):
+        return held[index * width : (index + 1) * width]
+
+    total_lower = before + rows_of(lower, 1) + rows_of(upper, 0)
+    total_upper = rows_of(lower, 2) + rows_of(upper, 1) + after
+    coarse_lower = total_lower * lower[3 * width : 3 * width + 1]
+    coarse_upper = total_upper * upper[3 * width : 3 * width + 1]
+    coarse_block = jnp.where(odd, coarse_upper, coarse_lower)
+    held = jnp.stack(
+        [
+            jnp.concatenate([coarse_lower, lower[3 * width + 1 :]], axis=0),
+            jnp.concatenate([coarse_upper, upper[3 * width + 1 :]], axis=0),
+        ]
+    )
+    held = jnp.concatenate([held, lax.ppermute(held, "gx", [(i, i ^ 2) for i in range(count)])], axis=0)
     members = [held[index] for index in range(4)]
     grouped = []
     for target in range(4):

time: 109 us -> 116 us (1.064)
  the two profiles are of different devices: /device:TPU:288 before, /device:TPU:161 now
where the time goes in v5:
time: 116 us; the launch traced here: 115 us
  starting transfers between devices  52.1 us (45%)
  waiting for transfers between devices  27 us (23%)
  between operations  13 us (11%)
  local copies, waits for them, and re-layouts  11.3 us (10%)
  matrix products  9.05 us (8%)
  other arithmetic  2.72 us (2%)
    ppermute x10, starting transfers between devices, shift(): return lax.ppermute(block, axis, pairs)  36.5 us
    ppermute x10, waiting for transfers between devices, shift(): return lax.ppermute(block, axis, pairs)  25.4 us
    ppermute x1, starting transfers between devices, local(): lax.ppermute(held, 'gx', [(i, i ^ 2) for i in range(count)])  7.74 us
    ppermute x1, starting transfers between devices, local(): lax.ppermute(edge_piece, 'gx', [pair for pair in near_pairs if 0 <= pair[...  3.64 us
    dot_general x5, matrix products, local(): jnp.dot(stencil_pos[:, first:last], part.reshape(len(group) * width, -1),...  3.1 us
  transfers between devices with their start and end apart: 14, of which 8 were waited for; matrix products, arithmetic and copies ran while one was open for 9% of the time, Pallas kernels for 0%

profile of v5, /device:TPU:161, one launch (start us, length us, event | category | flops | bytes accessed | tf_op | source)
XLA Modules:
  0.0 115.2 jit_solution(15635128405207090830)
XLA Ops:
  0.7 1.0 fusion.40
  1.7 4.6 %collective-permute-start = (f32[2,2,32,32]{2,3,1,0:T(8,128)S(1)}, f32[2,2,32,32]{2,3,1,0:T(8,128)S(1)}, u32[]{:S(2)}, u32[]{:S(2)}) collective-permute-start(f32[2,2,32,32]{2,3,1,0:T(8,128)S(1)} %bitcast.276), channel_id=1, source_target_pairs={{0,32},{32,64},{64,96},{96,128},{128,160},{160,192},{192,224},{224... | collective-permute-start | bytes 49160 | tf_op jit(solution)/shard_map/ppermute | solution.py:17
  6.4 1.9 %collective-permute-start.1 = (f32[2,2,32,32]{2,3,1,0:T(8,128)S(1)}, f32[2,2,32,32]{2,3,1,0:T(8,128)S(1)}, u32[]{:S(2)}, u32[]{:S(2)}) collective-permute-start(f32[2,2,32,32]{2,3,1,0:T(8,128)S(1)} %bitcast.275), channel_id=1, source_target_pairs={{32,0},{64,32},{96,64},{128,96},{160,128},{192,160},{224,192},{256... | collective-permute-start | bytes 49160 | tf_op jit(solution)/shard_map/ppermute | solution.py:17
  8.3 0.9 fusion.41
  9.2 0.7 convert_element_type.24
  10.0 0.1 mul.65
  10.3 0.1 fusion.48
  10.6 0.3 copy-done.9
  11.1 0.1 fusion.46
  11.5 0.1 fusion.44
  11.9 0.1 fusion.42
  12.0 0.1 concatenate.87
  12.1 0.2 copy-done.7
  12.3 0.1 concatenate.88
  12.6 1.5 %copy.69 = f32[1024,288]{0,1:T(8,128)} copy(f32[1024,288]{1,0:T(8,128)S(1)} %bitcast.253) | data formatting | bytes 2359296 | tf_op jit(solution)/shard_map/reshape | solution.py:93
  14.8 3.1 %collective-permute-start.2 = (f32[8,32,32]{1,2,0:T(8,128)S(1)}, f32[8,32,32]{1,2,0:T(8,128)S(1)}, u32[]{:S(2)}, u32[]{:S(2)}) collective-permute-start(f32[8,32,32]{1,2,0:T(8,128)S(1)} %constant_dynamic-update-slice_fusion.8), channel_id=1, source_target_pairs={{0,1},{1,2},{2,3},{3,4},{4,5},{5,6},{6,7},{7,8},{8,9},{9,10},{10,1... | collective-permute-start | bytes 98312 | tf_op jit(solution)/shard_map/ppermute | solution.py:17
  17.9 5.5 %collective-permute-start.3 = (f32[8,32,32]{1,2,0:T(8,128)S(1)}, f32[8,32,32]{1,2,0:T(8,128)S(1)}, u32[]{:S(2)}, u32[]{:S(2)}) collective-permute-start(f32[8,32,32]{1,2,0:T(8,128)S(1)} %get-tuple-element.153), channel_id=1, source_target_pairs={{1,0},{2,1},{3,2},{4,3},{5,4},{6,5},{7,6},{8,7},{9,8},{10,9},{11,1... | collective-permute-start | bytes 98312 | tf_op jit(solution)/shard_map/ppermute | solution.py:17
  23.5 1.9 %collective-permute-done.2 = f32[8,32,32]{1,2,0:T(8,128)S(1)} collective-permute-done((f32[8,32,32]{1,2,0:T(8,128)S(1)}, f32[8,32,32]{1,2,0:T(8,128)S(1)}, u32[]{:S(2)}, u32[]{:S(2)}) %collective-permute-start.2) | collective-permute-done | bytes 32800 | tf_op jit(solution)/shard_map/ppermute | solution.py:17
  25.3 0.9 collective-permute-done.3
  26.2 0.2 concatenate.90
  26.4 1.1 convolution_multiply_fusion
  27.6 1.8 %fusion.50 = f32[256,288]{1,0:T(8,128)S(1)} fusion(f32[256,1024]{1,0:T(8,128)S(1)} %constant_dynamic-update-slice_fusion, f32[1024,288]{0,1:T(8,128)S(1)} %convolution_multiply_fusion), kind=kOutput, calls=%fused_computation.176 | convolution fusion | flops 905969664 | bytes 2523136 | tf_op jit(solution)/shard_map/dot_general | solution.py:95
  29.5 0.5 convolution_multiply_fusion.1
  29.9 0.1 copy.71
  30.1 0.3 copy-done.2
  30.3 0.4 fusion.2
  30.8 0.3 slice_bitcast_fusion.4
  31.2 0.1 copy.74
  31.3 0.1 copy.73
  31.4 0.1 copy.72
  31.5 4.6 %collective-permute-start.4 = (f32[4,32,288]{2,1,0:T(8,128)S(1)}, f32[4,32,288]{2,1,0:T(8,128)S(1)}, u32[]{:S(2)}, u32[]{:S(2)}) collective-permute-start(f32[4,32,288]{2,1,0:T(8,128)S(1)} %pad_maximum_fusion.1), channel_id=1, source_target_pairs={{0,32},{32,64},{64,96},{96,128},{128,160},{160,192},{192,224},{224... | collective-permute-start | bytes 442376 | tf_op jit(solution)/shard_map/ppermute | solution.py:17
  36.2 0.1 copy.79
  36.3 0.1 copy.77
  36.4 0.1 copy.76
  36.6 2.1 %collective-permute-start.5 = (f32[4,32,288]{2,1,0:T(8,128)S(1)}, f32[4,32,288]{2,1,0:T(8,128)S(1)}, u32[]{:S(2)}, u32[]{:S(2)}) collective-permute-start(f32[4,32,288]{2,1,0:T(8,128)S(1)} %pad_maximum_fusion.2), channel_id=1, source_target_pairs={{32,0},{64,32},{96,64},{128,96},{160,128},{192,160},{224,192},{256... | collective-permute-start | bytes 442376 | tf_op jit(solution)/shard_map/ppermute | solution.py:17
  38.6 0.4 fusion.10
  39.2 4.5 %collective-permute-done.5 = f32[4,32,288]{2,1,0:T(8,128)S(1)} collective-permute-done((f32[4,32,288]{2,1,0:T(8,128)S(1)}, f32[4,32,288]{2,1,0:T(8,128)S(1)}, u32[]{:S(2)}, u32[]{:S(2)}) %collective-permute-start.5) | collective-permute-done | bytes 147488 | tf_op jit(solution)/shard_map/ppermute | solution.py:17
  43.7 7.4 %collective-permute-start.7 = (f32[8,32,288]{2,1,0:T(8,128)S(1)}, f32[8,32,288]{2,1,0:T(8,128)S(1)}, u32[]{:S(2)}, u32[]{:S(2)}) collective-permute-start(f32[8,32,288]{2,1,0:T(8,128)S(1)} %get-tuple-element.46), channel_id=1, source_target_pairs={{1,0},{2,1},{3,2},{4,3},{5,4},{6,5},{7,6},{8,7},{9,8},{10,9},{11,1... | collective-permute-start | bytes 884744 | tf_op jit(solution)/shard_map/ppermute | solution.py:17
  51.2 0.7 fusion.5
  51.9 2.1 %collective-permute-start.6 = (f32[8,32,288]{2,1,0:T(8,128)S(1)}, f32[8,32,288]{2,1,0:T(8,128)S(1)}, u32[]{:S(2)}, u32[]{:S(2)}) collective-permute-start(f32[8,32,288]{2,1,0:T(8,128)S(1)} %get-tuple-element.45), channel_id=1, source_target_pairs={{0,1},{1,2},{2,3},{3,4},{4,5},{5,6},{6,7},{7,8},{8,9},{9,10},{10,1... | collective-permute-start | bytes 884744 | tf_op jit(solution)/shard_map/ppermute | solution.py:17
  54.0 0.5 convolution_add_fusion.1
  54.6 4.1 %collective-permute-done.7 = f32[8,32,288]{2,1,0:T(8,128)S(1)} collective-permute-done((f32[8,32,288]{2,1,0:T(8,128)S(1)}, f32[8,32,288]{2,1,0:T(8,128)S(1)}, u32[]{:S(2)}, u32[]{:S(2)}) %collective-permute-start.7) | collective-permute-done | bytes 294944 | tf_op jit(solution)/shard_map/ppermute | solution.py:17
  58.6 0.8 fusion.6
  59.4 7.4 %collective-permute-done.6 = f32[8,32,288]{2,1,0:T(8,128)S(1)} collective-permute-done((f32[8,32,288]{2,1,0:T(8,128)S(1)}, f32[8,32,288]{2,1,0:T(8,128)S(1)}, u32[]{:S(2)}, u32[]{:S(2)}) %collective-permute-start.6) | collective-permute-done | bytes 294944 | tf_op jit(solution)/shard_map/ppermute | solution.py:17
  66.8 0.8 fusion.8
  67.5 0.6 fusion.3
  68.1 0.7 fusion.4
  68.8 0.6 fusion.51
  70.0 0.1 maximum_bitcast_fusion.6
  70.4 1.9 %collective-permute-start.9 = (f32[3,32,288]{2,1,0:T(8,128)S(1)}, f32[3,32,288]{2,1,0:T(8,128)S(1)}, u32[]{:S(2)}, u32[]{:S(2)}) collective-permute-start(f32[3,32,288]{2,1,0:T(8,128)S(1)} %get-tuple-element.14), channel_id=1, source_target_pairs={{1,0},{2,1},{3,2},{4,3},{5,4},{6,5},{7,6},{8,7},{9,8},{10,9},{11,1... | collective-permute-start | bytes 331784 | tf_op jit(solution)/shard_map/ppermute | solution.py:17
  72.3 3.4 %collective-permute-start.8 = (f32[3,32,288]{2,1,0:T(8,128)S(1)}, f32[3,32,288]{2,1,0:T(8,128)S(1)}, u32[]{:S(2)}, u32[]{:S(2)}) collective-permute-start(f32[3,32,288]{2,1,0:T(8,128)S(1)} %get-tuple-element.13), channel_id=1, source_target_pairs={{0,1},{1,2},{2,3},{3,4},{4,5},{5,6},{6,7},{7,8},{8,9},{9,10},{10,1... | collective-permute-start | bytes 331784 | tf_op jit(solution)/shard_map/ppermute | solution.py:17
  76.6 1.5 %collective-permute-done.9 = f32[3,32,288]{2,1,0:T(8,128)S(1)} collective-permute-done((f32[3,32,288]{2,1,0:T(8,128)S(1)}, f32[3,32,288]{2,1,0:T(8,128)S(1)}, u32[]{:S(2)}, u32[]{:S(2)}) %collective-permute-start.9) | collective-permute-done | bytes 110624 | tf_op jit(solution)/shard_map/ppermute | solution.py:17
  78.1 5.2 %collective-permute-done.8 = f32[3,32,288]{2,1,0:T(8,128)S(1)} collective-permute-done((f32[3,32,288]{2,1,0:T(8,128)S(1)}, f32[3,32,288]{2,1,0:T(8,128)S(1)}, u32[]{:S(2)}, u32[]{:S(2)}) %collective-permute-start.8) | collective-permute-done | bytes 110624 | tf_op jit(solution)/shard_map/ppermute | solution.py:17
  83.5 2.3 %collective-permute-start.10 = (f32[98,288]{1,0:T(8,128)S(1)}, f32[98,288]{1,0:T(8,128)S(1)}, u32[]{:S(2)}, u32[]{:S(2)}) collective-permute-start(f32[98,288]{1,0:T(8,128)S(1)} %maximum_maximum_fusion), channel_id=1, source_target_pairs={{0,32},{32,0},{64,96},{96,64},{128,160},{160,128},{192,224},{224,1... | collective-permute-start | bytes 338696 | tf_op jit(solution)/shard_map/ppermute | solution.py:151
  85.8 1.9 %collective-permute-start.12 = (f32[32,288]{1,0:T(8,128)S(1)}, f32[32,288]{1,0:T(8,128)S(1)}, u32[]{:S(2)}, u32[]{:S(2)}) collective-permute-start(f32[32,288]{1,0:T(8,128)S(1)} %fusion.21), channel_id=1, source_target_pairs={{32,96},{64,0},{96,160},{128,64},{160,224},{192,128},{224,288},{25... | collective-permute-start | bytes 110600 | tf_op jit(solution)/shard_map/ppermute | solution.py:156
  87.7 3.6 %collective-permute-start.11 = (f32[32,288]{1,0:T(8,128)S(1)}, f32[32,288]{1,0:T(8,128)S(1)}, u32[]{:S(2)}, u32[]{:S(2)}) collective-permute-start(f32[32,288]{1,0:T(8,128)S(1)} %fusion.21), channel_id=1, source_target_pairs={{32,64},{64,32},{96,128},{128,96},{160,192},{192,160},{224,256},{2... | collective-permute-start | bytes 110600 | tf_op jit(solution)/shard_map/ppermute | solution.py:155
  91.5 1.6 %collective-permute-done.11 = f32[32,288]{1,0:T(8,128)S(1)} collective-permute-done((f32[32,288]{1,0:T(8,128)S(1)}, f32[32,288]{1,0:T(8,128)S(1)}, u32[]{:S(2)}, u32[]{:S(2)}) %collective-permute-start.11) | collective-permute-done | bytes 36896 | tf_op jit(solution)/shard_map/ppermute | solution.py:155
  93.1 0.6 select_bitcast_fusion.4
  93.8 7.7 %collective-permute-start.13 = (f32[2,33,288]{2,1,0:T(8,128)S(1)}, f32[2,33,288]{2,1,0:T(8,128)S(1)}, u32[]{:S(2)}, u32[]{:S(2)}) collective-permute-start(f32[2,33,288]{2,1,0:T(8,128)S(1)} %pad_maximum_fusion.3), channel_id=1, source_target_pairs={{0,64},{32,96},{64,0},{96,32},{128,192},{160,224},{192,128},{224,1... | collective-permute-start | bytes 228104 | tf_op jit(solution)/shard_map/ppermute | solution.py:176
  101.6 0.5 slice.1123
  102.1 0.6 slice.1122
  108.0 0.5 slice.1120
  109.8 0.6 slice.1117
  114.5 0.7 maximum_bitcast_fusion
  (125 shorter events, 3.7 us)
Async XLA Ops:
  0.6 28.8 %copy-start = (f32[2,2,2,32,32]{4,3,2,1,0:T(8,128)S(1)}, f32[2,2,2,32,32]{4,3,2,1,0:T(8,128)}, u32[]{:S(2)}) copy-start(f32[2,2,2,32,32]{4,3,2,1,0:T(8,128)} %param.18) | copy-start | bytes 98308
  0.6 9.5 %copy-start.3 = (f32[2,2,2,32,864]{4,3,2,1,0:T(8,128)S(1)}, f32[2,2,2,32,864]{4,3,2,1,0:T(8,128)}, u32[]{:S(2)}) copy-start(f32[2,2,2,32,864]{4,3,2,1,0:T(8,128)} %param.15) | copy-start | bytes 2654212
  1.7 12.9 %collective-permute-start = (f32[2,2,32,32]{2,3,1,0:T(8,128)S(1)}, f32[2,2,32,32]{2,3,1,0:T(8,128)S(1)}, u32[]{:S(2)}, u32[]{:S(2)}) collective-permute-start(f32[2,2,32,32]{2,3,1,0:T(8,128)S(1)} %bitcast.276), channel_id=1, source_target_pairs={{0,32},{32,64},{64,96},{96,128},{128,160},{160,192},{192,224},{224... | collective-permute-start | bytes 49160 | tf_op jit(solution)/shard_map/ppermute | solution.py:17
  6.4 8.4 %collective-permute-start.1 = (f32[2,2,32,32]{2,3,1,0:T(8,128)S(1)}, f32[2,2,32,32]{2,3,1,0:T(8,128)S(1)}, u32[]{:S(2)}, u32[]{:S(2)}) collective-permute-start(f32[2,2,32,32]{2,3,1,0:T(8,128)S(1)} %bitcast.275), channel_id=1, source_target_pairs={{32,0},{64,32},{96,64},{128,96},{160,128},{192,160},{224,192},{256... | collective-permute-start | bytes 49160 | tf_op jit(solution)/shard_map/ppermute | solution.py:17
  10.2 0.7 copy-start.9
  10.2 0.7 copy-start.10
  10.2 0.7 copy-start.6
  11.6 0.7 copy-start.7
  11.6 0.7 copy-start.8
  14.0 12.4 %copy-start.1 = (f32[1024,288]{0,1:T(8,128)S(1)}, f32[1024,288]{0,1:T(8,128)}, u32[]{:S(2)}) copy-start(f32[1024,288]{0,1:T(8,128)} %copy.69) | copy-start | bytes 3538948
  14.0 12.4 %copy-start.5 = (f32[32,288]{1,0:T(8,128)S(1)}, f32[32,288]{1,0:T(8,128)}, u32[]{:S(2)}) copy-start(f32[32,288]{1,0:T(8,128)} %constant.87.clone) | copy-start | bytes 110596
  14.8 10.5 %collective-permute-start.2 = (f32[8,32,32]{1,2,0:T(8,128)S(1)}, f32[8,32,32]{1,2,0:T(8,128)S(1)}, u32[]{:S(2)}, u32[]{:S(2)}) collective-permute-start(f32[8,32,32]{1,2,0:T(8,128)S(1)} %constant_dynamic-update-slice_fusion.8), channel_id=1, source_target_pairs={{0,1},{1,2},{2,3},{3,4},{4,5},{5,6},{6,7},{7,8},{8,9},{9,10},{10,1... | collective-permute-start | bytes 98312 | tf_op jit(solution)/shard_map/ppermute | solution.py:17
  17.9 8.3 %collective-permute-start.3 = (f32[8,32,32]{1,2,0:T(8,128)S(1)}, f32[8,32,32]{1,2,0:T(8,128)S(1)}, u32[]{:S(2)}, u32[]{:S(2)}) collective-permute-start(f32[8,32,32]{1,2,0:T(8,128)S(1)} %get-tuple-element.153), channel_id=1, source_target_pairs={{1,0},{2,1},{3,2},{4,3},{5,4},{6,5},{7,6},{8,7},{9,8},{10,9},{11,1... | collective-permute-start | bytes 98312 | tf_op jit(solution)/shard_map/ppermute | solution.py:17
  29.4 0.9 copy-start.2
  31.5 7.5 %collective-permute-start.4 = (f32[4,32,288]{2,1,0:T(8,128)S(1)}, f32[4,32,288]{2,1,0:T(8,128)S(1)}, u32[]{:S(2)}, u32[]{:S(2)}) collective-permute-start(f32[4,32,288]{2,1,0:T(8,128)S(1)} %pad_maximum_fusion.1), channel_id=1, source_target_pairs={{0,32},{32,64},{64,96},{96,128},{128,160},{160,192},{192,224},{224... | collective-permute-start | bytes 442376 | tf_op jit(solution)/shard_map/ppermute | solution.py:17
  36.6 14.6 %copy-start.4 = (pred[288,288]{1,0:T(32,128)(4,1)S(1)}, pred[288,288]{1,0:T(32,128)(4,1)}, u32[]{:S(2)}) copy-start(pred[288,288]{1,0:T(32,128)(4,1)} %constant.95.clone) | copy-start | bytes 248836
  36.6 7.1 %collective-permute-start.5 = (f32[4,32,288]{2,1,0:T(8,128)S(1)}, f32[4,32,288]{2,1,0:T(8,128)S(1)}, u32[]{:S(2)}, u32[]{:S(2)}) collective-permute-start(f32[4,32,288]{2,1,0:T(8,128)S(1)} %pad_maximum_fusion.2), channel_id=1, source_target_pairs={{32,0},{64,32},{96,64},{128,96},{160,128},{192,160},{224,192},{256... | collective-permute-start | bytes 442376 | tf_op jit(solution)/shard_map/ppermute | solution.py:17
  43.7 14.9 %collective-permute-start.7 = (f32[8,32,288]{2,1,0:T(8,128)S(1)}, f32[8,32,288]{2,1,0:T(8,128)S(1)}, u32[]{:S(2)}, u32[]{:S(2)}) collective-permute-start(f32[8,32,288]{2,1,0:T(8,128)S(1)} %get-tuple-element.46), channel_id=1, source_target_pairs={{1,0},{2,1},{3,2},{4,3},{5,4},{6,5},{7,6},{8,7},{9,8},{10,9},{11,1... | collective-permute-start | bytes 884744 | tf_op jit(solution)/shard_map/ppermute | solution.py:17
  51.9 14.9 %collective-permute-start.6 = (f32[8,32,288]{2,1,0:T(8,128)S(1)}, f32[8,32,288]{2,1,0:T(8,128)S(1)}, u32[]{:S(2)}, u32[]{:S(2)}) collective-permute-start(f32[8,32,288]{2,1,0:T(8,128)S(1)} %get-tuple-element.45), channel_id=1, source_target_pairs={{0,1},{1,2},{2,3},{3,4},{4,5},{5,6},{6,7},{7,8},{8,9},{9,10},{10,1... | collective-permute-start | bytes 884744 | tf_op jit(solution)/shard_map/ppermute | solution.py:17
  70.1 5.6 %copy-start.11 = (s32[1,1,9]{2,1,0:T(1,128)S(1)}, s32[1,1,9]{2,1,0:T(1,128)}, u32[]{:S(2)}) copy-start(s32[1,1,9]{2,1,0:T(1,128)} %param.19) | copy-start | bytes 112
  70.4 7.7 %collective-permute-start.9 = (f32[3,32,288]{2,1,0:T(8,128)S(1)}, f32[3,32,288]{2,1,0:T(8,128)S(1)}, u32[]{:S(2)}, u32[]{:S(2)}) collective-permute-start(f32[3,32,288]{2,1,0:T(8,128)S(1)} %get-tuple-element.14), channel_id=1, source_target_pairs={{1,0},{2,1},{3,2},{4,3},{5,4},{6,5},{7,6},{8,7},{9,8},{10,9},{11,1... | collective-permute-start | bytes 331784 | tf_op jit(solution)/shard_map/ppermute | solution.py:17
  72.3 11.0 %collective-permute-start.8 = (f32[3,32,288]{2,1,0:T(8,128)S(1)}, f32[3,32,288]{2,1,0:T(8,128)S(1)}, u32[]{:S(2)}, u32[]{:S(2)}) collective-permute-start(f32[3,32,288]{2,1,0:T(8,128)S(1)} %get-tuple-element.13), channel_id=1, source_target_pairs={{0,1},{1,2},{2,3},{3,4},{4,5},{5,6},{6,7},{7,8},{8,9},{9,10},{10,1... | collective-permute-start | bytes 331784 | tf_op jit(solution)/shard_map/ppermute | solution.py:17
  83.5 7.9 %collective-permute-start.10 = (f32[98,288]{1,0:T(8,128)S(1)}, f32[98,288]{1,0:T(8,128)S(1)}, u32[]{:S(2)}, u32[]{:S(2)}) collective-permute-start(f32[98,288]{1,0:T(8,128)S(1)} %maximum_maximum_fusion), channel_id=1, source_target_pairs={{0,32},{32,0},{64,96},{96,64},{128,160},{160,128},{192,224},{224,1... | collective-permute-start | bytes 338696 | tf_op jit(solution)/shard_map/ppermute | solution.py:151
  85.8 5.7 %collective-permute-start.12 = (f32[32,288]{1,0:T(8,128)S(1)}, f32[32,288]{1,0:T(8,128)S(1)}, u32[]{:S(2)}, u32[]{:S(2)}) collective-permute-start(f32[32,288]{1,0:T(8,128)S(1)} %fusion.21), channel_id=1, source_target_pairs={{32,96},{64,0},{96,160},{128,64},{160,224},{192,128},{224,288},{25... | collective-permute-start | bytes 110600 | tf_op jit(solution)/shard_map/ppermute | solution.py:156
  87.7 5.4 %collective-permute-start.11 = (f32[32,288]{1,0:T(8,128)S(1)}, f32[32,288]{1,0:T(8,128)S(1)}, u32[]{:S(2)}, u32[]{:S(2)}) collective-permute-start(f32[32,288]{1,0:T(8,128)S(1)} %fusion.21), channel_id=1, source_target_pairs={{32,64},{64,32},{96,128},{128,96},{160,192},{192,160},{224,256},{2... | collective-permute-start | bytes 110600 | tf_op jit(solution)/shard_map/ppermute | solution.py:155
  93.8 14.1 %collective-permute-start.13 = (f32[2,33,288]{2,1,0:T(8,128)S(1)}, f32[2,33,288]{2,1,0:T(8,128)S(1)}, u32[]{:S(2)}, u32[]{:S(2)}) collective-permute-start(f32[2,33,288]{2,1,0:T(8,128)S(1)} %pad_maximum_fusion.3), channel_id=1, source_target_pairs={{0,64},{32,96},{64,0},{96,32},{128,192},{160,224},{192,128},{224,1... | collective-permute-start | bytes 228104 | tf_op jit(solution)/shard_map/ppermute | solution.py:176

commit v6 on v4

--- a/solution.py
+++ b/solution.py
@@ -92,7 +92,11 @@
     agg_mask = (block_of[None, :] == target[:, None]).astype(jnp.float32)
     agg_mask = jnp.broadcast_to(agg_mask[:, None, :], (32, width, 9 * width)).reshape(32 * width, 9 * width)
     tent_agg = jnp.dot(tent_frame, repeat, precision=HI) * agg_mask
-    coupled = jnp.dot(stencil_pos, tent_agg, precision=HI).reshape(8, width, 9 * width)
+    split = 16 * width
+    coupled = jnp.dot(stencil_pos[:, :split], tent_agg[:split], precision=HI) + jnp.dot(
+        stencil_pos[:, split:], tent_agg[split:], precision=HI
+    )
+    coupled = coupled.reshape(8, width, 9 * width)
     smoothed = jnp.einsum("crs,csn->crn", diag_inverse.reshape(8, width, width), coupled, precision=HI)
     own_mask = (block_of == column_block(0, 0)).astype(jnp.float32)[None, :]
     own_tent = jnp.dot(tentative.reshape(8 * width, width), repeat, precision=HI) * own_mask
@@ -109,21 +113,25 @@
     from_high = shift(jnp.stack([prolong[(spot[0], 1, spot[1])] for spot in ROW]), "gy", False)
     from_low = shift(jnp.stack([prolong[(spot[0], 2, spot[1])] for spot in ROW]), "gy", True)
     parts = [prolong_own, from_left, from_right, from_low, from_high]
-    applied = None
+    terms = []
     first = 0
     for group, part in zip(GROUPS, parts):
         last = first + len(group) * width
-        term = jnp.dot(stencil_pos[:, first:last], part.reshape(len(group) * width, -1), precision=HI)
-        applied = term if applied is None else applied + term
+        terms.append(jnp.dot(stencil_pos[:, first:last], part.reshape(len(group) * width, -1), precision=HI))
         first = last
+    applied_early = terms[0] + terms[1] + terms[2]
+    applied_late = terms[3] + terms[4]
 
     relative = np.arange(9 * width) // width
     moved = column_block(relative // 3 - 1, relative % 3 - 1)
     lane = np.arange(9 * width) % width
     reorder = ((block_of[:, None] == moved[None, :]) & (lane[:, None] == lane[None, :])).astype(jnp.float32)
-    applied = jnp.dot(applied, reorder, precision=HI)
     prolong_rel = jnp.dot(prolong_own, reorder, precision=HI)
-    product = lax.dot_general(prolong_rel, applied, (((0,), (0,)), ((), ())), precision=HI)
+    product = None
+    for applied in (applied_early, applied_late):
+        applied = jnp.dot(applied, reorder, precision=HI)
+        term = lax.dot_general(prolong_rel, applied, (((0,), (0,)), ((), ())), precision=HI)
+        product = term if product is None else product + term
     partial_rows = []
     for row_x in range(3):
         line = []

time: 109 us -> 113 us (1.037)
  the two profiles are of different devices: /device:TPU:288 before, /device:TPU:158 now
where the time goes in v6:
time: 113 us; the launch traced here: 112 us
  starting transfers between devices  52.9 us (47%)
  waiting for transfers between devices  26.9 us (24%)
  local copies, waits for them, and re-layouts  10.7 us (9%)
  between operations  10.2 us (9%)
  matrix products  9.95 us (9%)
  other arithmetic  1.86 us (2%)
    ppermute x12, starting transfers between devices, shift(): return lax.ppermute(block, axis, pairs)  42.3 us
    ppermute x12, waiting for transfers between devices, shift(): return lax.ppermute(block, axis, pairs)  25.3 us
    ppermute x2, starting transfers between devices, local(): lax.ppermute(held, 'gx', [(i, i ^ 1 << level) for i in range(count)])  10.6 us
    dot_general x5, matrix products, local(): jnp.dot(stencil_pos[:, first:last], part.reshape(len(group) * width, -1),...  3.09 us
  transfers between devices with their start and end apart: 14, of which 11 were waited for; matrix products, arithmetic and copies ran while one was open for 10% of the time, Pallas kernels for 0%

profile of v6, /device:TPU:158, one launch (start us, length us, event | category | flops | bytes accessed | tf_op | source)
XLA Modules:
  0.0 112.4 jit_solution(10588873730334119287)
XLA Ops:
  0.7 1.0 fusion.39
  1.7 1.9 %collective-permute-start = (f32[2,2,32,32]{2,3,1,0:T(8,128)S(1)}, f32[2,2,32,32]{2,3,1,0:T(8,128)S(1)}, u32[]{:S(2)}, u32[]{:S(2)}) collective-permute-start(f32[2,2,32,32]{2,3,1,0:T(8,128)S(1)} %bitcast.272), channel_id=1, source_target_pairs={{0,32},{32,64},{64,96},{96,128},{128,160},{160,192},{192,224},{224... | collective-permute-start | bytes 49160 | tf_op jit(solution)/shard_map/ppermute | solution.py:17
  3.7 3.6 %collective-permute-start.1 = (f32[2,2,32,32]{2,3,1,0:T(8,128)S(1)}, f32[2,2,32,32]{2,3,1,0:T(8,128)S(1)}, u32[]{:S(2)}, u32[]{:S(2)}) collective-permute-start(f32[2,2,32,32]{2,3,1,0:T(8,128)S(1)} %bitcast.271), channel_id=1, source_target_pairs={{32,0},{64,32},{96,64},{128,96},{160,128},{192,160},{224,192},{256... | collective-permute-start | bytes 49160 | tf_op jit(solution)/shard_map/ppermute | solution.py:17
  7.4 0.9 fusion.40
  8.3 0.7 convert_element_type.24
  9.1 0.1 mul.55
  9.4 0.1 fusion.47
  9.7 0.3 copy-done.10
  10.2 0.1 fusion.45
  10.5 0.1 fusion.43
  10.9 0.1 fusion.41
  11.1 0.1 concatenate.84
  11.2 0.2 copy-done.8
  12.1 0.1 broadcast_in_dim.149
  12.2 1.5 %copy.36 = f32[1024,288]{0,1:T(8,128)} copy(f32[1024,288]{1,0:T(8,128)S(1)} %bitcast.249) | data formatting | bytes 2359296 | tf_op jit(solution)/shard_map/reshape | solution.py:93
  13.9 4.7 %collective-permute-start.2 = (f32[8,32,32]{1,2,0:T(8,128)S(1)}, f32[8,32,32]{1,2,0:T(8,128)S(1)}, u32[]{:S(2)}, u32[]{:S(2)}) collective-permute-start(f32[8,32,32]{1,2,0:T(8,128)S(1)} %constant_dynamic-update-slice_fusion.8), channel_id=1, source_target_pairs={{0,1},{1,2},{2,3},{3,4},{4,5},{5,6},{6,7},{7,8},{8,9},{9,10},{10,1... | collective-permute-start | bytes 98312 | tf_op jit(solution)/shard_map/ppermute | solution.py:17
  18.7 1.9 %collective-permute-start.3 = (f32[8,32,32]{1,2,0:T(8,128)S(1)}, f32[8,32,32]{1,2,0:T(8,128)S(1)}, u32[]{:S(2)}, u32[]{:S(2)}) collective-permute-start(f32[8,32,32]{1,2,0:T(8,128)S(1)} %get-tuple-element.144), channel_id=1, source_target_pairs={{1,0},{2,1},{3,2},{4,3},{5,4},{6,5},{7,6},{8,7},{9,8},{10,9},{11,1... | collective-permute-start | bytes 98312 | tf_op jit(solution)/shard_map/ppermute | solution.py:17
  20.6 1.7 %collective-permute-done.2 = f32[8,32,32]{1,2,0:T(8,128)S(1)} collective-permute-done((f32[8,32,32]{1,2,0:T(8,128)S(1)}, f32[8,32,32]{1,2,0:T(8,128)S(1)}, u32[]{:S(2)}, u32[]{:S(2)}) %collective-permute-start.2) | collective-permute-done | bytes 32800 | tf_op jit(solution)/shard_map/ppermute | solution.py:17
  22.3 7.4 %collective-permute-done.3 = f32[8,32,32]{1,2,0:T(8,128)S(1)} collective-permute-done((f32[8,32,32]{1,2,0:T(8,128)S(1)}, f32[8,32,32]{1,2,0:T(8,128)S(1)}, u32[]{:S(2)}, u32[]{:S(2)}) %collective-permute-start.3) | collective-permute-done | bytes 32800 | tf_op jit(solution)/shard_map/ppermute | solution.py:17
  29.8 0.2 concatenate.87
  30.0 1.2 %convolution_multiply_fusion = f32[1024,288]{0,1:T(8,128)S(1)} fusion(f32[1024,288]{0,1:T(8,128)S(1)} %copy-done.1, f32[1024,32]{0,1:T(8,128)S(1)} %concatenate.87, f32[32,288]{1,0:T(8,128)S(1)} %copy-done.6), kind=kOutput, calls=%fused_computation | convolution fusion | flops 113541120 | bytes 2527232 | tf_op jit(solution)/shard_map/dot_general | solution.py:94
  31.1 0.7 fusion.3
  31.8 0.7 convolution_add_fusion.4
  32.5 0.2 copy.37
  32.7 0.5 convolution_multiply_fusion.1
  33.2 0.1 copy.38
  33.4 0.4 fusion.1
  33.9 0.3 slice_bitcast_fusion.3
  34.2 0.4 fusion.13
  34.7 0.1 copy.40
  35.1 1.9 %collective-permute-start.4 = (f32[4,32,288]{2,1,0:T(8,128)S(1)}, f32[4,32,288]{2,1,0:T(8,128)S(1)}, u32[]{:S(2)}, u32[]{:S(2)}) collective-permute-start(f32[4,32,288]{2,1,0:T(8,128)S(1)} %pad_maximum_fusion), channel_id=1, source_target_pairs={{0,32},{32,64},{64,96},{96,128},{128,160},{160,192},{192,224},{224... | collective-permute-start | bytes 442376 | tf_op jit(solution)/shard_map/ppermute | solution.py:17
  37.1 0.1 copy.44
  37.5 3.6 %collective-permute-start.5 = (f32[4,32,288]{2,1,0:T(8,128)S(1)}, f32[4,32,288]{2,1,0:T(8,128)S(1)}, u32[]{:S(2)}, u32[]{:S(2)}) collective-permute-start(f32[4,32,288]{2,1,0:T(8,128)S(1)} %pad_maximum_fusion.1), channel_id=1, source_target_pairs={{32,0},{64,32},{96,64},{128,96},{160,128},{192,160},{224,192},{256... | collective-permute-start | bytes 442376 | tf_op jit(solution)/shard_map/ppermute | solution.py:17
  41.1 0.7 fusion.9
  41.9 0.2 collective-permute-done.4
  42.2 2.1 %collective-permute-done.5 = f32[4,32,288]{2,1,0:T(8,128)S(1)} collective-permute-done((f32[4,32,288]{2,1,0:T(8,128)S(1)}, f32[4,32,288]{2,1,0:T(8,128)S(1)}, u32[]{:S(2)}, u32[]{:S(2)}) %collective-permute-start.5) | collective-permute-done | bytes 147488 | tf_op jit(solution)/shard_map/ppermute | solution.py:17
  44.3 1.9 %collective-permute-start.7 = (f32[8,32,288]{2,1,0:T(8,128)S(1)}, f32[8,32,288]{2,1,0:T(8,128)S(1)}, u32[]{:S(2)}, u32[]{:S(2)}) collective-permute-start(f32[8,32,288]{2,1,0:T(8,128)S(1)} %get-tuple-element.39), channel_id=1, source_target_pairs={{1,0},{2,1},{3,2},{4,3},{5,4},{6,5},{7,6},{8,7},{9,8},{10,9},{11,1... | collective-permute-start | bytes 884744 | tf_op jit(solution)/shard_map/ppermute | solution.py:17
  46.2 7.4 %collective-permute-start.6 = (f32[8,32,288]{2,1,0:T(8,128)S(1)}, f32[8,32,288]{2,1,0:T(8,128)S(1)}, u32[]{:S(2)}, u32[]{:S(2)}) collective-permute-start(f32[8,32,288]{2,1,0:T(8,128)S(1)} %get-tuple-element.38), channel_id=1, source_target_pairs={{0,1},{1,2},{2,3},{3,4},{4,5},{5,6},{6,7},{7,8},{8,9},{9,10},{10,1... | collective-permute-start | bytes 884744 | tf_op jit(solution)/shard_map/ppermute | solution.py:17
  53.7 0.5 convolution_add_fusion.3
  54.2 0.5 convolution_add_fusion.2
  54.8 0.7 fusion.8
  55.5 0.6 fusion.49
  56.1 3.9 %collective-permute-done.7 = f32[8,32,288]{2,1,0:T(8,128)S(1)} collective-permute-done((f32[8,32,288]{2,1,0:T(8,128)S(1)}, f32[8,32,288]{2,1,0:T(8,128)S(1)}, u32[]{:S(2)}, u32[]{:S(2)}) %collective-permute-start.7) | collective-permute-done | bytes 294944 | tf_op jit(solution)/shard_map/ppermute | solution.py:17
  60.1 0.8 fusion.10
  60.8 1.0 collective-permute-done.6
  61.8 0.8 convolution_add_fusion.1
  62.6 0.7 fusion.7
  63.3 0.6 convolution_add_fusion
  64.3 0.1 maximum_bitcast_fusion.1
  64.4 3.2 %collective-permute-start.8 = (f32[3,32,288]{2,1,0:T(8,128)S(1)}, f32[3,32,288]{2,1,0:T(8,128)S(1)}, u32[]{:S(2)}, u32[]{:S(2)}) collective-permute-start(f32[3,32,288]{2,1,0:T(8,128)S(1)} %pad_maximum_fusion.2), channel_id=1, source_target_pairs={{0,32},{32,64},{64,96},{96,128},{128,160},{160,192},{192,224},{224... | collective-permute-start | bytes 331784 | tf_op jit(solution)/shard_map/ppermute | solution.py:17
  67.8 2.4 %collective-permute-start.9 = (f32[3,32,288]{2,1,0:T(8,128)S(1)}, f32[3,32,288]{2,1,0:T(8,128)S(1)}, u32[]{:S(2)}, u32[]{:S(2)}) collective-permute-start(f32[3,32,288]{2,1,0:T(8,128)S(1)} %pad_maximum_fusion.3), channel_id=1, source_target_pairs={{32,0},{64,32},{96,64},{128,96},{160,128},{192,160},{224,192},{256... | collective-permute-start | bytes 331784 | tf_op jit(solution)/shard_map/ppermute | solution.py:17
  70.4 0.5 collective-permute-done.8
  70.9 2.0 %collective-permute-done.9 = f32[3,32,288]{2,1,0:T(8,128)S(1)} collective-permute-done((f32[3,32,288]{2,1,0:T(8,128)S(1)}, f32[3,32,288]{2,1,0:T(8,128)S(1)}, u32[]{:S(2)}, u32[]{:S(2)}) %collective-permute-start.9) | collective-permute-done | bytes 110624 | tf_op jit(solution)/shard_map/ppermute | solution.py:17
  72.9 7.7 %collective-permute-start.10 = (f32[32,288]{1,0:T(8,128)S(1)}, f32[32,288]{1,0:T(8,128)S(1)}, u32[]{:S(2)}, u32[]{:S(2)}) collective-permute-start(f32[32,288]{1,0:T(8,128)S(1)} %get-tuple-element.42), channel_id=1, source_target_pairs={{0,1},{1,2},{2,3},{3,4},{4,5},{5,6},{6,7},{7,8},{8,9},{9,10},{10,1... | collective-permute-start | bytes 110600 | tf_op jit(solution)/shard_map/ppermute | solution.py:17
  80.6 1.9 %collective-permute-start.11 = (f32[32,288]{1,0:T(8,128)S(1)}, f32[32,288]{1,0:T(8,128)S(1)}, u32[]{:S(2)}, u32[]{:S(2)}) collective-permute-start(f32[32,288]{1,0:T(8,128)S(1)} %get-tuple-element.43), channel_id=1, source_target_pairs={{1,0},{2,1},{3,2},{4,3},{5,4},{6,5},{7,6},{8,7},{9,8},{10,9},{11,1... | collective-permute-start | bytes 110600 | tf_op jit(solution)/shard_map/ppermute | solution.py:17
  83.4 6.5 %collective-permute-done.11 = f32[32,288]{1,0:T(8,128)S(1)} collective-permute-done((f32[32,288]{1,0:T(8,128)S(1)}, f32[32,288]{1,0:T(8,128)S(1)}, u32[]{:S(2)}, u32[]{:S(2)}) %collective-permute-start.11) | collective-permute-done | bytes 36896 | tf_op jit(solution)/shard_map/ppermute | solution.py:17
  89.9 2.4 %collective-permute-start.12 = (f32[1,33,288]{2,1,0:T(8,128)S(1)}, f32[1,33,288]{2,1,0:T(8,128)S(1)}, u32[]{:S(2)}, u32[]{:S(2)}) collective-permute-start(f32[1,33,288]{2,1,0:T(8,128)S(1)} %pad_bitcast_fusion), channel_id=1, source_target_pairs={{0,32},{32,0},{64,96},{96,64},{128,160},{160,128},{192,224},{224,1... | collective-permute-start | bytes 114056 | tf_op jit(solution)/shard_map/ppermute | solution.py:162
  92.3 0.9 collective-permute-done.12
  93.2 8.2 %collective-permute-start.13 = (f32[2,33,288]{2,1,0:T(8,128)S(1)}, f32[2,33,288]{2,1,0:T(8,128)S(1)}, u32[]{:S(2)}, u32[]{:S(2)}) collective-permute-start(f32[2,33,288]{2,1,0:T(8,128)S(1)} %pad_maximum_fusion.4), channel_id=1, source_target_pairs={{0,64},{32,96},{64,0},{96,32},{128,192},{160,224},{192,128},{224,1... | collective-permute-start | bytes 228104 | tf_op jit(solution)/shard_map/ppermute | solution.py:162
  101.5 0.5 slice.1098
  104.6 0.7 collective-permute-done.13
  105.3 0.6 slice.1093
  107.2 0.5 slice.1096
  111.7 0.7 maximum_bitcast_fusion
  (121 shorter events, 3.9 us)
Async XLA Ops:
  0.6 32.1 %copy-start = (f32[2,2,2,32,32]{4,3,2,1,0:T(8,128)S(1)}, f32[2,2,2,32,32]{4,3,2,1,0:T(8,128)}, u32[]{:S(2)}) copy-start(f32[2,2,2,32,32]{4,3,2,1,0:T(8,128)} %param.18) | copy-start | bytes 98308
  0.6 8.5 %copy-start.4 = (f32[2,2,2,32,864]{4,3,2,1,0:T(8,128)S(1)}, f32[2,2,2,32,864]{4,3,2,1,0:T(8,128)}, u32[]{:S(2)}) copy-start(f32[2,2,2,32,864]{4,3,2,1,0:T(8,128)} %param.15) | copy-start | bytes 2654212
  1.7 12.0 %collective-permute-start = (f32[2,2,32,32]{2,3,1,0:T(8,128)S(1)}, f32[2,2,32,32]{2,3,1,0:T(8,128)S(1)}, u32[]{:S(2)}, u32[]{:S(2)}) collective-permute-start(f32[2,2,32,32]{2,3,1,0:T(8,128)S(1)} %bitcast.272), channel_id=1, source_target_pairs={{0,32},{32,64},{64,96},{96,128},{128,160},{160,192},{192,224},{224... | collective-permute-start | bytes 49160 | tf_op jit(solution)/shard_map/ppermute | solution.py:17
  3.7 10.1 %collective-permute-start.1 = (f32[2,2,32,32]{2,3,1,0:T(8,128)S(1)}, f32[2,2,32,32]{2,3,1,0:T(8,128)S(1)}, u32[]{:S(2)}, u32[]{:S(2)}) collective-permute-start(f32[2,2,32,32]{2,3,1,0:T(8,128)S(1)} %bitcast.271), channel_id=1, source_target_pairs={{32,0},{64,32},{96,64},{128,96},{160,128},{192,160},{224,192},{256... | collective-permute-start | bytes 49160 | tf_op jit(solution)/shard_map/ppermute | solution.py:17
  9.3 0.7 copy-start.10
  9.3 0.7 copy-start.11
  9.3 0.7 copy-start.7
  10.7 0.7 copy-start.8
  10.7 0.7 copy-start.9
  13.8 16.2 %copy-start.1 = (f32[1024,288]{0,1:T(8,128)S(1)}, f32[1024,288]{0,1:T(8,128)}, u32[]{:S(2)}) copy-start(f32[1024,288]{0,1:T(8,128)} %copy.36) | copy-start | bytes 3538948
  13.8 16.2 %copy-start.6 = (f32[32,288]{1,0:T(8,128)S(1)}, f32[32,288]{1,0:T(8,128)}, u32[]{:S(2)}) copy-start(f32[32,288]{1,0:T(8,128)} %constant.76.clone) | copy-start | bytes 110596
  13.9 8.4 %collective-permute-start.2 = (f32[8,32,32]{1,2,0:T(8,128)S(1)}, f32[8,32,32]{1,2,0:T(8,128)S(1)}, u32[]{:S(2)}, u32[]{:S(2)}) collective-permute-start(f32[8,32,32]{1,2,0:T(8,128)S(1)} %constant_dynamic-update-slice_fusion.8), channel_id=1, source_target_pairs={{0,1},{1,2},{2,3},{3,4},{4,5},{5,6},{6,7},{7,8},{8,9},{9,10},{10,1... | collective-permute-start | bytes 98312 | tf_op jit(solution)/shard_map/ppermute | solution.py:17
  18.7 11.1 %collective-permute-start.3 = (f32[8,32,32]{1,2,0:T(8,128)S(1)}, f32[8,32,32]{1,2,0:T(8,128)S(1)}, u32[]{:S(2)}, u32[]{:S(2)}) collective-permute-start(f32[8,32,32]{1,2,0:T(8,128)S(1)} %get-tuple-element.144), channel_id=1, source_target_pairs={{1,0},{2,1},{3,2},{4,3},{5,4},{6,5},{7,6},{8,7},{9,8},{10,9},{11,1... | collective-permute-start | bytes 98312 | tf_op jit(solution)/shard_map/ppermute | solution.py:17
  32.5 0.9 copy-start.2
  34.6 6.5 %copy-start.3 = (pred[288,288]{1,0:T(32,128)(4,1)S(1)}, pred[288,288]{1,0:T(32,128)(4,1)}, u32[]{:S(2)}) copy-start(pred[288,288]{1,0:T(32,128)(4,1)} %constant.84.clone) | copy-start | bytes 248836
  35.1 7.0 %collective-permute-start.4 = (f32[4,32,288]{2,1,0:T(8,128)S(1)}, f32[4,32,288]{2,1,0:T(8,128)S(1)}, u32[]{:S(2)}, u32[]{:S(2)}) collective-permute-start(f32[4,32,288]{2,1,0:T(8,128)S(1)} %pad_maximum_fusion), channel_id=1, source_target_pairs={{0,32},{32,64},{64,96},{96,128},{128,160},{160,192},{192,224},{224... | collective-permute-start | bytes 442376 | tf_op jit(solution)/shard_map/ppermute | solution.py:17
  37.5 6.8 %collective-permute-start.5 = (f32[4,32,288]{2,1,0:T(8,128)S(1)}, f32[4,32,288]{2,1,0:T(8,128)S(1)}, u32[]{:S(2)}, u32[]{:S(2)}) collective-permute-start(f32[4,32,288]{2,1,0:T(8,128)S(1)} %pad_maximum_fusion.1), channel_id=1, source_target_pairs={{32,0},{64,32},{96,64},{128,96},{160,128},{192,160},{224,192},{256... | collective-permute-start | bytes 442376 | tf_op jit(solution)/shard_map/ppermute | solution.py:17
  44.3 15.7 %collective-permute-start.7 = (f32[8,32,288]{2,1,0:T(8,128)S(1)}, f32[8,32,288]{2,1,0:T(8,128)S(1)}, u32[]{:S(2)}, u32[]{:S(2)}) collective-permute-start(f32[8,32,288]{2,1,0:T(8,128)S(1)} %get-tuple-element.39), channel_id=1, source_target_pairs={{1,0},{2,1},{3,2},{4,3},{5,4},{6,5},{7,6},{8,7},{9,8},{10,9},{11,1... | collective-permute-start | bytes 884744 | tf_op jit(solution)/shard_map/ppermute | solution.py:17
  46.2 15.6 %collective-permute-start.6 = (f32[8,32,288]{2,1,0:T(8,128)S(1)}, f32[8,32,288]{2,1,0:T(8,128)S(1)}, u32[]{:S(2)}, u32[]{:S(2)}) collective-permute-start(f32[8,32,288]{2,1,0:T(8,128)S(1)} %get-tuple-element.38), channel_id=1, source_target_pairs={{0,1},{1,2},{2,3},{3,4},{4,5},{5,6},{6,7},{7,8},{8,9},{9,10},{10,1... | collective-permute-start | bytes 884744 | tf_op jit(solution)/shard_map/ppermute | solution.py:17
  64.2 18.4 %copy-start.12 = (s32[1,1,9]{2,1,0:T(1,128)S(1)}, s32[1,1,9]{2,1,0:T(1,128)}, u32[]{:S(2)}) copy-start(s32[1,1,9]{2,1,0:T(1,128)} %param.19) | copy-start | bytes 112
  64.4 6.5 %collective-permute-start.8 = (f32[3,32,288]{2,1,0:T(8,128)S(1)}, f32[3,32,288]{2,1,0:T(8,128)S(1)}, u32[]{:S(2)}, u32[]{:S(2)}) collective-permute-start(f32[3,32,288]{2,1,0:T(8,128)S(1)} %pad_maximum_fusion.2), channel_id=1, source_target_pairs={{0,32},{32,64},{64,96},{96,128},{128,160},{160,192},{192,224},{224... | collective-permute-start | bytes 331784 | tf_op jit(solution)/shard_map/ppermute | solution.py:17
  67.8 5.0 %collective-permute-start.9 = (f32[3,32,288]{2,1,0:T(8,128)S(1)}, f32[3,32,288]{2,1,0:T(8,128)S(1)}, u32[]{:S(2)}, u32[]{:S(2)}) collective-permute-start(f32[3,32,288]{2,1,0:T(8,128)S(1)} %pad_maximum_fusion.3), channel_id=1, source_target_pairs={{32,0},{64,32},{96,64},{128,96},{160,128},{192,160},{224,192},{256... | collective-permute-start | bytes 331784 | tf_op jit(solution)/shard_map/ppermute | solution.py:17
  72.9 10.5 %collective-permute-start.10 = (f32[32,288]{1,0:T(8,128)S(1)}, f32[32,288]{1,0:T(8,128)S(1)}, u32[]{:S(2)}, u32[]{:S(2)}) collective-permute-start(f32[32,288]{1,0:T(8,128)S(1)} %get-tuple-element.42), channel_id=1, source_target_pairs={{0,1},{1,2},{2,3},{3,4},{4,5},{5,6},{6,7},{7,8},{8,9},{9,10},{10,1... | collective-permute-start | bytes 110600 | tf_op jit(solution)/shard_map/ppermute | solution.py:17
  80.6 9.3 %collective-permute-start.11 = (f32[32,288]{1,0:T(8,128)S(1)}, f32[32,288]{1,0:T(8,128)S(1)}, u32[]{:S(2)}, u32[]{:S(2)}) collective-permute-start(f32[32,288]{1,0:T(8,128)S(1)} %get-tuple-element.43), channel_id=1, source_target_pairs={{1,0},{2,1},{3,2},{4,3},{5,4},{6,5},{7,6},{8,7},{9,8},{10,9},{11,1... | collective-permute-start | bytes 110600 | tf_op jit(solution)/shard_map/ppermute | solution.py:17
  89.9 22.5 %copy-start.5 = (f32[32,288]{1,0:T(8,128)}, f32[32,288]{1,0:T(8,128)S(1)}, u32[]{:S(2)}) copy-start(f32[32,288]{1,0:T(8,128)S(1)} %fusion.26) | copy-start | bytes 110596
  89.9 3.3 %collective-permute-start.12 = (f32[1,33,288]{2,1,0:T(8,128)S(1)}, f32[1,33,288]{2,1,0:T(8,128)S(1)}, u32[]{:S(2)}, u32[]{:S(2)}) collective-permute-start(f32[1,33,288]{2,1,0:T(8,128)S(1)} %pad_bitcast_fusion), channel_id=1, source_target_pairs={{0,32},{32,0},{64,96},{96,64},{128,160},{160,128},{192,224},{224,1... | collective-permute-start | bytes 114056 | tf_op jit(solution)/shard_map/ppermute | solution.py:162
  93.2 12.0 %collective-permute-start.13 = (f32[2,33,288]{2,1,0:T(8,128)S(1)}, f32[2,33,288]{2,1,0:T(8,128)S(1)}, u32[]{:S(2)}, u32[]{:S(2)}) collective-permute-start(f32[2,33,288]{2,1,0:T(8,128)S(1)} %pad_maximum_fusion.4), channel_id=1, source_target_pairs={{0,64},{32,96},{64,0},{96,32},{128,192},{160,224},{192,128},{224,1... | collective-permute-start | bytes 228104 | tf_op jit(solution)/shard_map/ppermute | solution.py:162

commit v7 on v4

--- a/solution.py
+++ b/solution.py
@@ -70,20 +70,38 @@
     tent = {}
     for cell in CELLS:
         tent[(cell[0] + 1, cell[1] + 1, cell[2])] = tentative[cell]
+    count_x, count_y = lax.axis_size("gx"), lax.axis_size("gy")
+
+    def from_neighbour(block, step_x, step_y):
+        pairs = []
+        for source_x in range(count_x):
+            for source_y in range(count_y):
+                target_x, target_y = source_x + step_x, source_y + step_y
+                if 0 <= target_x < count_x and 0 <= target_y < count_y:
+                    pairs.append((source_x * count_y + source_y, target_x * count_y + target_y))
+        return lax.ppermute(block, ("gx", "gy"), pairs)
+
     left = shift(tentative[1], "gx", True)
     right = shift(tentative[0], "gx", False)
+    low = shift(tentative[:, 1], "gy", True)
+    high = shift(tentative[:, 0], "gy", False)
+    corners = {
+        (0, 0): from_neighbour(tentative[1, 1], 1, 1),
+        (0, 3): from_neighbour(tentative[1, 0], 1, -1),
+        (3, 0): from_neighbour(tentative[0, 1], -1, 1),
+        (3, 3): from_neighbour(tentative[0, 0], -1, -1),
+    }
     for cell_y in range(2):
         for cell_z in range(2):
             tent[(0, cell_y + 1, cell_z)] = left[cell_y, cell_z]
             tent[(3, cell_y + 1, cell_z)] = right[cell_y, cell_z]
-    send_high = jnp.stack([tent[(pos_x, 2, pos_z)] for pos_x in range(4) for pos_z in range(2)])
-    send_low = jnp.stack([tent[(pos_x, 1, pos_z)] for pos_x in range(4) for pos_z in range(2)])
-    low = shift(send_high, "gy", True)
-    high = shift(send_low, "gy", False)
-    for pos_x in range(4):
-        for pos_z in range(2):
-            tent[(pos_x, 0, pos_z)] = low[2 * pos_x + pos_z]
-            tent[(pos_x, 3, pos_z)] = high[2 * pos_x + pos_z]
+    for cell_x in range(2):
+        for cell_z in range(2):
+            tent[(cell_x + 1, 0, cell_z)] = low[cell_x, cell_z]
+            tent[(cell_x + 1, 3, cell_z)] = high[cell_x, cell_z]
+    for (pos_x, pos_y), block in corners.items():
+        for cell_z in range(2):
+            tent[(pos_x, pos_y, cell_z)] = block[cell_z]
 
     tent_frame = jnp.concatenate([tent[pos] for pos in POSITIONS], axis=0)
     reach_x = np.array([REACH[pos[0]] - 1 for pos in POSITIONS])

time: 109 us -> 128 us (1.17)
  starting transfers between devices: 46.6 us -> 64.8 us
  local copies, waits for them, and re-layouts: 10.6 us -> 15 us
  waiting for transfers between devices: 29.9 us -> 27.2 us
    ppermute x0 -> x4, starting transfers between devices: none -> 15.3 us  [from_neighbour(): return lax.ppermute(block, ('gx', 'gy'), pairs)]
    ppermute x12, waiting for transfers between devices: 26.5 us -> 22.2 us  [shift(): return lax.ppermute(block, axis, pairs)]
    ppermute x12, starting transfers between devices: 42.8 us -> 45.7 us  [shift(): return lax.ppermute(block, axis, pairs)]
    unnamed x63 -> x60, local copies, waits for them, and re-layouts: 1.74 us -> 3.77 us
    slice x0 -> x2, local copies, waits for them, and re-layouts: none -> 1.71 us  [the longest x1 0.89 us: local(): high = shift(tentative[:, 0], 'gy', False)]
    ppermute x0 -> x4, waiting for transfers between devices: none -> 1.57 us  [from_neighbour(): return lax.ppermute(block, ('gx', 'gy'), pairs)]
    squeeze x2 -> x6, local copies, waits for them, and re-layouts: 0.02 us -> 1.5 us  [the longest x4 1.49 us: local(): tent[pos_x, pos_y, cell_z] = block[cell_z]]
  transfers between devices with their start and end apart: 14 -> 18, of which waited for: 10 -> 10; matrix products, arithmetic and copies ran while one was open for 9% -> 11% of each run, Pallas kernels for 0% -> 0%
where the time goes in v7:
time: 128 us; the launch traced here: 127 us
  starting transfers between devices  64.8 us (51%)
  waiting for transfers between devices  27.2 us (21%)
  local copies, waits for them, and re-layouts  15 us (12%)
  between operations  9.88 us (8%)
  matrix products  9.05 us (7%)
    ppermute x12, starting transfers between devices, shift(): return lax.ppermute(block, axis, pairs)  45.7 us
    ppermute x12, waiting for transfers between devices, shift(): return lax.ppermute(block, axis, pairs)  22.2 us
    ppermute x4, starting transfers between devices, from_neighbour(): return lax.ppermute(block, ('gx', 'gy'), pairs)  15.3 us
    ppermute x2, starting transfers between devices, local(): lax.ppermute(held, 'gx', [(i, i ^ 1 << level) for i in range(count)])  3.84 us
    unnamed x60, local copies, waits for them, and re-layouts  3.77 us
    ppermute x2, waiting for transfers between devices, local(): lax.ppermute(held, 'gx', [(i, i ^ 1 << level) for i in range(count)])  3.45 us
    dot_general x5, matrix products, local(): jnp.dot(stencil_pos[:, first:last], part.reshape(len(group) * width, -1),...  3.1 us
  transfers between devices with their start and end apart: 18, of which 10 were waited for; matrix products, arithmetic and copies ran while one was open for 11% of the time, Pallas kernels for 0%

profile of v7, /device:TPU:288, one launch (start us, length us, event | category | flops | bytes accessed | tf_op | source)
XLA Modules:
  0.0 127.2 jit_solution(1896309142342310365)
XLA Ops:
  0.7 1.0 fusion.36
  1.7 1.9 %collective-permute-start = (f32[2,2,32,32]{2,3,1,0:T(8,128)S(1)}, f32[2,2,32,32]{2,3,1,0:T(8,128)S(1)}, u32[]{:S(2)}, u32[]{:S(2)}) collective-permute-start(f32[2,2,32,32]{2,3,1,0:T(8,128)S(1)} %bitcast.245), channel_id=1, source_target_pairs={{0,32},{32,64},{64,96},{96,128},{128,160},{160,192},{192,224},{224... | collective-permute-start | bytes 49160 | tf_op jit(solution)/shard_map/ppermute | solution.py:17
  3.8 4.9 %collective-permute-start.1 = (f32[2,2,32,32]{2,3,1,0:T(8,128)S(1)}, f32[2,2,32,32]{2,3,1,0:T(8,128)S(1)}, u32[]{:S(2)}, u32[]{:S(2)}) collective-permute-start(f32[2,2,32,32]{2,3,1,0:T(8,128)S(1)} %bitcast.244), channel_id=1, source_target_pairs={{32,0},{64,32},{96,64},{128,96},{160,128},{192,160},{224,192},{256... | collective-permute-start | bytes 49160 | tf_op jit(solution)/shard_map/ppermute | solution.py:17
  8.6 0.8 fusion.34
  9.4 0.7 copy.109
  10.1 1.9 %collective-permute-start.2 = (f32[2,32,32]{1,2,0:T(8,128)}, f32[2,32,32]{1,2,0:T(8,128)}, u32[]{:S(2)}, u32[]{:S(2)}) collective-permute-start(f32[2,32,32]{1,2,0:T(8,128)} %bitcast.28), channel_id=1, source_target_pairs={{0,33},{1,34},{2,35},{3,36},{4,37},{5,38},{6,39},{7,40},{8,41},{9,... | collective-permute-start | bytes 24584 | tf_op jit(solution)/shard_map/ppermute | solution.py:82
  12.0 0.9 fusion.35
  12.9 0.7 copy.110
  13.7 3.4 %collective-permute-start.3 = (f32[2,2,32,32]{2,3,1,0:T(8,128)}, f32[2,2,32,32]{2,3,1,0:T(8,128)S(1)}, u32[]{:S(2)}, u32[]{:S(2)}) collective-permute-start(f32[2,2,32,32]{2,3,1,0:T(8,128)} %bitcast.31), channel_id=1, source_target_pairs={{0,1},{1,2},{2,3},{3,4},{4,5},{5,6},{6,7},{7,8},{8,9},{9,10},{10,1... | collective-permute-start | bytes 49160 | tf_op jit(solution)/shard_map/ppermute | solution.py:17
  17.0 0.7 copy.111
  17.7 6.1 %collective-permute-start.4 = (f32[2,32,32]{1,2,0:T(8,128)}, f32[2,32,32]{1,2,0:T(8,128)}, u32[]{:S(2)}, u32[]{:S(2)}) collective-permute-start(f32[2,32,32]{1,2,0:T(8,128)} %bitcast.36), channel_id=1, source_target_pairs={{32,1},{33,2},{34,3},{35,4},{36,5},{37,6},{38,7},{39,8},{40,9},{41... | collective-permute-start | bytes 24584 | tf_op jit(solution)/shard_map/ppermute | solution.py:82
  24.0 0.1 mul.55
  24.4 0.1 fusion.44
  24.7 0.3 copy-done.11
  25.2 0.1 fusion.42
  25.5 0.1 fusion.40
  25.9 0.1 fusion.38
  26.1 0.1 concatenate.84
  26.2 0.2 copy-done.9
  26.6 1.5 %copy.79 = f32[1024,288]{0,1:T(8,128)} copy(f32[1024,288]{1,0:T(8,128)S(1)} %bitcast.222) | data formatting | bytes 2359296 | tf_op jit(solution)/shard_map/reshape | solution.py:111
  29.0 2.7 %collective-permute-start.5 = (f32[2,32,32]{1,2,0:T(8,128)S(1)}, f32[2,32,32]{1,2,0:T(8,128)S(1)}, u32[]{:S(2)}, u32[]{:S(2)}) collective-permute-start(f32[2,32,32]{1,2,0:T(8,128)S(1)} %bitcast.248), channel_id=1, source_target_pairs={{1,32},{2,33},{3,34},{4,35},{5,36},{6,37},{7,38},{8,39},{9,40},{10... | collective-permute-start | bytes 24584 | tf_op jit(solution)/shard_map/ppermute | solution.py:82
  31.7 0.7 slice_bitcast_fusion.39
  32.5 5.2 %collective-permute-start.6 = (f32[2,2,32,32]{2,3,1,0:T(8,128)S(1)}, f32[2,2,32,32]{2,3,1,0:T(8,128)S(1)}, u32[]{:S(2)}, u32[]{:S(2)}) collective-permute-start(f32[2,2,32,32]{2,3,1,0:T(8,128)S(1)} %bitcast.246), channel_id=1, source_target_pairs={{1,0},{2,1},{3,2},{4,3},{5,4},{6,5},{7,6},{8,7},{9,8},{10,9},{11,1... | collective-permute-start | bytes 49160 | tf_op jit(solution)/shard_map/ppermute | solution.py:17
  37.7 0.7 slice_bitcast_fusion.33
  38.5 4.5 %collective-permute-start.7 = (f32[2,32,32]{1,2,0:T(8,128)S(1)}, f32[2,32,32]{1,2,0:T(8,128)S(1)}, u32[]{:S(2)}, u32[]{:S(2)}) collective-permute-start(f32[2,32,32]{1,2,0:T(8,128)S(1)} %bitcast.247), channel_id=1, source_target_pairs={{33,0},{34,1},{35,2},{36,3},{37,4},{38,5},{39,6},{40,7},{41,8},{42... | collective-permute-start | bytes 24584 | tf_op jit(solution)/shard_map/ppermute | solution.py:82
  43.0 1.6 %collective-permute-done.7 = f32[2,32,32]{1,2,0:T(8,128)S(1)} collective-permute-done((f32[2,32,32]{1,2,0:T(8,128)S(1)}, f32[2,32,32]{1,2,0:T(8,128)S(1)}, u32[]{:S(2)}, u32[]{:S(2)}) %collective-permute-start.7) | collective-permute-done | bytes 8224 | tf_op jit(solution)/shard_map/ppermute | solution.py:82
  44.6 0.2 concatenate.87
  44.8 1.1 convolution_multiply_fusion
  46.0 1.8 %fusion.46 = f32[256,288]{1,0:T(8,128)S(1)} fusion(f32[256,1024]{1,0:T(8,128)S(1)} %constant_dynamic-update-slice_fusion, f32[1024,288]{0,1:T(8,128)S(1)} %convolution_multiply_fusion), kind=kOutput, calls=%fused_computation.147 | convolution fusion | flops 905969664 | bytes 2523136 | tf_op jit(solution)/shard_map/dot_general | solution.py:113
  47.8 0.5 convolution_multiply_fusion.1
  48.3 0.1 copy.81
  48.5 0.4 fusion.2
  48.9 0.3 slice_bitcast_fusion.1
  49.7 4.4 %collective-permute-start.8 = (f32[4,32,288]{2,1,0:T(8,128)S(1)}, f32[4,32,288]{2,1,0:T(8,128)S(1)}, u32[]{:S(2)}, u32[]{:S(2)}) collective-permute-start(f32[4,32,288]{2,1,0:T(8,128)S(1)} %pad_maximum_fusion), channel_id=1, source_target_pairs={{0,32},{32,64},{64,96},{96,128},{128,160},{160,192},{192,224},{224... | collective-permute-start | bytes 442376 | tf_op jit(solution)/shard_map/ppermute | solution.py:17
  54.5 3.5 %collective-permute-start.9 = (f32[4,32,288]{2,1,0:T(8,128)S(1)}, f32[4,32,288]{2,1,0:T(8,128)S(1)}, u32[]{:S(2)}, u32[]{:S(2)}) collective-permute-start(f32[4,32,288]{2,1,0:T(8,128)S(1)} %pad_maximum_fusion.1), channel_id=1, source_target_pairs={{32,0},{64,32},{96,64},{128,96},{160,128},{192,160},{224,192},{256... | collective-permute-start | bytes 442376 | tf_op jit(solution)/shard_map/ppermute | solution.py:17
  58.0 0.4 fusion.10
  58.4 0.4 collective-permute-done.8
  58.9 2.2 %collective-permute-done.9 = f32[4,32,288]{2,1,0:T(8,128)S(1)} collective-permute-done((f32[4,32,288]{2,1,0:T(8,128)S(1)}, f32[4,32,288]{2,1,0:T(8,128)S(1)}, u32[]{:S(2)}, u32[]{:S(2)}) %collective-permute-start.9) | collective-permute-done | bytes 147488 | tf_op jit(solution)/shard_map/ppermute | solution.py:17
  61.2 8.9 %collective-permute-start.11 = (f32[8,32,288]{2,1,0:T(8,128)S(1)}, f32[8,32,288]{2,1,0:T(8,128)S(1)}, u32[]{:S(2)}, u32[]{:S(2)}) collective-permute-start(f32[8,32,288]{2,1,0:T(8,128)S(1)} %get-tuple-element.39), channel_id=1, source_target_pairs={{1,0},{2,1},{3,2},{4,3},{5,4},{6,5},{7,6},{8,7},{9,8},{10,9},{11,1... | collective-permute-start | bytes 884744 | tf_op jit(solution)/shard_map/ppermute | solution.py:17
  70.1 0.7 fusion.5
  70.9 2.1 %collective-permute-start.10 = (f32[8,32,288]{2,1,0:T(8,128)S(1)}, f32[8,32,288]{2,1,0:T(8,128)S(1)}, u32[]{:S(2)}, u32[]{:S(2)}) collective-permute-start(f32[8,32,288]{2,1,0:T(8,128)S(1)} %get-tuple-element.38), channel_id=1, source_target_pairs={{0,1},{1,2},{2,3},{3,4},{4,5},{5,6},{6,7},{7,8},{8,9},{9,10},{10,1... | collective-permute-start | bytes 884744 | tf_op jit(solution)/shard_map/ppermute | solution.py:17
  73.0 0.5 convolution_add_fusion.1
  73.5 2.1 %collective-permute-done.11 = f32[8,32,288]{2,1,0:T(8,128)S(1)} collective-permute-done((f32[8,32,288]{2,1,0:T(8,128)S(1)}, f32[8,32,288]{2,1,0:T(8,128)S(1)}, u32[]{:S(2)}, u32[]{:S(2)}) %collective-permute-start.11) | collective-permute-done | bytes 294944 | tf_op jit(solution)/shard_map/ppermute | solution.py:17
  75.7 0.8 fusion.6
  76.5 7.4 %collective-permute-done.10 = f32[8,32,288]{2,1,0:T(8,128)S(1)} collective-permute-done((f32[8,32,288]{2,1,0:T(8,128)S(1)}, f32[8,32,288]{2,1,0:T(8,128)S(1)}, u32[]{:S(2)}, u32[]{:S(2)}) %collective-permute-start.10) | collective-permute-done | bytes 294944 | tf_op jit(solution)/shard_map/ppermute | solution.py:17
  83.9 0.8 fusion.8
  84.6 0.6 fusion.3
  85.2 0.7 fusion.4
  85.9 0.6 fusion.47
  87.1 3.7 %collective-permute-start.13 = (f32[3,32,288]{2,1,0:T(8,128)S(1)}, f32[3,32,288]{2,1,0:T(8,128)S(1)}, u32[]{:S(2)}, u32[]{:S(2)}) collective-permute-start(f32[3,32,288]{2,1,0:T(8,128)S(1)} %pad_maximum_fusion.3), channel_id=1, source_target_pairs={{32,0},{64,32},{96,64},{128,96},{160,128},{192,160},{224,192},{256... | collective-permute-start | bytes 331784 | tf_op jit(solution)/shard_map/ppermute | solution.py:17
  90.9 1.9 %collective-permute-start.12 = (f32[3,32,288]{2,1,0:T(8,128)S(1)}, f32[3,32,288]{2,1,0:T(8,128)S(1)}, u32[]{:S(2)}, u32[]{:S(2)}) collective-permute-start(f32[3,32,288]{2,1,0:T(8,128)S(1)} %pad_maximum_fusion.2), channel_id=1, source_target_pairs={{0,32},{32,64},{64,96},{96,128},{128,160},{160,192},{192,224},{224... | collective-permute-start | bytes 331784 | tf_op jit(solution)/shard_map/ppermute | solution.py:17
  93.0 0.4 collective-permute-done.13
  93.4 5.1 %collective-permute-done.12 = f32[3,32,288]{2,1,0:T(8,128)S(1)} collective-permute-done((f32[3,32,288]{2,1,0:T(8,128)S(1)}, f32[3,32,288]{2,1,0:T(8,128)S(1)}, u32[]{:S(2)}, u32[]{:S(2)}) %collective-permute-start.12) | collective-permute-done | bytes 110624 | tf_op jit(solution)/shard_map/ppermute | solution.py:17
  98.6 1.9 %collective-permute-start.15 = (f32[32,288]{1,0:T(8,128)S(1)}, f32[32,288]{1,0:T(8,128)S(1)}, u32[]{:S(2)}, u32[]{:S(2)}) collective-permute-start(f32[32,288]{1,0:T(8,128)S(1)} %get-tuple-element.43), channel_id=1, source_target_pairs={{1,0},{2,1},{3,2},{4,3},{5,4},{6,5},{7,6},{8,7},{9,8},{10,9},{11,1... | collective-permute-start | bytes 110600 | tf_op jit(solution)/shard_map/ppermute | solution.py:17
  100.6 3.9 %collective-permute-start.14 = (f32[32,288]{1,0:T(8,128)S(1)}, f32[32,288]{1,0:T(8,128)S(1)}, u32[]{:S(2)}, u32[]{:S(2)}) collective-permute-start(f32[32,288]{1,0:T(8,128)S(1)} %get-tuple-element.42), channel_id=1, source_target_pairs={{0,1},{1,2},{2,3},{3,4},{4,5},{5,6},{6,7},{7,8},{8,9},{9,10},{10,1... | collective-permute-start | bytes 110600 | tf_op jit(solution)/shard_map/ppermute | solution.py:17
  105.3 4.5 %collective-permute-done.14 = f32[32,288]{1,0:T(8,128)S(1)} collective-permute-done((f32[32,288]{1,0:T(8,128)S(1)}, f32[32,288]{1,0:T(8,128)S(1)}, u32[]{:S(2)}, u32[]{:S(2)}) %collective-permute-start.14) | collective-permute-done | bytes 36896 | tf_op jit(solution)/shard_map/ppermute | solution.py:17
  109.9 1.9 %collective-permute-start.16 = (f32[1,33,288]{2,1,0:T(8,128)S(1)}, f32[1,33,288]{2,1,0:T(8,128)S(1)}, u32[]{:S(2)}, u32[]{:S(2)}) collective-permute-start(f32[1,33,288]{2,1,0:T(8,128)S(1)} %pad_bitcast_fusion), channel_id=1, source_target_pairs={{0,32},{32,0},{64,96},{96,64},{128,160},{160,128},{192,224},{224,1... | collective-permute-start | bytes 114056 | tf_op jit(solution)/shard_map/ppermute | solution.py:172
  111.8 1.2 collective-permute-done.16
  113.1 1.9 %collective-permute-start.17 = (f32[2,33,288]{2,1,0:T(8,128)S(1)}, f32[2,33,288]{2,1,0:T(8,128)S(1)}, u32[]{:S(2)}, u32[]{:S(2)}) collective-permute-start(f32[2,33,288]{2,1,0:T(8,128)S(1)} %pad_maximum_fusion.4), channel_id=1, source_target_pairs={{0,64},{32,96},{64,0},{96,32},{128,192},{160,224},{192,128},{224,1... | collective-permute-start | bytes 228104 | tf_op jit(solution)/shard_map/ppermute | solution.py:172
  115.0 0.5 slice.1102
  118.1 2.2 %collective-permute-done.17 = f32[2,33,288]{2,1,0:T(8,128)S(1)} collective-permute-done((f32[2,33,288]{2,1,0:T(8,128)S(1)}, f32[2,33,288]{2,1,0:T(8,128)S(1)}, u32[]{:S(2)}, u32[]{:S(2)}) %collective-permute-start.17) | collective-permute-done | bytes 76064 | tf_op jit(solution)/shard_map/ppermute | solution.py:172
  120.4 0.5 slice.1100
  122.2 0.5 slice.1097
  126.5 0.7 maximum_bitcast_fusion
  (126 shorter events, 4.4 us)
Async XLA Ops:
  0.6 47.2 %copy-start = (f32[2,2,2,32,32]{4,3,2,1,0:T(8,128)S(1)}, f32[2,2,2,32,32]{4,3,2,1,0:T(8,128)}, u32[]{:S(2)}) copy-start(f32[2,2,2,32,32]{4,3,2,1,0:T(8,128)} %param.18) | copy-start | bytes 98308
  0.6 23.2 %copy-start.2 = (f32[2,2,2,32,32]{4,3,2,1,0:T(8,128)S(1)}, f32[2,2,2,32,32]{4,3,2,1,0:T(8,128)}, u32[]{:S(2)}) copy-start(f32[2,2,2,32,32]{4,3,2,1,0:T(8,128)} %param.17) | copy-start | bytes 98308
  0.7 23.3 %copy-start.8 = (s32[2,2,2,27]{3,2,1,0:T(2,128)S(1)}, s32[2,2,2,27]{3,2,1,0:T(2,128)}, u32[]{:S(2)}) copy-start(s32[2,2,2,27]{3,2,1,0:T(2,128)} %param.16) | copy-start | bytes 2596
  0.7 23.5 %copy-start.3 = (f32[2,2,2,32,864]{4,3,2,1,0:T(8,128)S(1)}, f32[2,2,2,32,864]{4,3,2,1,0:T(8,128)}, u32[]{:S(2)}) copy-start(f32[2,2,2,32,864]{4,3,2,1,0:T(8,128)} %param.15) | copy-start | bytes 2654212
  1.7 42.8 %collective-permute-start = (f32[2,2,32,32]{2,3,1,0:T(8,128)S(1)}, f32[2,2,32,32]{2,3,1,0:T(8,128)S(1)}, u32[]{:S(2)}, u32[]{:S(2)}) collective-permute-start(f32[2,2,32,32]{2,3,1,0:T(8,128)S(1)} %bitcast.245), channel_id=1, source_target_pairs={{0,32},{32,64},{64,96},{96,128},{128,160},{160,192},{192,224},{224... | collective-permute-start | bytes 49160 | tf_op jit(solution)/shard_map/ppermute | solution.py:17
  3.8 40.8 %collective-permute-start.1 = (f32[2,2,32,32]{2,3,1,0:T(8,128)S(1)}, f32[2,2,32,32]{2,3,1,0:T(8,128)S(1)}, u32[]{:S(2)}, u32[]{:S(2)}) collective-permute-start(f32[2,2,32,32]{2,3,1,0:T(8,128)S(1)} %bitcast.244), channel_id=1, source_target_pairs={{32,0},{64,32},{96,64},{128,96},{160,128},{192,160},{224,192},{256... | collective-permute-start | bytes 49160 | tf_op jit(solution)/shard_map/ppermute | solution.py:17
  10.1 18.9 %collective-permute-start.2 = (f32[2,32,32]{1,2,0:T(8,128)}, f32[2,32,32]{1,2,0:T(8,128)}, u32[]{:S(2)}, u32[]{:S(2)}) collective-permute-start(f32[2,32,32]{1,2,0:T(8,128)} %bitcast.28), channel_id=1, source_target_pairs={{0,33},{1,34},{2,35},{3,36},{4,37},{5,38},{6,39},{7,40},{8,41},{9,... | collective-permute-start | bytes 24584 | tf_op jit(solution)/shard_map/ppermute | solution.py:82
  13.7 30.9 %collective-permute-start.3 = (f32[2,2,32,32]{2,3,1,0:T(8,128)}, f32[2,2,32,32]{2,3,1,0:T(8,128)S(1)}, u32[]{:S(2)}, u32[]{:S(2)}) collective-permute-start(f32[2,2,32,32]{2,3,1,0:T(8,128)} %bitcast.31), channel_id=1, source_target_pairs={{0,1},{1,2},{2,3},{3,4},{4,5},{5,6},{6,7},{7,8},{8,9},{9,10},{10,1... | collective-permute-start | bytes 49160 | tf_op jit(solution)/shard_map/ppermute | solution.py:17
  17.7 14.8 %collective-permute-start.4 = (f32[2,32,32]{1,2,0:T(8,128)}, f32[2,32,32]{1,2,0:T(8,128)}, u32[]{:S(2)}, u32[]{:S(2)}) collective-permute-start(f32[2,32,32]{1,2,0:T(8,128)} %bitcast.36), channel_id=1, source_target_pairs={{32,1},{33,2},{34,3},{35,4},{36,5},{37,6},{38,7},{39,8},{40,9},{41... | collective-permute-start | bytes 24584 | tf_op jit(solution)/shard_map/ppermute | solution.py:82
  24.3 0.7 copy-start.11
  24.3 0.7 copy-start.12
  24.3 0.7 copy-start.7
  25.7 0.7 copy-start.9
  25.7 0.7 copy-start.10
  28.1 16.7 %copy-start.1 = (f32[1024,288]{0,1:T(8,128)S(1)}, f32[1024,288]{0,1:T(8,128)}, u32[]{:S(2)}) copy-start(f32[1024,288]{0,1:T(8,128)} %copy.79) | copy-start | bytes 3538948
  28.1 16.7 %copy-start.6 = (f32[32,288]{1,0:T(8,128)S(1)}, f32[32,288]{1,0:T(8,128)}, u32[]{:S(2)}) copy-start(f32[32,288]{1,0:T(8,128)} %constant.76.clone) | copy-start | bytes 110596
  29.0 9.5 %collective-permute-start.5 = (f32[2,32,32]{1,2,0:T(8,128)S(1)}, f32[2,32,32]{1,2,0:T(8,128)S(1)}, u32[]{:S(2)}, u32[]{:S(2)}) collective-permute-start(f32[2,32,32]{1,2,0:T(8,128)S(1)} %bitcast.248), channel_id=1, source_target_pairs={{1,32},{2,33},{3,34},{4,35},{5,36},{6,37},{7,38},{8,39},{9,40},{10... | collective-permute-start | bytes 24584 | tf_op jit(solution)/shard_map/ppermute | solution.py:82
  32.5 12.1 %collective-permute-start.6 = (f32[2,2,32,32]{2,3,1,0:T(8,128)S(1)}, f32[2,2,32,32]{2,3,1,0:T(8,128)S(1)}, u32[]{:S(2)}, u32[]{:S(2)}) collective-permute-start(f32[2,2,32,32]{2,3,1,0:T(8,128)S(1)} %bitcast.246), channel_id=1, source_target_pairs={{1,0},{2,1},{3,2},{4,3},{5,4},{6,5},{7,6},{8,7},{9,8},{10,9},{11,1... | collective-permute-start | bytes 49160 | tf_op jit(solution)/shard_map/ppermute | solution.py:17
  38.5 6.1 %collective-permute-start.7 = (f32[2,32,32]{1,2,0:T(8,128)S(1)}, f32[2,32,32]{1,2,0:T(8,128)S(1)}, u32[]{:S(2)}, u32[]{:S(2)}) collective-permute-start(f32[2,32,32]{1,2,0:T(8,128)S(1)} %bitcast.247), channel_id=1, source_target_pairs={{33,0},{34,1},{35,2},{36,3},{37,4},{38,5},{39,6},{40,7},{41,8},{42... | collective-permute-start | bytes 24584 | tf_op jit(solution)/shard_map/ppermute | solution.py:82
  49.7 9.1 %collective-permute-start.8 = (f32[4,32,288]{2,1,0:T(8,128)S(1)}, f32[4,32,288]{2,1,0:T(8,128)S(1)}, u32[]{:S(2)}, u32[]{:S(2)}) collective-permute-start(f32[4,32,288]{2,1,0:T(8,128)S(1)} %pad_maximum_fusion), channel_id=1, source_target_pairs={{0,32},{32,64},{64,96},{96,128},{128,160},{160,192},{192,224},{224... | collective-permute-start | bytes 442376 | tf_op jit(solution)/shard_map/ppermute | solution.py:17
  54.5 15.6 %copy-start.5 = (pred[288,288]{1,0:T(32,128)(4,1)S(1)}, pred[288,288]{1,0:T(32,128)(4,1)}, u32[]{:S(2)}) copy-start(pred[288,288]{1,0:T(32,128)(4,1)} %constant.84.clone) | copy-start | bytes 248836
  54.5 6.7 %collective-permute-start.9 = (f32[4,32,288]{2,1,0:T(8,128)S(1)}, f32[4,32,288]{2,1,0:T(8,128)S(1)}, u32[]{:S(2)}, u32[]{:S(2)}) collective-permute-start(f32[4,32,288]{2,1,0:T(8,128)S(1)} %pad_maximum_fusion.1), channel_id=1, source_target_pairs={{32,0},{64,32},{96,64},{128,96},{160,128},{192,160},{224,192},{256... | collective-permute-start | bytes 442376 | tf_op jit(solution)/shard_map/ppermute | solution.py:17
  61.2 14.5 %collective-permute-start.11 = (f32[8,32,288]{2,1,0:T(8,128)S(1)}, f32[8,32,288]{2,1,0:T(8,128)S(1)}, u32[]{:S(2)}, u32[]{:S(2)}) collective-permute-start(f32[8,32,288]{2,1,0:T(8,128)S(1)} %get-tuple-element.39), channel_id=1, source_target_pairs={{1,0},{2,1},{3,2},{4,3},{5,4},{6,5},{7,6},{8,7},{9,8},{10,9},{11,1... | collective-permute-start | bytes 884744 | tf_op jit(solution)/shard_map/ppermute | solution.py:17
  70.9 13.0 %collective-permute-start.10 = (f32[8,32,288]{2,1,0:T(8,128)S(1)}, f32[8,32,288]{2,1,0:T(8,128)S(1)}, u32[]{:S(2)}, u32[]{:S(2)}) collective-permute-start(f32[8,32,288]{2,1,0:T(8,128)S(1)} %get-tuple-element.38), channel_id=1, source_target_pairs={{0,1},{1,2},{2,3},{3,4},{4,5},{5,6},{6,7},{7,8},{8,9},{9,10},{10,1... | collective-permute-start | bytes 884744 | tf_op jit(solution)/shard_map/ppermute | solution.py:17
  86.9 17.6 %copy-start.13 = (s32[1,1,9]{2,1,0:T(1,128)S(1)}, s32[1,1,9]{2,1,0:T(1,128)}, u32[]{:S(2)}) copy-start(s32[1,1,9]{2,1,0:T(1,128)} %param.19) | copy-start | bytes 112
  87.1 6.4 %collective-permute-start.13 = (f32[3,32,288]{2,1,0:T(8,128)S(1)}, f32[3,32,288]{2,1,0:T(8,128)S(1)}, u32[]{:S(2)}, u32[]{:S(2)}) collective-permute-start(f32[3,32,288]{2,1,0:T(8,128)S(1)} %pad_maximum_fusion.3), channel_id=1, source_target_pairs={{32,0},{64,32},{96,64},{128,96},{160,128},{192,160},{224,192},{256... | collective-permute-start | bytes 331784 | tf_op jit(solution)/shard_map/ppermute | solution.py:17
  90.9 7.7 %collective-permute-start.12 = (f32[3,32,288]{2,1,0:T(8,128)S(1)}, f32[3,32,288]{2,1,0:T(8,128)S(1)}, u32[]{:S(2)}, u32[]{:S(2)}) collective-permute-start(f32[3,32,288]{2,1,0:T(8,128)S(1)} %pad_maximum_fusion.2), channel_id=1, source_target_pairs={{0,32},{32,64},{64,96},{96,128},{128,160},{160,192},{192,224},{224... | collective-permute-start | bytes 331784 | tf_op jit(solution)/shard_map/ppermute | solution.py:17
  98.6 6.7 %collective-permute-start.15 = (f32[32,288]{1,0:T(8,128)S(1)}, f32[32,288]{1,0:T(8,128)S(1)}, u32[]{:S(2)}, u32[]{:S(2)}) collective-permute-start(f32[32,288]{1,0:T(8,128)S(1)} %get-tuple-element.43), channel_id=1, source_target_pairs={{1,0},{2,1},{3,2},{4,3},{5,4},{6,5},{7,6},{8,7},{9,8},{10,9},{11,1... | collective-permute-start | bytes 110600 | tf_op jit(solution)/shard_map/ppermute | solution.py:17
  100.6 9.3 %collective-permute-start.14 = (f32[32,288]{1,0:T(8,128)S(1)}, f32[32,288]{1,0:T(8,128)S(1)}, u32[]{:S(2)}, u32[]{:S(2)}) collective-permute-start(f32[32,288]{1,0:T(8,128)S(1)} %get-tuple-element.42), channel_id=1, source_target_pairs={{0,1},{1,2},{2,3},{3,4},{4,5},{5,6},{6,7},{7,8},{8,9},{9,10},{10,1... | collective-permute-start | bytes 110600 | tf_op jit(solution)/shard_map/ppermute | solution.py:17
  109.9 17.3 %copy-start.4 = (f32[32,288]{1,0:T(8,128)}, f32[32,288]{1,0:T(8,128)S(1)}, u32[]{:S(2)}) copy-start(f32[32,288]{1,0:T(8,128)S(1)} %fusion.21) | copy-start | bytes 110596
  109.9 3.1 %collective-permute-start.16 = (f32[1,33,288]{2,1,0:T(8,128)S(1)}, f32[1,33,288]{2,1,0:T(8,128)S(1)}, u32[]{:S(2)}, u32[]{:S(2)}) collective-permute-start(f32[1,33,288]{2,1,0:T(8,128)S(1)} %pad_bitcast_fusion), channel_id=1, source_target_pairs={{0,32},{32,0},{64,96},{96,64},{128,160},{160,128},{192,224},{224,1... | collective-permute-start | bytes 114056 | tf_op jit(solution)/shard_map/ppermute | solution.py:172
  113.1 7.3 %collective-permute-start.17 = (f32[2,33,288]{2,1,0:T(8,128)S(1)}, f32[2,33,288]{2,1,0:T(8,128)S(1)}, u32[]{:S(2)}, u32[]{:S(2)}) collective-permute-start(f32[2,33,288]{2,1,0:T(8,128)S(1)} %pad_maximum_fusion.4), channel_id=1, source_target_pairs={{0,64},{32,96},{64,0},{96,32},{128,192},{160,224},{192,128},{224,1... | collective-permute-start | bytes 228104 | tf_op jit(solution)/shard_map/ppermute | solution.py:172

commit v8 on v4

--- a/solution.py
+++ b/solution.py
@@ -106,8 +106,31 @@
     for index, spot in enumerate(EDGE):
         prolong[(3,) + spot] = from_right[index]
         prolong[(0,) + spot] = from_left[index]
-    from_high = shift(jnp.stack([prolong[(spot[0], 1, spot[1])] for spot in ROW]), "gy", False)
-    from_low = shift(jnp.stack([prolong[(spot[0], 2, spot[1])] for spot in ROW]), "gy", True)
+    lane_of = np.arange(9 * width) % width
+    narrow = np.arange(4 * width)
+
+    def picker(sender_x, sender_y, first_x, first_y):
+        quad_x, quad_y = narrow // width // 2, narrow // width % 2
+        chosen = 3 * ((sender_x + first_x + quad_x + 3) % 3) + (sender_y + first_y + quad_y + 3) % 3
+        hit = (block_of[:, None] == chosen[None, :]) & (lane_of[:, None] == (narrow % width)[None, :])
+        return hit.astype(jnp.float32)
+
+    def narrowed(pos_y, first_y):
+        halves = []
+        for first_x, xs in ((-1, (0, 1)), (0, (2, 3))):
+            rows = jnp.concatenate([prolong[(pos_x, pos_y, pos_z)] for pos_x in xs for pos_z in range(2)], axis=0)
+            halves.append(jnp.dot(rows, picker(here_x, here_y, first_x, first_y), precision=HI))
+        return jnp.concatenate(halves, axis=0)
+
+    def widened(received, sender_y, first_y):
+        halves = []
+        for half, first_x in enumerate((-1, 0)):
+            rows = received[half * 4 * width : (half + 1) * 4 * width]
+            halves.append(jnp.dot(rows, picker(here_x, sender_y, first_x, first_y).T, precision=HI))
+        return jnp.concatenate(halves, axis=0)
+
+    from_high = widened(shift(narrowed(1, -1), "gy", False), here_y + 1, -1)
+    from_low = widened(shift(narrowed(2, 0), "gy", True), here_y - 1, 0)
     parts = [prolong_own, from_left, from_right, from_low, from_high]
     applied = None
     first = 0

time: 109 us -> 114 us (1.046)
  waiting for transfers between devices: 29.9 us -> 21.6 us
  matrix products: 9.05 us -> 16.1 us
  local copies, waits for them, and re-layouts: 10.6 us -> 14.5 us
  other arithmetic: 1.86 us -> 4.32 us
    ppermute x12, waiting for transfers between devices: 26.5 us -> 18.2 us  [shift(): return lax.ppermute(block, axis, pairs)]
    dot_general x0 -> x8, matrix products: none -> 6.76 us  [the longest x4 3.99 us: narrowed(): jnp.dot(rows, picker(here_x, here_y, first_x, first_y), precision=HI)]
    add x0 -> x4, other arithmetic: none -> 1.75 us  [picker(): 3 * ((sender_x + first_x + quad_x + 3) % 3)]
    unnamed x63 -> x76, local copies, waits for them, and re-layouts: 1.74 us -> 3.25 us
  transfers between devices with their start and end apart: 14 -> 14, of which waited for: 10 -> 7; matrix products, arithmetic and copies ran while one was open for 9% -> 16% of each run, Pallas kernels for 0% -> 0%
where the time goes in v8:
time: 114 us; the launch traced here: 113 us
  starting transfers between devices  46.4 us (41%)
  waiting for transfers between devices  21.6 us (19%)
  matrix products  16.1 us (14%)
  local copies, waits for them, and re-layouts  14.5 us (13%)
  between operations  10.4 us (9%)
  other arithmetic  4.32 us (4%)
    ppermute x12, starting transfers between devices, shift(): return lax.ppermute(block, axis, pairs)  42.5 us
    ppermute x12, waiting for transfers between devices, shift(): return lax.ppermute(block, axis, pairs)  18.2 us
    dot_general x4, matrix products, narrowed(): jnp.dot(rows, picker(here_x, here_y, first_x, first_y), precision=HI)  3.99 us
    ppermute x2, starting transfers between devices, local(): lax.ppermute(held, 'gx', [(i, i ^ 1 << level) for i in range(count)])  3.84 us
    ppermute x2, waiting for transfers between devices, local(): lax.ppermute(held, 'gx', [(i, i ^ 1 << level) for i in range(count)])  3.45 us
    unnamed x76, local copies, waits for them, and re-layouts  3.25 us
    dot_general x4, matrix products, widened(): jnp.dot(rows, picker(here_x, sender_y, first_x, first_y).T, precision=HI)  2.76 us
    dot_general x5, matrix products, local(): jnp.dot(stencil_pos[:, first:last], part.reshape(len(group) * width, -1),...  2.41 us
  transfers between devices with their start and end apart: 14, of which 7 were waited for; matrix products, arithmetic and copies ran while one was open for 16% of the time, Pallas kernels for 0%

profile of v8, /device:TPU:288, one launch (start us, length us, event | category | flops | bytes accessed | tf_op | source)
XLA Modules:
  0.0 113.3 jit_solution(15717612345268438230)
XLA Ops:
  0.7 1.0 fusion.102
  1.7 1.9 %collective-permute-start = (f32[2,2,32,32]{2,3,1,0:T(8,128)S(1)}, f32[2,2,32,32]{2,3,1,0:T(8,128)S(1)}, u32[]{:S(2)}, u32[]{:S(2)}) collective-permute-start(f32[2,2,32,32]{2,3,1,0:T(8,128)S(1)} %bitcast.281), channel_id=1, source_target_pairs={{0,32},{32,64},{64,96},{96,128},{128,160},{160,192},{192,224},{224... | collective-permute-start | bytes 49160 | tf_op jit(solution)/shard_map/ppermute | solution.py:17
  3.7 4.9 %collective-permute-start.1 = (f32[2,2,32,32]{2,3,1,0:T(8,128)S(1)}, f32[2,2,32,32]{2,3,1,0:T(8,128)S(1)}, u32[]{:S(2)}, u32[]{:S(2)}) collective-permute-start(f32[2,2,32,32]{2,3,1,0:T(8,128)S(1)} %bitcast.280), channel_id=1, source_target_pairs={{32,0},{64,32},{96,64},{128,96},{160,128},{192,160},{224,192},{256... | collective-permute-start | bytes 49160 | tf_op jit(solution)/shard_map/ppermute | solution.py:17
  8.6 0.9 fusion.103
  9.5 0.7 convert_element_type.32
  10.6 0.1 fusion.110
  10.9 0.2 copy-done.17
  11.3 0.6 fusion.92
  11.9 0.5 fusion.95
  13.6 0.2 copy-done.13
  14.0 1.5 %copy.93 = f32[1024,288]{0,1:T(8,128)} copy(f32[1024,288]{1,0:T(8,128)S(1)} %bitcast.252) | data formatting | bytes 2359296 | tf_op jit(solution)/shard_map/reshape | solution.py:93
  16.1 0.6 add.389
  16.9 3.4 %collective-permute-start.2 = (f32[8,32,32]{1,2,0:T(8,128)S(1)}, f32[8,32,32]{1,2,0:T(8,128)S(1)}, u32[]{:S(2)}, u32[]{:S(2)}) collective-permute-start(f32[8,32,32]{1,2,0:T(8,128)S(1)} %constant_dynamic-update-slice_fusion.8), channel_id=1, source_target_pairs={{0,1},{1,2},{2,3},{3,4},{4,5},{5,6},{6,7},{7,8},{8,9},{9,10},{10,1... | collective-permute-start | bytes 98312 | tf_op jit(solution)/shard_map/ppermute | solution.py:17
  20.3 5.8 %collective-permute-start.3 = (f32[8,32,32]{1,2,0:T(8,128)S(1)}, f32[8,32,32]{1,2,0:T(8,128)S(1)}, u32[]{:S(2)}, u32[]{:S(2)}) collective-permute-start(f32[8,32,32]{1,2,0:T(8,128)S(1)} %get-tuple-element.159), channel_id=1, source_target_pairs={{1,0},{2,1},{3,2},{4,3},{5,4},{6,5},{7,6},{8,7},{9,8},{10,9},{11,1... | collective-permute-start | bytes 98312 | tf_op jit(solution)/shard_map/ppermute | solution.py:17
  26.1 1.0 collective-permute-done.2
  27.1 1.5 %collective-permute-done.3 = f32[8,32,32]{1,2,0:T(8,128)S(1)} collective-permute-done((f32[8,32,32]{1,2,0:T(8,128)S(1)}, f32[8,32,32]{1,2,0:T(8,128)S(1)}, u32[]{:S(2)}, u32[]{:S(2)}) %collective-permute-start.3) | collective-permute-done | bytes 32800 | tf_op jit(solution)/shard_map/ppermute | solution.py:17
  28.6 0.2 concatenate.115
  28.8 1.2 %convolution_multiply_fusion = f32[1024,288]{0,1:T(8,128)S(1)} fusion(f32[1024,288]{0,1:T(8,128)S(1)} %copy-done.1, f32[1024,32]{0,1:T(8,128)S(1)} %concatenate.115, f32[32,288]{1,0:T(8,128)S(1)} %copy-done.9), kind=kOutput, calls=%fused_computation | convolution fusion | flops 113541120 | bytes 2527232 | tf_op jit(solution)/shard_map/dot_general | solution.py:94
  29.9 1.9 %fusion.112 = f32[256,288]{1,0:T(8,128)S(1)} fusion(f32[256,1024]{1,0:T(8,128)S(1)} %constant_dynamic-update-slice_fusion, f32[1024,288]{0,1:T(8,128)S(1)} %convolution_multiply_fusion), kind=kOutput, calls=%fused_computation.226 | convolution fusion | flops 905969664 | bytes 2523136 | tf_op jit(solution)/shard_map/dot_general | solution.py:95
  31.8 0.5 convolution_multiply_fusion.1
  32.3 0.1 copy.95
  32.4 0.3 copy-done.3
  32.7 0.4 fusion.2
  33.2 0.9 slice_bitcast_fusion.7
  34.1 0.1 fusion.99
  34.2 0.4 fusion.14
  34.7 1.0 copy.103
  36.1 1.9 %collective-permute-start.5 = (f32[4,32,288]{2,1,0:T(8,128)S(1)}, f32[4,32,288]{2,1,0:T(8,128)S(1)}, u32[]{:S(2)}, u32[]{:S(2)}) collective-permute-start(f32[4,32,288]{2,1,0:T(8,128)S(1)} %pad_maximum_fusion.1), channel_id=1, source_target_pairs={{32,0},{64,32},{96,64},{128,96},{160,128},{192,160},{224,192},{256... | collective-permute-start | bytes 442376 | tf_op jit(solution)/shard_map/ppermute | solution.py:17
  38.4 0.7 pad_maximum_fusion
  39.1 2.5 %collective-permute-start.4 = (f32[4,32,288]{2,1,0:T(8,128)}, f32[4,32,288]{2,1,0:T(8,128)S(1)}, u32[]{:S(2)}, u32[]{:S(2)}) collective-permute-start(f32[4,32,288]{2,1,0:T(8,128)} %pad_maximum_fusion), channel_id=1, source_target_pairs={{0,32},{32,64},{64,96},{96,128},{128,160},{160,192},{192,224},{224... | collective-permute-start | bytes 442376 | tf_op jit(solution)/shard_map/ppermute | solution.py:17
  41.6 1.6 %fusion.4 = f32[256,288]{0,1:T(8,128)S(1)} fusion(f32[256,288]{0,1:T(8,128)S(1)} %fusion.2, pred[288,288]{1,0:T(32,128)(4,1)} %constant.150.clone, s32[288]{0:T(512)S(1)} %fusion.75, s32[288]{0:T(512)S(1)} %copy-done.7), kind=kOutput, calls=%fused_computation.12 | convolution fusion | flops 254969856 | bytes 675072 | tf_op jit(solution)/shard_map/dot_general | solution.py:148
  43.5 4.1 %collective-permute-done.4 = f32[4,32,288]{2,1,0:T(8,128)S(1)} collective-permute-done((f32[4,32,288]{2,1,0:T(8,128)}, f32[4,32,288]{2,1,0:T(8,128)S(1)}, u32[]{:S(2)}, u32[]{:S(2)}) %collective-permute-start.4) | collective-permute-done | bytes 147488 | tf_op jit(solution)/shard_map/ppermute | solution.py:17
  47.6 0.6 fusion.100
  48.4 0.9 copy.123
  49.3 1.1 fusion.26
  50.4 0.5 fusion.20
  51.0 2.0 %collective-permute-start.6 = (f32[256,128]{1,0:T(8,128)S(1)}, f32[256,128]{1,0:T(8,128)}, u32[]{:S(2)}, u32[]{:S(2)}) collective-permute-start(f32[256,128]{1,0:T(8,128)S(1)} %pad_maximum_fusion.4), channel_id=1, source_target_pairs={{0,1},{1,2},{2,3},{3,4},{4,5},{5,6},{6,7},{7,8},{8,9},{9,10},{10,1... | collective-permute-start | bytes 393224 | tf_op jit(solution)/shard_map/ppermute | solution.py:17
  53.4 1.2 %fusion.38 = f32[128,128]{1,0:T(8,128)S(1)} fusion(f32[32,288]{0,1:T(8,128)S(1)} %bitcast.263, f32[32,288]{0,1:T(8,128)S(1)} %bitcast.266, f32[64,288]{0,1:T(8,128)S(1)} %get-tuple-element.34, pred[288,128]{1,0:T(32,128)(4,1)S(1)} %copy-done.2, s32[128]{0:T(128)} %add.389, s32[288]{0:T(512)S(1)} %copy-done.7), kind=kOutput, calls=%fused_computation.57 | convolution fusion | flops 56770560 | bytes 251520 | tf_op jit(solution)/shard_map/dot_general | solution.py:122
  54.6 1.2 %fusion.32 = f32[128,128]{1,0:T(8,128)S(1)} fusion(f32[64,288]{0,1:T(8,128)S(1)} %get-tuple-element.33, f32[32,288]{0,1:T(8,128)S(1)} %bitcast.261, f32[32,288]{0,1:T(8,128)S(1)} %bitcast.265, pred[288,128]{1,0:T(32,128)(4,1)S(1)} %copy-done.2, s32[128]{0:T(128)} %get-tuple-element.2, s32[288]{0:T(512)S(1)} %copy-done.7), kind=kOutput, calls=%fused_computation.51 | convolution fusion | flops 56770560 | bytes 251520 | tf_op jit(solution)/shard_map/dot_general | solution.py:122
  55.8 7.8 %collective-permute-start.7 = (f32[256,128]{1,0:T(8,128)S(1)}, f32[256,128]{1,0:T(8,128)S(1)}, u32[]{:S(2)}, u32[]{:S(2)}) collective-permute-start(f32[256,128]{1,0:T(8,128)S(1)} %pad_maximum_fusion.5), channel_id=1, source_target_pairs={{1,0},{2,1},{3,2},{4,3},{5,4},{6,5},{7,6},{8,7},{9,8},{10,9},{11,1... | collective-permute-start | bytes 393224 | tf_op jit(solution)/shard_map/ppermute | solution.py:17
  63.6 0.5 convolution_add_fusion.2
  64.2 1.1 fusion.45
  65.3 1.1 fusion.46
  66.5 0.4 fusion.5
  66.9 0.5 fusion
  67.5 0.3 fusion.47
  67.8 0.3 fusion.48
  68.0 0.4 convolution_add_fusion
  68.5 0.7 fusion.3
  69.2 0.6 fusion.113
  70.4 1.9 %collective-permute-start.9 = (f32[3,32,288]{2,1,0:T(8,128)S(1)}, f32[3,32,288]{2,1,0:T(8,128)S(1)}, u32[]{:S(2)}, u32[]{:S(2)}) collective-permute-start(f32[3,32,288]{2,1,0:T(8,128)S(1)} %pad_maximum_fusion.3), channel_id=1, source_target_pairs={{32,0},{64,32},{96,64},{128,96},{160,128},{192,160},{224,192},{256... | collective-permute-start | bytes 331784 | tf_op jit(solution)/shard_map/ppermute | solution.py:17
  72.4 2.4 %collective-permute-start.8 = (f32[3,32,288]{2,1,0:T(8,128)S(1)}, f32[3,32,288]{2,1,0:T(8,128)S(1)}, u32[]{:S(2)}, u32[]{:S(2)}) collective-permute-start(f32[3,32,288]{2,1,0:T(8,128)S(1)} %pad_maximum_fusion.2), channel_id=1, source_target_pairs={{0,32},{32,64},{64,96},{96,128},{128,160},{160,192},{192,224},{224... | collective-permute-start | bytes 331784 | tf_op jit(solution)/shard_map/ppermute | solution.py:17
  75.1 5.0 %collective-permute-done.8 = f32[3,32,288]{2,1,0:T(8,128)S(1)} collective-permute-done((f32[3,32,288]{2,1,0:T(8,128)S(1)}, f32[3,32,288]{2,1,0:T(8,128)S(1)}, u32[]{:S(2)}, u32[]{:S(2)}) %collective-permute-start.8) | collective-permute-done | bytes 110624 | tf_op jit(solution)/shard_map/ppermute | solution.py:17
  80.1 6.1 %collective-permute-start.11 = (f32[32,288]{1,0:T(8,128)S(1)}, f32[32,288]{1,0:T(8,128)S(1)}, u32[]{:S(2)}, u32[]{:S(2)}) collective-permute-start(f32[32,288]{1,0:T(8,128)S(1)} %get-tuple-element.58), channel_id=1, source_target_pairs={{1,0},{2,1},{3,2},{4,3},{5,4},{6,5},{7,6},{8,7},{9,8},{10,9},{11,1... | collective-permute-start | bytes 110600 | tf_op jit(solution)/shard_map/ppermute | solution.py:17
  86.3 1.9 %collective-permute-start.10 = (f32[32,288]{1,0:T(8,128)S(1)}, f32[32,288]{1,0:T(8,128)S(1)}, u32[]{:S(2)}, u32[]{:S(2)}) collective-permute-start(f32[32,288]{1,0:T(8,128)S(1)} %get-tuple-element.57), channel_id=1, source_target_pairs={{0,1},{1,2},{2,3},{3,4},{4,5},{5,6},{6,7},{7,8},{8,9},{9,10},{10,1... | collective-permute-start | bytes 110600 | tf_op jit(solution)/shard_map/ppermute | solution.py:17
  89.1 6.5 %collective-permute-done.10 = f32[32,288]{1,0:T(8,128)S(1)} collective-permute-done((f32[32,288]{1,0:T(8,128)S(1)}, f32[32,288]{1,0:T(8,128)S(1)}, u32[]{:S(2)}, u32[]{:S(2)}) %collective-permute-start.10) | collective-permute-done | bytes 36896 | tf_op jit(solution)/shard_map/ppermute | solution.py:17
  95.6 1.9 %collective-permute-start.12 = (f32[1,33,288]{2,1,0:T(8,128)S(1)}, f32[1,33,288]{2,1,0:T(8,128)S(1)}, u32[]{:S(2)}, u32[]{:S(2)}) collective-permute-start(f32[1,33,288]{2,1,0:T(8,128)S(1)} %pad_bitcast_fusion), channel_id=1, source_target_pairs={{0,32},{32,0},{64,96},{96,64},{128,160},{160,128},{192,224},{224,1... | collective-permute-start | bytes 114056 | tf_op jit(solution)/shard_map/ppermute | solution.py:177
  97.6 1.2 %collective-permute-done.12 = f32[1,33,288]{2,1,0:T(8,128)S(1)} collective-permute-done((f32[1,33,288]{2,1,0:T(8,128)S(1)}, f32[1,33,288]{2,1,0:T(8,128)S(1)}, u32[]{:S(2)}, u32[]{:S(2)}) %collective-permute-start.12) | collective-permute-done | bytes 38048 | tf_op jit(solution)/shard_map/ppermute | solution.py:177
  98.8 1.9 %collective-permute-start.13 = (f32[2,33,288]{2,1,0:T(8,128)S(1)}, f32[2,33,288]{2,1,0:T(8,128)S(1)}, u32[]{:S(2)}, u32[]{:S(2)}) collective-permute-start(f32[2,33,288]{2,1,0:T(8,128)S(1)} %pad_maximum_fusion.6), channel_id=1, source_target_pairs={{0,64},{32,96},{64,0},{96,32},{128,192},{160,224},{192,128},{224,1... | collective-permute-start | bytes 228104 | tf_op jit(solution)/shard_map/ppermute | solution.py:177
  100.7 0.5 slice.1130
  103.8 2.2 %collective-permute-done.13 = f32[2,33,288]{2,1,0:T(8,128)S(1)} collective-permute-done((f32[2,33,288]{2,1,0:T(8,128)S(1)}, f32[2,33,288]{2,1,0:T(8,128)S(1)}, u32[]{:S(2)}, u32[]{:S(2)}) %collective-permute-start.13) | collective-permute-done | bytes 76064 | tf_op jit(solution)/shard_map/ppermute | solution.py:177
  106.1 0.5 slice.1128
  107.9 0.6 slice.1125
  112.6 0.7 maximum_bitcast_fusion
  (146 shorter events, 5.4 us)
Async XLA Ops:
  0.6 31.2 %copy-start = (f32[2,2,2,32,32]{4,3,2,1,0:T(8,128)S(1)}, f32[2,2,2,32,32]{4,3,2,1,0:T(8,128)}, u32[]{:S(2)}) copy-start(f32[2,2,2,32,32]{4,3,2,1,0:T(8,128)} %param.50) | copy-start | bytes 98308
  0.6 9.7 %copy-start.4 = (f32[2,2,2,32,864]{4,3,2,1,0:T(8,128)S(1)}, f32[2,2,2,32,864]{4,3,2,1,0:T(8,128)}, u32[]{:S(2)}) copy-start(f32[2,2,2,32,864]{4,3,2,1,0:T(8,128)} %param.47) | copy-start | bytes 2654212
  1.7 15.0 %collective-permute-start = (f32[2,2,32,32]{2,3,1,0:T(8,128)S(1)}, f32[2,2,32,32]{2,3,1,0:T(8,128)S(1)}, u32[]{:S(2)}, u32[]{:S(2)}) collective-permute-start(f32[2,2,32,32]{2,3,1,0:T(8,128)S(1)} %bitcast.281), channel_id=1, source_target_pairs={{0,32},{32,64},{64,96},{96,128},{128,160},{160,192},{192,224},{224... | collective-permute-start | bytes 49160 | tf_op jit(solution)/shard_map/ppermute | solution.py:17
  3.7 13.1 %collective-permute-start.1 = (f32[2,2,32,32]{2,3,1,0:T(8,128)S(1)}, f32[2,2,32,32]{2,3,1,0:T(8,128)S(1)}, u32[]{:S(2)}, u32[]{:S(2)}) collective-permute-start(f32[2,2,32,32]{2,3,1,0:T(8,128)S(1)} %bitcast.280), channel_id=1, source_target_pairs={{32,0},{64,32},{96,64},{128,96},{160,128},{192,160},{224,192},{256... | collective-permute-start | bytes 49160 | tf_op jit(solution)/shard_map/ppermute | solution.py:17
  10.5 0.7 copy-start.17
  10.5 0.7 copy-start.18
  10.5 0.7 copy-start.7
  10.5 0.8 copy-start.15
  10.5 0.8 copy-start.16
  13.0 0.7 copy-start.13
  13.1 0.7 copy-start.14
  15.5 13.2 %copy-start.1 = (f32[1024,288]{0,1:T(8,128)S(1)}, f32[1024,288]{0,1:T(8,128)}, u32[]{:S(2)}) copy-start(f32[1024,288]{0,1:T(8,128)} %copy.93) | copy-start | bytes 3538948
  15.5 13.2 %copy-start.9 = (f32[32,288]{1,0:T(8,128)S(1)}, f32[32,288]{1,0:T(8,128)}, u32[]{:S(2)}) copy-start(f32[32,288]{1,0:T(8,128)} %constant.139.clone) | copy-start | bytes 110596
  16.9 10.2 %collective-permute-start.2 = (f32[8,32,32]{1,2,0:T(8,128)S(1)}, f32[8,32,32]{1,2,0:T(8,128)S(1)}, u32[]{:S(2)}, u32[]{:S(2)}) collective-permute-start(f32[8,32,32]{1,2,0:T(8,128)S(1)} %constant_dynamic-update-slice_fusion.8), channel_id=1, source_target_pairs={{0,1},{1,2},{2,3},{3,4},{4,5},{5,6},{6,7},{7,8},{8,9},{9,10},{10,1... | collective-permute-start | bytes 98312 | tf_op jit(solution)/shard_map/ppermute | solution.py:17
  20.3 8.3 %collective-permute-start.3 = (f32[8,32,32]{1,2,0:T(8,128)S(1)}, f32[8,32,32]{1,2,0:T(8,128)S(1)}, u32[]{:S(2)}, u32[]{:S(2)}) collective-permute-start(f32[8,32,32]{1,2,0:T(8,128)S(1)} %get-tuple-element.159), channel_id=1, source_target_pairs={{1,0},{2,1},{3,2},{4,3},{5,4},{6,5},{7,6},{8,7},{9,8},{10,9},{11,1... | collective-permute-start | bytes 98312 | tf_op jit(solution)/shard_map/ppermute | solution.py:17
  31.8 0.9 copy-start.3
  36.1 7.2 %collective-permute-start.5 = (f32[4,32,288]{2,1,0:T(8,128)S(1)}, f32[4,32,288]{2,1,0:T(8,128)S(1)}, u32[]{:S(2)}, u32[]{:S(2)}) collective-permute-start(f32[4,32,288]{2,1,0:T(8,128)S(1)} %pad_maximum_fusion.1), channel_id=1, source_target_pairs={{32,0},{64,32},{96,64},{128,96},{160,128},{192,160},{224,192},{256... | collective-permute-start | bytes 442376 | tf_op jit(solution)/shard_map/ppermute | solution.py:17
  39.1 10.2 %copy-start.2 = (pred[288,128]{1,0:T(32,128)(4,1)S(1)}, pred[288,128]{1,0:T(32,128)(4,1)}, u32[]{:S(2)}) copy-start(pred[288,128]{1,0:T(32,128)(4,1)} %constant.147.clone) | copy-start | bytes 110596
  39.1 8.5 %collective-permute-start.4 = (f32[4,32,288]{2,1,0:T(8,128)}, f32[4,32,288]{2,1,0:T(8,128)S(1)}, u32[]{:S(2)}, u32[]{:S(2)}) collective-permute-start(f32[4,32,288]{2,1,0:T(8,128)} %pad_maximum_fusion), channel_id=1, source_target_pairs={{0,32},{32,64},{64,96},{96,128},{128,160},{160,192},{192,224},{224... | collective-permute-start | bytes 442376 | tf_op jit(solution)/shard_map/ppermute | solution.py:17
  50.4 2.8 %copy-start.8 = (f32[1,32,288]{2,1,0:T(8,128)S(1)}, f32[1,32,288]{2,1,0:T(8,128)}, u32[]{:S(2)}) copy-start(f32[1,32,288]{2,1,0:T(8,128)} %get-tuple-element.52) | copy-start | bytes 110596
  51.0 13.2 %collective-permute-start.6 = (f32[256,128]{1,0:T(8,128)S(1)}, f32[256,128]{1,0:T(8,128)}, u32[]{:S(2)}, u32[]{:S(2)}) collective-permute-start(f32[256,128]{1,0:T(8,128)S(1)} %pad_maximum_fusion.4), channel_id=1, source_target_pairs={{0,1},{1,2},{2,3},{3,4},{4,5},{5,6},{6,7},{7,8},{8,9},{9,10},{10,1... | collective-permute-start | bytes 393224 | tf_op jit(solution)/shard_map/ppermute | solution.py:17
  53.4 10.8 %copy-start.12 = (s32[128]{0:T(128)S(1)}, s32[128]{0:T(128)}, u32[]{:S(2)}) copy-start(s32[128]{0:T(128)} %add.389) | copy-start | bytes 1540
  53.4 11.9 %copy-start.11 = (s32[128]{0:T(128)S(1)}, s32[128]{0:T(128)}, u32[]{:S(2)}) copy-start(s32[128]{0:T(128)} %get-tuple-element.2) | copy-start | bytes 1540
  55.8 11.6 %collective-permute-start.7 = (f32[256,128]{1,0:T(8,128)S(1)}, f32[256,128]{1,0:T(8,128)S(1)}, u32[]{:S(2)}, u32[]{:S(2)}) collective-permute-start(f32[256,128]{1,0:T(8,128)S(1)} %pad_maximum_fusion.5), channel_id=1, source_target_pairs={{1,0},{2,1},{3,2},{4,3},{5,4},{6,5},{7,6},{8,7},{9,8},{10,9},{11,1... | collective-permute-start | bytes 393224 | tf_op jit(solution)/shard_map/ppermute | solution.py:17
  65.3 2.1 %copy-start.10 = (s32[128]{0:T(128)S(1)}, s32[128]{0:T(128)}, u32[]{:S(2)}) copy-start(s32[128]{0:T(128)} %get-tuple-element.7) | copy-start | bytes 1540
  66.9 1.6 %copy-start.6 = (pred[288,288]{1,0:T(32,128)(4,1)S(1)}, pred[288,288]{1,0:T(32,128)(4,1)}, u32[]{:S(2)}) copy-start(pred[288,288]{1,0:T(32,128)(4,1)} %constant.150.clone) | copy-start | bytes 248836
  70.1 18.1 %copy-start.19 = (s32[1,1,9]{2,1,0:T(1,128)S(1)}, s32[1,1,9]{2,1,0:T(1,128)}, u32[]{:S(2)}) copy-start(s32[1,1,9]{2,1,0:T(1,128)} %param.51) | copy-start | bytes 112
  70.4 4.7 %collective-permute-start.9 = (f32[3,32,288]{2,1,0:T(8,128)S(1)}, f32[3,32,288]{2,1,0:T(8,128)S(1)}, u32[]{:S(2)}, u32[]{:S(2)}) collective-permute-start(f32[3,32,288]{2,1,0:T(8,128)S(1)} %pad_maximum_fusion.3), channel_id=1, source_target_pairs={{32,0},{64,32},{96,64},{128,96},{160,128},{192,160},{224,192},{256... | collective-permute-start | bytes 331784 | tf_op jit(solution)/shard_map/ppermute | solution.py:17
  72.4 7.7 %collective-permute-start.8 = (f32[3,32,288]{2,1,0:T(8,128)S(1)}, f32[3,32,288]{2,1,0:T(8,128)S(1)}, u32[]{:S(2)}, u32[]{:S(2)}) collective-permute-start(f32[3,32,288]{2,1,0:T(8,128)S(1)} %pad_maximum_fusion.2), channel_id=1, source_target_pairs={{0,32},{32,64},{64,96},{96,128},{128,160},{160,192},{192,224},{224... | collective-permute-start | bytes 331784 | tf_op jit(solution)/shard_map/ppermute | solution.py:17
  80.1 8.9 %collective-permute-start.11 = (f32[32,288]{1,0:T(8,128)S(1)}, f32[32,288]{1,0:T(8,128)S(1)}, u32[]{:S(2)}, u32[]{:S(2)}) collective-permute-start(f32[32,288]{1,0:T(8,128)S(1)} %get-tuple-element.58), channel_id=1, source_target_pairs={{1,0},{2,1},{3,2},{4,3},{5,4},{6,5},{7,6},{8,7},{9,8},{10,9},{11,1... | collective-permute-start | bytes 110600 | tf_op jit(solution)/shard_map/ppermute | solution.py:17
  86.3 9.3 %collective-permute-start.10 = (f32[32,288]{1,0:T(8,128)S(1)}, f32[32,288]{1,0:T(8,128)S(1)}, u32[]{:S(2)}, u32[]{:S(2)}) collective-permute-start(f32[32,288]{1,0:T(8,128)S(1)} %get-tuple-element.57), channel_id=1, source_target_pairs={{0,1},{1,2},{2,3},{3,4},{4,5},{5,6},{6,7},{7,8},{8,9},{9,10},{10,1... | collective-permute-start | bytes 110600 | tf_op jit(solution)/shard_map/ppermute | solution.py:17
  95.6 17.7 %copy-start.5 = (f32[32,288]{1,0:T(8,128)}, f32[32,288]{1,0:T(8,128)S(1)}, u32[]{:S(2)}) copy-start(f32[32,288]{1,0:T(8,128)S(1)} %fusion.73) | copy-start | bytes 110596
  95.6 3.1 %collective-permute-start.12 = (f32[1,33,288]{2,1,0:T(8,128)S(1)}, f32[1,33,288]{2,1,0:T(8,128)S(1)}, u32[]{:S(2)}, u32[]{:S(2)}) collective-permute-start(f32[1,33,288]{2,1,0:T(8,128)S(1)} %pad_bitcast_fusion), channel_id=1, source_target_pairs={{0,32},{32,0},{64,96},{96,64},{128,160},{160,128},{192,224},{224,1... | collective-permute-start | bytes 114056 | tf_op jit(solution)/shard_map/ppermute | solution.py:177
  98.8 7.3 %collective-permute-start.13 = (f32[2,33,288]{2,1,0:T(8,128)S(1)}, f32[2,33,288]{2,1,0:T(8,128)S(1)}, u32[]{:S(2)}, u32[]{:S(2)}) collective-permute-start(f32[2,33,288]{2,1,0:T(8,128)S(1)} %pad_maximum_fusion.6), channel_id=1, source_target_pairs={{0,64},{32,96},{64,0},{96,32},{128,192},{160,224},{192,128},{224,1... | collective-permute-start | bytes 228104 | tf_op jit(solution)/shard_map/ppermute | solution.py:177
